TPU v7x, 128 devices: a whole 4x4x4 slice. The times are simulated.
128 devices in a mesh: row: 8 (over z, core), col: 16 (over x, y).
Axes of the slice: x: 4, y: 4, z: 4, core: 2. Of those that a mesh axis runs over, the one named last changes fastest.
Arguments:
- updates: float32 [16384, 8192], P('col', 'row'), may hold values from -6 to 6
- block_map: int32 [2, 64], replicated, may hold values from 0 to 79, as said below
- own_diag: float32 [10240], P('row'), may hold values from 2 to 6
- panel_inverse: float32 [512, 512], replicated, as said below
Outputs:
- factor_panel: float32 [10240, 512], P('row')
- trailing: float32 [10240, 10240], P('row', 'col')
Inputs may be any that keep to these rules, and one draw needn't show every extreme that they name: `block_map`: within one child the 64 entries name distinct front blocks. Take the child blocks (a, b) held by one device in updates, and the front blocks held by one device in trailing: either exactly 1 of the former land in the latter, or none do. `panel_inverse`: lower triangular with a positive diagonal.
All inputs are finite; a program needn't handle non-finite values.
Results may differ from a plain program's by a relative error of at most 0.000075.
Values sent between devices are 32-bit elements; how exact they have to be, the bound alone decides.
No kernel may reach another device: no remote copies, remote signals or barrier semaphores. Data moves between devices by JAX's collectives and lax.ppermute only.
A program may use at most 128 MiB of HBM per device.

v0:
```python
import jax
import jax.numpy as jnp
from jax import lax
from jax.sharding import PartitionSpec as P

F = 10240
M = 8192
BLK = 128
PANEL = 512


def broadcast(shard, axis, root):
    mine = lax.axis_index(axis) == root
    return lax.psum(jnp.where(mine, shard, jnp.zeros_like(shard)), axis)


def item_routes(source_row, source_col, block_map, row_count, col_count):
    half_cols = col_count // 2
    row_items = 2 * M // col_count // BLK
    col_items = M // row_count // BLK
    front_rows = F // BLK // row_count
    front_cols = F // BLK // col_count
    child_map = jnp.take(block_map, source_col // half_cols, axis=0)
    row_parent = jnp.take(
        child_map, source_col % half_cols * row_items + jnp.arange(row_items, dtype=jnp.int32)
    )
    col_parent = jnp.take(
        child_map, source_row * col_items + jnp.arange(col_items, dtype=jnp.int32)
    )
    target_dev = (
        (row_parent // front_rows)[:, None] * col_count + (col_parent // front_cols)[None, :]
    ).reshape(-1)
    target_blk = (
        (row_parent % front_rows)[:, None] * front_cols + (col_parent % front_cols)[None, :]
    ).reshape(-1)
    position = jnp.arange(target_dev.shape[0], dtype=jnp.int32)
    same_target = (target_dev[:, None] == target_dev[None, :]) & (
        position[:, None] > position[None, :]
    )
    ranking = jnp.sum(same_target.astype(jnp.int32), axis=1)
    return (target_dev, ranking, target_blk)


def on_device(updates, block_map, own_diag, panel_inverse):
    row_count = lax.axis_size("row")
    col_count = lax.axis_size("col")
    row_index = lax.axis_index("row")
    col_index = lax.axis_index("col")
    devices_all = row_count * col_count
    local_rows, local_cols = updates.shape
    row_items = local_rows // BLK
    col_items = local_cols // BLK
    capacity = max(1, row_items // row_count) * max(1, col_items // col_count)
    front_rows = F // BLK // row_count
    front_cols = F // BLK // col_count
    slot_total = devices_all * capacity
    target_dev, ranking, unused_blk = item_routes(
        row_index, col_index, block_map, row_count, col_count
    )
    child_tiles = (
        updates.reshape(row_items, BLK, col_items, BLK)
        .transpose(0, 2, 1, 3)
        .reshape(row_items * col_items, BLK, BLK)
    )
    outgoing = (
        jnp.zeros((slot_total, BLK, BLK), jnp.float32)
        .at[target_dev * capacity + ranking]
        .set(child_tiles)
    )
    incoming = lax.all_to_all(
        outgoing.reshape(devices_all, capacity, BLK, BLK),
        ("row", "col"),
        split_axis=0,
        concat_axis=0,
        tiled=True,
    )
    sources = jnp.arange(devices_all, dtype=jnp.int32)
    all_dev, all_rank, all_blk = jax.vmap(
        lambda source_row, source_col: item_routes(
            source_row, source_col, block_map, row_count, col_count
        )
    )(sources // col_count, sources % col_count)
    myself = row_index * col_count + col_index
    slot_of = jnp.where(all_dev == myself, sources[:, None] * capacity + all_rank, slot_total)
    dump_slot = front_rows * front_cols
    slot_target = (
        jnp.full((slot_total + 1,), dump_slot, jnp.int32)
        .at[slot_of.reshape(-1)]
        .set(all_blk.reshape(-1))
    )
    slot_target = slot_target[:slot_total]
    assembled = (
        jnp.zeros((dump_slot + 1, BLK, BLK), jnp.float32)
        .at[slot_target]
        .add(incoming.reshape(slot_total, BLK, BLK))
    )
    height = front_rows * BLK
    col_width = front_cols * BLK
    front_local = (
        assembled[:dump_slot]
        .reshape(front_rows, front_cols, BLK, BLK)
        .transpose(0, 2, 1, 3)
        .reshape(height, col_width)
    )
    row_global = row_index * height + jnp.arange(height, dtype=jnp.int32)
    col_global = col_index * col_width + jnp.arange(col_width, dtype=jnp.int32)
    front_local = front_local + jnp.where(
        row_global[:, None] == col_global[None, :], own_diag[:, None], 0.0
    )
    raw_panel = broadcast(front_local[:, :PANEL], "col", 0)
    factor_panel = jnp.dot(
        raw_panel,
        panel_inverse.T,
        precision=lax.Precision.HIGHEST,
        preferred_element_type=jnp.float32,
    )
    gathered = lax.all_gather(factor_panel, "row", axis=0, tiled=True)
    across = lax.dynamic_slice_in_dim(gathered, col_index * col_width, col_width, 0)
    update_term = lax.dot_general(
        factor_panel,
        across,
        (((1,), (1,)), ((), ())),
        precision=lax.Precision.HIGHEST,
        preferred_element_type=jnp.float32,
    )
    trailing = front_local - update_term
    return (factor_panel, trailing)


def solution(mesh):
    return jax.shard_map(
        on_device,
        mesh=mesh,
        in_specs=(P("col", "row"), P(), P("row"), P()),
        out_specs=(P("row", None), P("row", "col")),
        check_vma=False,
    )
```

profile of v0, /device:TPU:1, one launch (start us, length us, event | category | flops | bytes accessed | tf_op | source)
XLA Modules:
  0.0 404.0 jit_solution(12149989379777365822)
XLA Ops:
  7.2 0.8 fusion.13
  8.7 0.6 gather_fusion.3
  9.8 3.2 copy.42
  13.3 2.7 copy.40
  16.0 4.3 %broadcast_in_dim.89 = f32[128,128,128]{2,1,0:T(8,128)} broadcast(f32[]{:T(128)} %constant.172.clone.1), dimensions={} | broadcast | bytes 8388612 | tf_op jit(solution)/shard_map/broadcast_in_dim | solution.py:66
  20.2 12.2 %scatter_fusion = f32[128,128,128]{2,1,0:T(8,128)} fusion(f32[128,128,128]{2,1,0:T(8,128)} %broadcast_in_dim.89, s32[64]{0:T(128)S(1)} %fusion.17, f32[64,128,128]{2,1,0:T(8,128)} %bitcast.45), kind=kCustom, calls=%fused_computation.6 | custom fusion | bytes 12583168 | tf_op jit(solution)/shard_map/scatter | solution.py:68
  32.4 12.0 %all-to-all-start = ((f32[128,1,128,128]{3,2,1,0:T(8,128)}), f32[128,1,128,128]{3,2,1,0:T(8,128)}, u32[]{:S(2)}, u32[]{:S(2)}) async-start(f32[128,1,128,128]{3,2,1,0:T(8,128)} %bitcast.43), calls=%async_computation | async-start | bytes 16777216 | tf_op jit(solution)/shard_map/all_to_all | solution.py:70
  44.9 0.6 gather_fusion
  45.7 7.1 %gather_fusion.2 = s32[1024]{0:T(1024)S(1)} fusion(s32[128,64]{1,0:T(8,128)S(1)} %broadcast_select_fusion, s32[1024]{0:T(1024)S(1)} %reshape.442), kind=kCustom, calls=%fused_computation.2.clone | custom fusion | bytes 16384 | tf_op jit(solution)/shard_map/vmap(jit(_take))/gather | solution.py:27
  52.8 7.1 %gather_fusion.1 = s32[1024]{0:T(1024)S(1)} fusion(s32[128,64]{1,0:T(8,128)S(1)} %broadcast_select_fusion, s32[1024]{0:T(1024)S(1)} %reshape.437), kind=kCustom, calls=%fused_computation.clone | custom fusion | bytes 16384 | tf_op jit(solution)/shard_map/vmap(jit(_take))/gather | solution.py:24
  60.3 0.7 convert_reduce_fusion
  62.5 30.6 %scatter_custom_fusion = s32[129]{0:T(256)S(1)} fusion(s32[8192]{0:T(1024)S(1)} %bitcast.49, s32[8192]{0:T(1024)S(1)} %reshape.403, s32[]{:T(128)} %constant.173.clone.1), kind=kCustom, calls=%fused_computation.87 | custom fusion | bytes 520 | tf_op jit(solution)/shard_map/scatter | solution.py:89
  93.1 51.8 %all-to-all-done = f32[128,1,128,128]{3,2,1,0:T(8,128)} async-done(((f32[128,1,128,128]{3,2,1,0:T(8,128)}), f32[128,1,128,128]{3,2,1,0:T(8,128)}, u32[]{:S(2)}, u32[]{:S(2)}) %all-to-all-start) | async-done | bytes 8388640 | tf_op jit(solution)/shard_map/all_to_all | solution.py:70
  145.0 2.2 broadcast_in_dim.83
  147.2 27.8 %scatter_fusion.1 = f32[51,128,128]{2,1,0:T(8,128)} fusion(f32[51,128,128]{2,1,0:T(8,128)} %broadcast_in_dim.83, s32[128]{0:T(128)S(1)} %compare_select_fusion.6, f32[128,128,128]{2,1,0:T(8,128)} %bitcast.11), kind=kCustom, calls=%fused_computation.7 | custom fusion | flops 2097152 | bytes 25166336 | tf_op jit(solution)/shard_map/scatter-add | solution.py:95
  175.0 2.1 slice.29
  177.1 1.9 copy.41
  179.1 0.7 bitcast_add_fusion
  179.8 1.7 copy-done.2
  181.5 1.9 slice_select_fusion
  183.5 92.7 %all-reduce.2.cloned.1.call-done = f32[1280,512]{1,0:T(8,128)} async-done(((f32[1280,512]{1,0:T(8,128)}), f32[1280,512]{1,0:T(8,128)}) %all-reduce.2.cloned.1.call-update) | async-done | bytes 2621456 | tf_op jit(solution)/shard_map/psum | solution.py:14
  276.2 7.5 %fusion.22 = f32[1280,512]{1,0:T(8,128)} fusion(f32[1280,512]{1,0:T(8,128)} %all-reduce.2.cloned.1.call-done, f32[512,512]{1,0:T(8,128)S(1)} %copy-done), kind=kOutput, calls=%fused_computation.90 | convolution fusion | flops 4026531840 | bytes 6291456 | tf_op jit(solution)/shard_map/dot_general | solution.py:111
  283.7 103.4 %all-gather.2.cloned.1.call-done = f32[10240,512]{1,0:T(8,128)} async-done(((f32[1280,512]{1,0:T(8,128)}), f32[10240,512]{1,0:T(8,128)}) %all-gather.2.cloned.1.call-update) | async-done | bytes 20971536 | tf_op jit(solution)/shard_map/all_gather | solution.py:117
  387.1 10.0 %convolution_subtract_fusion = f32[1280,640]{1,0:T(8,128)} fusion(f32[1280,640]{1,0:T(8,128)} %copy-done.2, f32[1280,512]{1,0:T(8,128)} %fusion.22, f32[10240,512]{1,0:T(8,128)} %all-gather.2.cloned.1.call-done, s32[]{:T(128)S(6)} %select_n.210), kind=kOutput, calls=%fused_computation.9 | convolution fusion | flops 5033984000 | bytes 10485764 | tf_op jit(solution)/shard_map/dot_general | solution.py:119
  (56 shorter events, 3.9 us)
Async XLA Ops:
  7.2 269.0 %copy-start = (f32[512,512]{1,0:T(8,128)S(1)}, f32[512,512]{1,0:T(8,128)}, u32[]{:S(2)}) copy-start(f32[512,512]{1,0:T(8,128)} %param.11) | copy-start | bytes 3145732
  32.4 12.5 %copy-start.1 = (s32[2,64]{1,0:T(2,128)S(1)}, s32[2,64]{1,0:T(2,128)}, u32[]{:S(2)}) copy-start(s32[2,64]{1,0:T(2,128)} %param.9) | copy-start | bytes 1540
  32.4 112.6 %all-to-all-start = ((f32[128,1,128,128]{3,2,1,0:T(8,128)}), f32[128,1,128,128]{3,2,1,0:T(8,128)}, u32[]{:S(2)}, u32[]{:S(2)}) async-start(f32[128,1,128,128]{3,2,1,0:T(8,128)} %bitcast.43), calls=%async_computation | async-start | bytes 16777216 | tf_op jit(solution)/shard_map/all_to_all | solution.py:70
  44.4 231.8 %all-reduce.2.cloned.1.call-start = ((), (), s32[]{:S(2)}) async-start(), calls=%async_computation.1 | async-start | bytes 5242880 | tf_op jit(solution)/shard_map/psum | solution.py:14
  177.1 2.0 copy-start.3
  179.8 1.7 copy-start.2
  183.4 203.7 %all-gather.2.cloned.1.call-start = ((), (), s32[]{:S(2)}) async-start(), calls=%async_computation.2 | async-start | bytes 23592960 | tf_op jit(solution)/shard_map/all_gather | solution.py:117
Sparse Core Ops, SparseCore 0:
  183.5 92.5 all-reduce.1
  283.9 103.2 all-gather.1
where the time goes:
time: 405 us; the launch traced here: 404 us
  waiting for transfers between devices  248 us (61%)
  local copies, waits for them, and re-layouts  79.2 us (20%)
  other arithmetic  32.7 us (8%)
  matrix products  17.6 us (4%)
  between operations  14.4 us (4%)
  starting transfers between devices  12.1 us (3%)
    all_gather x1, waiting for transfers between devices, on_device(): gathered = lax.all_gather(factor_panel, 'row', axis=0, tiled=True)  103 us
    psum x1, waiting for transfers between devices, broadcast(): return lax.psum(jnp.where(mine, shard, jnp.zeros_like(shard)), axis)  92.7 us
    all_to_all x1, waiting for transfers between devices, on_device(): lax.all_to_all(outgoing.reshape(devices_all, capacity, BLK, BLK), ('row',...  51.8 us
    scatter x1, local copies, waits for them, and re-layouts, on_device(): slot_target = jnp.full((slot_total + 1,), dump_slot, jnp.int32).at[slot_o...  30.6 us
    scatter-add x1, other arithmetic, on_device(): assembled = jnp.zeros((dump_slot + 1, BLK, BLK), jnp.float32).at[slot_tar...  27.8 us
    scatter x1, local copies, waits for them, and re-layouts, on_device(): outgoing = jnp.zeros((slot_total, BLK, BLK), jnp.float32).at[target_dev *...  12.2 us
    all_to_all x1, starting transfers between devices, on_device(): lax.all_to_all(outgoing.reshape(devices_all, capacity, BLK, BLK), ('row',...  12 us
    dot_general x1, matrix products, on_device(): lax.dot_general(factor_panel, across, (((1,), (1,)), ((), ())), precision...  10 us
  transfers between devices with their start and end apart: 3, of which 3 were waited for; matrix products, arithmetic and copies ran while one was open for 12% of the time, Pallas kernels for 0%

commit v1 on v0

--- a/solution.py
+++ b/solution.py
@@ -114,8 +114,15 @@
         precision=lax.Precision.HIGHEST,
         preferred_element_type=jnp.float32,
     )
-    gathered = lax.all_gather(factor_panel, "row", axis=0, tiled=True)
-    across = lax.dynamic_slice_in_dim(gathered, col_index * col_width, col_width, 0)
+    ratio = col_count // row_count
+    pieces = height // col_width
+    half = lax.dynamic_slice_in_dim(factor_panel, (col_index % pieces) * col_width, col_width, 0)
+    pairs = [
+        (r * col_count + t, (t // ratio) * col_count + r * ratio + t % ratio)
+        for r in range(row_count)
+        for t in range(col_count)
+    ]
+    across = lax.ppermute(half, ("row", "col"), pairs)
     update_term = lax.dot_general(
         factor_panel,
         across,

time: 405 us -> 384 us (0.948)
  waiting for transfers between devices: 248 us -> 224 us
  starting transfers between devices: 12.1 us -> 16.6 us
    all_gather x1 -> x0, waiting for transfers between devices: 103 us -> none  [on_device(): gathered = lax.all_gather(factor_panel, 'row', axis=0, tiled=True)]
    ppermute x0 -> x1, waiting for transfers between devices: none -> 79.3 us  [on_device(): across = lax.ppermute(half, ('row', 'col'), pairs)]
    ppermute x0 -> x1, starting transfers between devices: none -> 4.67 us  [on_device(): across = lax.ppermute(half, ('row', 'col'), pairs)]
  transfers between devices with their start and end apart: 3 -> 3, of which waited for: 3 -> 3; matrix products, arithmetic and copies ran while one was open for 12% -> 13% of each run, Pallas kernels for 0% -> 0%
where the time goes in v1:
time: 384 us; the launch traced here: 380 us
  waiting for transfers between devices  224 us (58%)
  local copies, waits for them, and re-layouts  79.3 us (21%)
  other arithmetic  30.8 us (8%)
  starting transfers between devices  16.6 us (4%)
  matrix products  14.7 us (4%)
  between operations  14.5 us (4%)
    psum x1, waiting for transfers between devices, broadcast(): return lax.psum(jnp.where(mine, shard, jnp.zeros_like(shard)), axis)  92.7 us
    ppermute x1, waiting for transfers between devices, on_device(): across = lax.ppermute(half, ('row', 'col'), pairs)  79.3 us
    all_to_all x1, waiting for transfers between devices, on_device(): lax.all_to_all(outgoing.reshape(devices_all, capacity, BLK, BLK), ('row',...  51.8 us
    scatter x1, local copies, waits for them, and re-layouts, on_device(): slot_target = jnp.full((slot_total + 1,), dump_slot, jnp.int32).at[slot_o...  30.6 us
    scatter-add x1, other arithmetic, on_device(): assembled = jnp.zeros((dump_slot + 1, BLK, BLK), jnp.float32).at[slot_tar...  25.9 us
    scatter x1, local copies, waits for them, and re-layouts, on_device(): outgoing = jnp.zeros((slot_total, BLK, BLK), jnp.float32).at[target_dev *...  12.1 us
    all_to_all x1, starting transfers between devices, on_device(): lax.all_to_all(outgoing.reshape(devices_all, capacity, BLK, BLK), ('row',...  11.9 us
    dot_general x1, matrix products, on_device(): lax.dot_general(factor_panel, across, (((1,), (1,)), ((), ())), precision...  8.37 us
  transfers between devices with their start and end apart: 3, of which 3 were waited for; matrix products, arithmetic and copies ran while one was open for 13% of the time, Pallas kernels for 0%

profile of v1, /device:TPU:1, one launch (start us, length us, event | category | flops | bytes accessed | tf_op | source)
XLA Modules:
  0.0 379.7 jit_solution(9491555772123099179)
XLA Ops:
  7.2 0.8 fusion.12
  9.8 3.2 copy.42
  13.3 2.7 copy.40
  15.9 4.3 %broadcast_in_dim.89 = f32[128,128,128]{2,1,0:T(8,128)} broadcast(f32[]{:T(128)} %constant.179.clone.1), dimensions={} | broadcast | bytes 8388612 | tf_op jit(solution)/shard_map/broadcast_in_dim | solution.py:66
  20.2 12.1 %scatter_fusion = f32[128,128,128]{2,1,0:T(8,128)} fusion(f32[128,128,128]{2,1,0:T(8,128)} %broadcast_in_dim.89, s32[64]{0:T(128)S(1)} %fusion.16, f32[64,128,128]{2,1,0:T(8,128)} %bitcast.44), kind=kCustom, calls=%fused_computation.6 | custom fusion | bytes 12583168 | tf_op jit(solution)/shard_map/scatter | solution.py:68
  32.3 11.9 %all-to-all-start = ((f32[128,1,128,128]{3,2,1,0:T(8,128)}), f32[128,1,128,128]{3,2,1,0:T(8,128)}, u32[]{:S(2)}, u32[]{:S(2)}) async-start(f32[128,1,128,128]{3,2,1,0:T(8,128)} %bitcast.42), calls=%async_computation | async-start | bytes 16777216 | tf_op jit(solution)/shard_map/all_to_all | solution.py:70
  44.5 0.6 gather_fusion
  45.3 7.1 %gather_fusion.1 = s32[1024]{0:T(1024)S(1)} fusion(s32[128,64]{1,0:T(8,128)S(1)} %broadcast_select_fusion, s32[1024]{0:T(1024)S(1)} %reshape.437), kind=kCustom, calls=%fused_computation.clone | custom fusion | bytes 16384 | tf_op jit(solution)/shard_map/vmap(jit(_take))/gather | solution.py:24
  52.7 7.1 %gather_fusion.2 = s32[1024]{0:T(1024)S(1)} fusion(s32[128,64]{1,0:T(8,128)S(1)} %broadcast_select_fusion, s32[1024]{0:T(1024)S(1)} %reshape.442), kind=kCustom, calls=%fused_computation.2.clone | custom fusion | bytes 16384 | tf_op jit(solution)/shard_map/vmap(jit(_take))/gather | solution.py:27
  60.6 0.7 convert_reduce_fusion
  62.3 30.6 %scatter_custom_fusion = s32[129]{0:T(256)S(1)} fusion(s32[8192]{0:T(1024)S(1)} %bitcast.48, s32[8192]{0:T(1024)S(1)} %reshape.403, s32[]{:T(128)} %constant.180.clone.1), kind=kCustom, calls=%fused_computation.86 | custom fusion | bytes 520 | tf_op jit(solution)/shard_map/scatter | solution.py:89
  92.9 51.8 %all-to-all-done = f32[128,1,128,128]{3,2,1,0:T(8,128)} async-done(((f32[128,1,128,128]{3,2,1,0:T(8,128)}), f32[128,1,128,128]{3,2,1,0:T(8,128)}, u32[]{:S(2)}, u32[]{:S(2)}) %all-to-all-start) | async-done | bytes 8388640 | tf_op jit(solution)/shard_map/all_to_all | solution.py:70
  144.8 2.2 broadcast_in_dim.83
  147.0 25.9 %scatter_fusion.1 = f32[51,128,128]{2,1,0:T(8,128)} fusion(f32[51,128,128]{2,1,0:T(8,128)} %broadcast_in_dim.83, s32[128]{0:T(128)S(1)} %compare_select_fusion.6, f32[128,128,128]{2,1,0:T(8,128)} %bitcast.11), kind=kCustom, calls=%fused_computation.7 | custom fusion | flops 2097152 | bytes 25166336 | tf_op jit(solution)/shard_map/scatter-add | solution.py:95
  172.9 2.1 slice.29
  175.0 1.9 copy.41
  177.0 0.7 bitcast_add_fusion
  177.7 1.7 copy-done.2
  179.4 1.9 slice_select_fusion
  181.3 92.7 %all-reduce.2.cloned.1.call-done = f32[1280,512]{1,0:T(8,128)} async-done(((f32[1280,512]{1,0:T(8,128)}), f32[1280,512]{1,0:T(8,128)}) %all-reduce.2.cloned.1.call-update) | async-done | bytes 2621456 | tf_op jit(solution)/shard_map/psum | solution.py:14
  274.0 6.3 %fusion.20 = f32[1280,512]{1,0:T(8,128)S(1)} fusion(f32[1280,512]{1,0:T(8,128)} %all-reduce.2.cloned.1.call-done, f32[512,512]{1,0:T(8,128)S(1)} %copy-done), kind=kOutput, calls=%fused_computation.89 | convolution fusion | flops 4026531840 | bytes 6291456 | tf_op jit(solution)/shard_map/dot_general | solution.py:111
  280.5 4.7 %collective-permute-start = (f32[640,512]{1,0:T(8,128)S(1)}, f32[640,512]{1,0:T(8,128)S(1)}, u32[]{:S(2)}, u32[]{:S(2)}) collective-permute-start(f32[640,512]{1,0:T(8,128)S(1)} %constant_dynamic-slice_fusion), channel_id=1, source_target_pairs={{0,0},{1,1},{2,16},{3,17},{4,32},{5,33},{6,48},{7,49},{8,64},{9,65... | collective-permute-start | bytes 3932168 | tf_op jit(solution)/shard_map/ppermute | solution.py:125
  285.2 79.3 %collective-permute-done = f32[640,512]{1,0:T(8,128)S(1)} collective-permute-done((f32[640,512]{1,0:T(8,128)S(1)}, f32[640,512]{1,0:T(8,128)S(1)}, u32[]{:S(2)}, u32[]{:S(2)}) %collective-permute-start) | collective-permute-done | bytes 1310752 | tf_op jit(solution)/shard_map/ppermute | solution.py:125
  364.5 8.4 %convolution_subtract_fusion = f32[1280,640]{1,0:T(8,128)} fusion(f32[1280,640]{1,0:T(8,128)S(1)} %copy-done.3, f32[1280,512]{1,0:T(8,128)S(1)} %fusion.20, f32[640,512]{1,0:T(8,128)S(1)} %collective-permute-done), kind=kOutput, calls=%fused_computation.9 | convolution fusion | flops 5033984000 | bytes 10485760 | tf_op jit(solution)/shard_map/dot_general | solution.py:126
  (60 shorter events, 4.6 us)
Async XLA Ops:
  7.2 266.9 %copy-start = (f32[512,512]{1,0:T(8,128)S(1)}, f32[512,512]{1,0:T(8,128)}, u32[]{:S(2)}) copy-start(f32[512,512]{1,0:T(8,128)} %param.11) | copy-start | bytes 3145732
  32.3 12.2 %copy-start.1 = (s32[2,64]{1,0:T(2,128)S(1)}, s32[2,64]{1,0:T(2,128)}, u32[]{:S(2)}) copy-start(s32[2,64]{1,0:T(2,128)} %param.9) | copy-start | bytes 1540
  32.3 112.4 %all-to-all-start = ((f32[128,1,128,128]{3,2,1,0:T(8,128)}), f32[128,1,128,128]{3,2,1,0:T(8,128)}, u32[]{:S(2)}, u32[]{:S(2)}) async-start(f32[128,1,128,128]{3,2,1,0:T(8,128)} %bitcast.42), calls=%async_computation | async-start | bytes 16777216 | tf_op jit(solution)/shard_map/all_to_all | solution.py:70
  44.2 229.8 %all-reduce.2.cloned.1.call-start = ((), (), s32[]{:S(2)}) async-start(), calls=%async_computation.1 | async-start | bytes 5242880 | tf_op jit(solution)/shard_map/psum | solution.py:14
  175.0 2.0 copy-start.5
  177.7 1.7 copy-start.2
  274.0 90.5 %copy-start.3 = (f32[1280,640]{1,0:T(8,128)S(1)}, f32[1280,640]{1,0:T(8,128)}, u32[]{:S(2)}) copy-start(f32[1280,640]{1,0:T(8,128)} %copy-done.2) | copy-start | bytes 9830404
  280.4 92.5 %copy-start.4 = (f32[1280,512]{1,0:T(8,128)}, f32[1280,512]{1,0:T(8,128)S(1)}, u32[]{:S(2)}) copy-start(f32[1280,512]{1,0:T(8,128)S(1)} %fusion.20) | copy-start | bytes 7864324
  280.5 84.0 %collective-permute-start = (f32[640,512]{1,0:T(8,128)S(1)}, f32[640,512]{1,0:T(8,128)S(1)}, u32[]{:S(2)}, u32[]{:S(2)}) collective-permute-start(f32[640,512]{1,0:T(8,128)S(1)} %constant_dynamic-slice_fusion), channel_id=1, source_target_pairs={{0,0},{1,1},{2,16},{3,17},{4,32},{5,33},{6,48},{7,49},{8,64},{9,65... | collective-permute-start | bytes 3932168 | tf_op jit(solution)/shard_map/ppermute | solution.py:125
Sparse Core Ops, SparseCore 0:
  181.4 92.5 all-reduce.1

commit v2 on v1

--- a/solution.py
+++ b/solution.py
@@ -107,22 +107,29 @@
     front_local = front_local + jnp.where(
         row_global[:, None] == col_global[None, :], own_diag[:, None], 0.0
     )
-    raw_panel = broadcast(front_local[:, :PANEL], "col", 0)
-    factor_panel = jnp.dot(
-        raw_panel,
+    piece_rows = height // col_count
+    raw_panel = front_local[:, :PANEL]
+    piece = jnp.where(col_index == 0, raw_panel[:piece_rows], 0.0)
+    for k in range(1, col_count):
+        pairs = [(r * col_count, r * col_count + k) for r in range(row_count)]
+        piece = piece + lax.ppermute(
+            raw_panel[k * piece_rows:(k + 1) * piece_rows], ("row", "col"), pairs
+        )
+    factor_piece = jnp.dot(
+        piece,
         panel_inverse.T,
         precision=lax.Precision.HIGHEST,
         preferred_element_type=jnp.float32,
     )
+    factor_panel = lax.all_gather(factor_piece, "col", axis=0, tiled=True)
     ratio = col_count // row_count
-    pieces = height // col_width
-    half = lax.dynamic_slice_in_dim(factor_panel, (col_index % pieces) * col_width, col_width, 0)
     pairs = [
-        (r * col_count + t, (t // ratio) * col_count + r * ratio + t % ratio)
+        (r * col_count + k, (k % row_count) * col_count + r * ratio + k // row_count)
         for r in range(row_count)
-        for t in range(col_count)
+        for k in range(col_count)
     ]
-    across = lax.ppermute(half, ("row", "col"), pairs)
+    moved = lax.ppermute(factor_piece, ("row", "col"), pairs)
+    across = lax.all_gather(moved, "row", axis=0, tiled=True)
     update_term = lax.dot_general(
         factor_panel,
         across,

time: 384 us -> 315 us (0.82)
  waiting for transfers between devices: 224 us -> 136 us
  starting transfers between devices: 16.6 us -> 39.8 us
    psum x1 -> x0, waiting for transfers between devices: 92.7 us -> none  [broadcast(): return lax.psum(jnp.where(mine, shard, jnp.zeros_like(shard)), axis)]
    all_gather x0 -> x2, waiting for transfers between devices: none -> 64 us  [the longest x1 37.2 us: on_device(): factor_panel = lax.all_gather(factor_piece, 'col', axis=0, tiled=True)]
    ppermute x1 -> x16, waiting for transfers between devices: 79.3 us -> 20 us  [the longest x15 12.7 us: on_device(): lax.ppermute(raw_panel[k * piece_rows:(k + 1) * piece_rows], ('row', 'col...]
    ppermute x1 -> x16, starting transfers between devices: 4.67 us -> 27.9 us  [the longest x15 26 us: on_device(): lax.ppermute(raw_panel[k * piece_rows:(k + 1) * piece_rows], ('row', 'col...]
  transfers between devices with their start and end apart: 3 -> 19, of which waited for: 3 -> 9; matrix products, arithmetic and copies ran while one was open for 13% -> 15% of each run, Pallas kernels for 0% -> 0%
where the time goes in v2:
time: 315 us; the launch traced here: 314 us
  waiting for transfers between devices  136 us (43%)
  local copies, waits for them, and re-layouts  81.5 us (26%)
  starting transfers between devices  39.8 us (13%)
  other arithmetic  28.9 us (9%)
  between operations  14.5 us (5%)
  matrix products  13.3 us (4%)
    all_to_all x1, waiting for transfers between devices, on_device(): lax.all_to_all(outgoing.reshape(devices_all, capacity, BLK, BLK), ('row',...  51.9 us
    all_gather x1, waiting for transfers between devices, on_device(): factor_panel = lax.all_gather(factor_piece, 'col', axis=0, tiled=True)  37.2 us
    scatter x1, local copies, waits for them, and re-layouts, on_device(): slot_target = jnp.full((slot_total + 1,), dump_slot, jnp.int32).at[slot_o...  30.6 us
    all_gather x1, waiting for transfers between devices, on_device(): across = lax.all_gather(moved, 'row', axis=0, tiled=True)  26.8 us
    ppermute x15, starting transfers between devices, on_device(): lax.ppermute(raw_panel[k * piece_rows:(k + 1) * piece_rows], ('row', 'col...  26 us
    scatter-add x1, other arithmetic, on_device(): assembled = jnp.zeros((dump_slot + 1, BLK, BLK), jnp.float32).at[slot_tar...  26 us
    ppermute x15, waiting for transfers between devices, on_device(): lax.ppermute(raw_panel[k * piece_rows:(k + 1) * piece_rows], ('row', 'col...  12.7 us
    scatter x1, local copies, waits for them, and re-layouts, on_device(): outgoing = jnp.zeros((slot_total, BLK, BLK), jnp.float32).at[target_dev *...  12.1 us
  transfers between devices with their start and end apart: 19, of which 9 were waited for; matrix products, arithmetic and copies ran while one was open for 15% of the time, Pallas kernels for 0%

profile of v2, /device:TPU:1, one launch (start us, length us, event | category | flops | bytes accessed | tf_op | source)
XLA Modules:
  0.0 314.0 jit_solution(12508903441898814116)
XLA Ops:
  9.8 3.2 %copy.42 = f32[128,8,8,128]{3,2,1,0:T(8,128)S(1)} copy(f32[128,8,8,128]{3,1,2,0:T(8,128)} %bitcast.46) | data formatting | bytes 8388608
  13.2 2.7 copy.40
  15.9 4.3 %broadcast_in_dim.90 = f32[128,128,128]{2,1,0:T(8,128)} broadcast(f32[]{:T(128)} %constant.170.clone.1), dimensions={} | broadcast | bytes 8388612 | tf_op jit(solution)/shard_map/broadcast_in_dim | solution.py:66
  20.2 12.1 %scatter_fusion = f32[128,128,128]{2,1,0:T(8,128)} fusion(f32[128,128,128]{2,1,0:T(8,128)} %broadcast_in_dim.90, s32[64]{0:T(128)S(1)} %fusion.35, f32[64,128,128]{2,1,0:T(8,128)} %bitcast.43), kind=kCustom, calls=%fused_computation.6 | custom fusion | bytes 12583168 | tf_op jit(solution)/shard_map/scatter | solution.py:68
  32.3 11.8 %all-to-all-start = ((f32[128,1,128,128]{3,2,1,0:T(8,128)}), f32[128,1,128,128]{3,2,1,0:T(8,128)}, u32[]{:S(2)}, u32[]{:S(2)}) async-start(f32[128,1,128,128]{3,2,1,0:T(8,128)} %bitcast.41), calls=%async_computation | async-start | bytes 16777216 | tf_op jit(solution)/shard_map/all_to_all | solution.py:70
  45.2 7.1 %gather_fusion.1 = s32[1024]{0:T(1024)S(1)} fusion(s32[128,64]{1,0:T(8,128)S(1)} %broadcast_select_fusion, s32[1024]{0:T(1024)S(1)} %reshape.437), kind=kCustom, calls=%fused_computation.clone | custom fusion | bytes 16384 | tf_op jit(solution)/shard_map/vmap(jit(_take))/gather | solution.py:24
  52.7 7.1 %gather_fusion.2 = s32[1024]{0:T(1024)S(1)} fusion(s32[128,64]{1,0:T(8,128)S(1)} %broadcast_select_fusion, s32[1024]{0:T(1024)S(1)} %reshape.442), kind=kCustom, calls=%fused_computation.2.clone | custom fusion | bytes 16384 | tf_op jit(solution)/shard_map/vmap(jit(_take))/gather | solution.py:27
  62.2 30.6 %scatter_custom_fusion = s32[129]{0:T(256)S(1)} fusion(s32[8192]{0:T(1024)S(1)} %bitcast.47, s32[8192]{0:T(1024)S(1)} %reshape.403, s32[]{:T(128)} %constant.171.clone.1), kind=kCustom, calls=%fused_computation.104 | custom fusion | bytes 520 | tf_op jit(solution)/shard_map/scatter | solution.py:89
  92.9 51.9 %all-to-all-done = f32[128,1,128,128]{3,2,1,0:T(8,128)} async-done(((f32[128,1,128,128]{3,2,1,0:T(8,128)}), f32[128,1,128,128]{3,2,1,0:T(8,128)}, u32[]{:S(2)}, u32[]{:S(2)}) %all-to-all-start) | async-done | bytes 8388640 | tf_op jit(solution)/shard_map/all_to_all | solution.py:70
  144.8 2.1 broadcast_in_dim.84
  146.9 26.0 %scatter_fusion.1 = f32[51,128,128]{2,1,0:T(8,128)} fusion(f32[51,128,128]{2,1,0:T(8,128)} %broadcast_in_dim.84, s32[128]{0:T(128)S(1)} %compare_select_fusion.6, f32[128,128,128]{2,1,0:T(8,128)} %bitcast.11), kind=kCustom, calls=%fused_computation.7 | custom fusion | flops 2097152 | bytes 25166336 | tf_op jit(solution)/shard_map/scatter-add | solution.py:95
  172.9 2.1 slice.106
  182.3 4.5 %collective-permute-start.10 = (f32[80,512]{1,0:T(8,128)S(1)}, f32[80,512]{1,0:T(8,128)S(1)}, u32[]{:S(2)}, u32[]{:S(2)}) collective-permute-start(f32[80,512]{1,0:T(8,128)S(1)} %get-tuple-element.20), channel_id=1, source_target_pairs={{0,11},{16,27},{32,43},{48,59},{64,75},{80,91},{96,107},{112,123}} | collective-permute-start | bytes 491528 | tf_op jit(solution)/shard_map/ppermute | solution.py:115
  201.3 1.9 collective-permute-start.6
  205.2 2.0 collective-permute-start.8
  207.2 1.9 collective-permute-start.9
  209.1 2.3 collective-permute-done.7
  211.4 3.5 %collective-permute-done.8 = f32[80,512]{1,0:T(8,128)} collective-permute-done((f32[80,512]{1,0:T(8,128)S(1)}, f32[80,512]{1,0:T(8,128)}, u32[]{:S(2)}, u32[]{:S(2)}) %collective-permute-start.8) | collective-permute-done | bytes 163872 | tf_op jit(solution)/shard_map/ppermute | solution.py:115
  214.9 3.5 %collective-permute-done.9 = f32[80,512]{1,0:T(8,128)} collective-permute-done((f32[80,512]{1,0:T(8,128)S(1)}, f32[80,512]{1,0:T(8,128)}, u32[]{:S(2)}, u32[]{:S(2)}) %collective-permute-start.9) | collective-permute-done | bytes 163872 | tf_op jit(solution)/shard_map/ppermute | solution.py:115
  218.4 3.1 fusion.15
  223.6 7.3 %collective-permute-done.15 = f32[80,512]{1,0:T(8,128)S(1)} collective-permute-done((f32[80,512]{1,0:T(8,128)}, f32[80,512]{1,0:T(8,128)S(1)}, u32[]{:S(2)}, u32[]{:S(2)}) %collective-permute-start.15) | collective-permute-done | bytes 163872 | tf_op jit(solution)/shard_map/ppermute | solution.py:131
  231.6 37.2 %all-gather.3.cloned.1.call-done = f32[1280,512]{1,0:T(8,128)} async-done(((f32[80,512]{1,0:T(8,128)}), f32[1280,512]{1,0:T(8,128)}) %all-gather.3.cloned.1.call-update) | async-done | bytes 2621456 | tf_op jit(solution)/shard_map/all_gather | solution.py:124
  268.8 26.8 %all-gather.5.cloned.1.call-done = f32[640,512]{1,0:T(8,128)} async-done(((f32[80,512]{1,0:T(8,128)}), f32[640,512]{1,0:T(8,128)}) %all-gather.5.cloned.1.call-update) | async-done | bytes 1310736 | tf_op jit(solution)/shard_map/all_gather | solution.py:132
  295.5 10.2 %convolution_subtract_fusion = f32[1280,640]{1,0:T(8,128)} fusion(f32[1280,640]{1,0:T(8,128)} %copy-done.2, f32[1280,512]{1,0:T(8,128)} %all-gather.3.cloned.1.call-done, f32[640,512]{1,0:T(8,128)} %all-gather.5.cloned.1.call-done), kind=kOutput, calls=%fused_computation.9 | convolution fusion | flops 5033984000 | bytes 10485760 | tf_op jit(solution)/shard_map/dot_general | solution.py:133
  (93 shorter events, 34.3 us)
Async XLA Ops:
  7.2 211.3 %copy-start = (f32[512,512]{1,0:T(8,128)S(1)}, f32[512,512]{1,0:T(8,128)}, u32[]{:S(2)}) copy-start(f32[512,512]{1,0:T(8,128)} %param.11) | copy-start | bytes 3145732
  32.3 11.9 %copy-start.1 = (s32[2,64]{1,0:T(2,128)S(1)}, s32[2,64]{1,0:T(2,128)}, u32[]{:S(2)}) copy-start(s32[2,64]{1,0:T(2,128)} %param.9) | copy-start | bytes 1540
  32.3 112.4 %all-to-all-start = ((f32[128,1,128,128]{3,2,1,0:T(8,128)}), f32[128,1,128,128]{3,2,1,0:T(8,128)}, u32[]{:S(2)}, u32[]{:S(2)}) async-start(f32[128,1,128,128]{3,2,1,0:T(8,128)} %bitcast.41), calls=%async_computation | async-start | bytes 16777216 | tf_op jit(solution)/shard_map/all_to_all | solution.py:70
  44.2 224.6 %all-gather.3.cloned.1.call-start = ((), (), s32[]{:S(2)}) async-start(), calls=%async_computation.1 | async-start | bytes 2785280 | tf_op jit(solution)/shard_map/all_gather | solution.py:124
  175.0 2.0 copy-start.5
  177.7 1.7 copy-start.2
  179.6 9.8 %collective-permute-start = (f32[80,512]{1,0:T(8,128)S(1)}, f32[80,512]{1,0:T(8,128)S(1)}, u32[]{:S(2)}, u32[]{:S(2)}) collective-permute-start(f32[80,512]{1,0:T(8,128)S(1)} %get-tuple-element.15), channel_id=1, source_target_pairs={{0,1},{16,17},{32,33},{48,49},{64,65},{80,81},{96,97},{112,113}} | collective-permute-start | bytes 491528 | tf_op jit(solution)/shard_map/ppermute | solution.py:115
  180.9 9.8 %collective-permute-start.1 = (f32[80,512]{1,0:T(8,128)S(1)}, f32[80,512]{1,0:T(8,128)S(1)}, u32[]{:S(2)}, u32[]{:S(2)}) collective-permute-start(f32[80,512]{1,0:T(8,128)S(1)} %get-tuple-element.29), channel_id=1, source_target_pairs={{0,2},{16,18},{32,34},{48,50},{64,66},{80,82},{96,98},{112,114}} | collective-permute-start | bytes 491528 | tf_op jit(solution)/shard_map/ppermute | solution.py:115
  182.3 9.8 %collective-permute-start.10 = (f32[80,512]{1,0:T(8,128)S(1)}, f32[80,512]{1,0:T(8,128)S(1)}, u32[]{:S(2)}, u32[]{:S(2)}) collective-permute-start(f32[80,512]{1,0:T(8,128)S(1)} %get-tuple-element.20), channel_id=1, source_target_pairs={{0,11},{16,27},{32,43},{48,59},{64,75},{80,91},{96,107},{112,123}} | collective-permute-start | bytes 491528 | tf_op jit(solution)/shard_map/ppermute | solution.py:115
  186.8 6.6 %collective-permute-start.11 = (f32[80,512]{1,0:T(8,128)S(1)}, f32[80,512]{1,0:T(8,128)S(1)}, u32[]{:S(2)}, u32[]{:S(2)}) collective-permute-start(f32[80,512]{1,0:T(8,128)S(1)} %get-tuple-element.19), channel_id=1, source_target_pairs={{0,12},{16,28},{32,44},{48,60},{64,76},{80,92},{96,108},{112,124}} | collective-permute-start | bytes 491528 | tf_op jit(solution)/shard_map/ppermute | solution.py:115
  188.1 6.6 %collective-permute-start.12 = (f32[80,512]{1,0:T(8,128)S(1)}, f32[80,512]{1,0:T(8,128)S(1)}, u32[]{:S(2)}, u32[]{:S(2)}) collective-permute-start(f32[80,512]{1,0:T(8,128)S(1)} %get-tuple-element.18), channel_id=1, source_target_pairs={{0,13},{16,29},{32,45},{48,61},{64,77},{80,93},{96,109},{112,125}} | collective-permute-start | bytes 491528 | tf_op jit(solution)/shard_map/ppermute | solution.py:115
  189.4 8.4 %collective-permute-start.13 = (f32[80,512]{1,0:T(8,128)S(1)}, f32[80,512]{1,0:T(8,128)S(1)}, u32[]{:S(2)}, u32[]{:S(2)}) collective-permute-start(f32[80,512]{1,0:T(8,128)S(1)} %get-tuple-element.17), channel_id=1, source_target_pairs={{0,14},{16,30},{32,46},{48,62},{64,78},{80,94},{96,110},{112,126}} | collective-permute-start | bytes 491528 | tf_op jit(solution)/shard_map/ppermute | solution.py:115
  190.7 10.6 %collective-permute-start.14 = (f32[80,512]{1,0:T(8,128)S(1)}, f32[80,512]{1,0:T(8,128)S(1)}, u32[]{:S(2)}, u32[]{:S(2)}) collective-permute-start(f32[80,512]{1,0:T(8,128)S(1)} %get-tuple-element.16), channel_id=1, source_target_pairs={{0,15},{16,31},{32,47},{48,63},{64,79},{80,95},{96,111},{112,127}} | collective-permute-start | bytes 491528 | tf_op jit(solution)/shard_map/ppermute | solution.py:115
  192.0 11.2 %collective-permute-start.2 = (f32[80,512]{1,0:T(8,128)S(1)}, f32[80,512]{1,0:T(8,128)S(1)}, u32[]{:S(2)}, u32[]{:S(2)}) collective-permute-start(f32[80,512]{1,0:T(8,128)S(1)} %get-tuple-element.28), channel_id=1, source_target_pairs={{0,3},{16,19},{32,35},{48,51},{64,67},{80,83},{96,99},{112,115}} | collective-permute-start | bytes 491528 | tf_op jit(solution)/shard_map/ppermute | solution.py:115
  193.4 11.9 %collective-permute-start.3 = (f32[80,512]{1,0:T(8,128)S(1)}, f32[80,512]{1,0:T(8,128)S(1)}, u32[]{:S(2)}, u32[]{:S(2)}) collective-permute-start(f32[80,512]{1,0:T(8,128)S(1)} %get-tuple-element.27), channel_id=1, source_target_pairs={{0,4},{16,20},{32,36},{48,52},{64,68},{80,84},{96,100},{112,116}} | collective-permute-start | bytes 491528 | tf_op jit(solution)/shard_map/ppermute | solution.py:115
  194.7 12.5 %collective-permute-start.4 = (f32[80,512]{1,0:T(8,128)S(1)}, f32[80,512]{1,0:T(8,128)S(1)}, u32[]{:S(2)}, u32[]{:S(2)}) collective-permute-start(f32[80,512]{1,0:T(8,128)S(1)} %get-tuple-element.26), channel_id=1, source_target_pairs={{0,5},{16,21},{32,37},{48,53},{64,69},{80,85},{96,101},{112,117}} | collective-permute-start | bytes 491528 | tf_op jit(solution)/shard_map/ppermute | solution.py:115
  197.8 11.3 %collective-permute-start.5 = (f32[80,512]{1,0:T(8,128)S(1)}, f32[80,512]{1,0:T(8,128)}, u32[]{:S(2)}, u32[]{:S(2)}) collective-permute-start(f32[80,512]{1,0:T(8,128)S(1)} %get-tuple-element.25), channel_id=1, source_target_pairs={{0,6},{16,22},{32,38},{48,54},{64,70},{80,86},{96,102},{112,118}} | collective-permute-start | bytes 491528 | tf_op jit(solution)/shard_map/ppermute | solution.py:115
  201.3 7.8 %collective-permute-start.6 = (f32[80,512]{1,0:T(8,128)S(1)}, f32[80,512]{1,0:T(8,128)}, u32[]{:S(2)}, u32[]{:S(2)}) collective-permute-start(f32[80,512]{1,0:T(8,128)S(1)} %get-tuple-element.24), channel_id=1, source_target_pairs={{0,7},{16,23},{32,39},{48,55},{64,71},{80,87},{96,103},{112,119}} | collective-permute-start | bytes 491528 | tf_op jit(solution)/shard_map/ppermute | solution.py:115
  203.3 8.1 %collective-permute-start.7 = (f32[80,512]{1,0:T(8,128)S(1)}, f32[80,512]{1,0:T(8,128)}, u32[]{:S(2)}, u32[]{:S(2)}) collective-permute-start(f32[80,512]{1,0:T(8,128)S(1)} %get-tuple-element.23), channel_id=1, source_target_pairs={{0,8},{16,24},{32,40},{48,56},{64,72},{80,88},{96,104},{112,120}} | collective-permute-start | bytes 491528 | tf_op jit(solution)/shard_map/ppermute | solution.py:115
  205.2 9.7 %collective-permute-start.8 = (f32[80,512]{1,0:T(8,128)S(1)}, f32[80,512]{1,0:T(8,128)}, u32[]{:S(2)}, u32[]{:S(2)}) collective-permute-start(f32[80,512]{1,0:T(8,128)S(1)} %get-tuple-element.22), channel_id=1, source_target_pairs={{0,9},{16,25},{32,41},{48,57},{64,73},{80,89},{96,105},{112,121}} | collective-permute-start | bytes 491528 | tf_op jit(solution)/shard_map/ppermute | solution.py:115
  207.2 11.3 %collective-permute-start.9 = (f32[80,512]{1,0:T(8,128)S(1)}, f32[80,512]{1,0:T(8,128)}, u32[]{:S(2)}, u32[]{:S(2)}) collective-permute-start(f32[80,512]{1,0:T(8,128)S(1)} %get-tuple-element.21), channel_id=1, source_target_pairs={{0,10},{16,26},{32,42},{48,58},{64,74},{80,90},{96,106},{112,122}} | collective-permute-start | bytes 491528 | tf_op jit(solution)/shard_map/ppermute | solution.py:115
  221.6 73.9 %all-gather.5.cloned.1.call-start = ((), (), s32[]{:S(2)}) async-start(), calls=%async_computation.2 | async-start | bytes 1474560 | tf_op jit(solution)/shard_map/all_gather | solution.py:132
  221.6 9.3 %collective-permute-start.15 = (f32[80,512]{1,0:T(8,128)}, f32[80,512]{1,0:T(8,128)S(1)}, u32[]{:S(2)}, u32[]{:S(2)}) collective-permute-start(f32[80,512]{1,0:T(8,128)} %fusion.15), channel_id=1, source_target_pairs={{0,0},{1,16},{2,32},{3,48},{4,64},{5,80},{6,96},{7,112},{8,1},{9,1... | collective-permute-start | bytes 491528 | tf_op jit(solution)/shard_map/ppermute | solution.py:131
  295.5 10.2 %copy-start.3 = (f32[1280,512]{1,0:T(8,128)S(1)}, f32[1280,512]{1,0:T(8,128)}, u32[]{:S(2)}) copy-start(f32[1280,512]{1,0:T(8,128)} %all-gather.3.cloned.1.call-done) | copy-start | bytes 7864324
  (1 other events, 0.7 us)
Sparse Core Ops, SparseCore 0:
  221.7 47.0 all-gather.2
  270.5 25.0 all-gather.4

commit v3 on v2

v3 whole, which is shorter than its diff:
```python
import jax
import jax.numpy as jnp
from jax import lax
from jax.sharding import PartitionSpec as P

F = 10240
M = 8192
BLK = 128
PANEL = 512


def broadcast(shard, axis, root):
    mine = lax.axis_index(axis) == root
    return lax.psum(jnp.where(mine, shard, jnp.zeros_like(shard)), axis)


def on_device(updates, block_map, own_diag, panel_inverse):
    row_count = lax.axis_size("row")
    col_count = lax.axis_size("col")
    row_index = lax.axis_index("row")
    col_index = lax.axis_index("col")
    devices_all = row_count * col_count
    local_rows, local_cols = updates.shape
    row_items = local_rows // BLK
    col_items = local_cols // BLK
    half_cols = col_count // 2
    front_blocks = F // BLK
    front_rows = front_blocks // row_count
    front_cols = front_blocks // col_count
    height = front_rows * BLK
    col_width = front_cols * BLK
    block_map = block_map.astype(jnp.int32)
    child = col_index // half_cols
    child_map = jnp.take(block_map, child, axis=0)
    row_parent = lax.dynamic_slice_in_dim(child_map, col_index % half_cols * row_items, row_items)
    col_parent = lax.dynamic_slice_in_dim(child_map, row_index * col_items, col_items)
    inv_k = (
        jnp.zeros((row_count,), jnp.int32)
        .at[row_parent // front_rows]
        .set(jnp.arange(row_items, dtype=jnp.int32))
    )
    inv_l = (
        jnp.full((col_count,), -1, jnp.int32)
        .at[col_parent // front_cols]
        .set(jnp.arange(col_items, dtype=jnp.int32))
    )
    row_sorted = jnp.take(updates.reshape(row_items, BLK, local_cols), inv_k, axis=0)
    picked = jnp.take(
        row_sorted.reshape(row_count, BLK, col_items, BLK), jnp.maximum(inv_l, 0), axis=2
    )
    picked = jnp.where((inv_l >= 0)[None, None, :, None], picked, 0.0)
    outgoing = picked.transpose(0, 2, 1, 3).reshape(devices_all, 1, BLK, BLK)
    incoming = lax.all_to_all(
        outgoing, ("row", "col"), split_axis=0, concat_axis=0, tiled=True
    ).reshape(devices_all, BLK, BLK)
    slots = jnp.arange(front_blocks, dtype=jnp.int32)
    my_rows = row_index * front_rows + jnp.arange(front_rows, dtype=jnp.int32)
    my_cols = col_index * front_cols + jnp.arange(front_cols, dtype=jnp.int32)
    front_local = None
    for child_id in range(2):
        inverse = (
            jnp.full((front_blocks,), -1, jnp.int32)
            .at[block_map[child_id]]
            .set(jnp.arange(block_map.shape[1], dtype=jnp.int32))
        )
        a = jnp.take(inverse, my_rows)
        b = jnp.take(inverse, my_cols)
        source = (jnp.maximum(b, 0) // col_items)[None, :] * col_count + (
            child_id * half_cols + jnp.maximum(a, 0) // row_items
        )[:, None]
        valid = (a >= 0)[:, None] & (b >= 0)[None, :]
        part = jnp.take(incoming, source.reshape(-1), axis=0).reshape(
            front_rows, front_cols, BLK, BLK
        )
        part = jnp.where(valid[:, :, None, None], part, 0.0)
        front_local = part if front_local is None else front_local + part
    front_local = front_local.transpose(0, 2, 1, 3).reshape(height, col_width)
    row_global = row_index * height + jnp.arange(height, dtype=jnp.int32)
    col_global = col_index * col_width + jnp.arange(col_width, dtype=jnp.int32)
    front_local = front_local + jnp.where(
        row_global[:, None] == col_global[None, :], own_diag[:, None], 0.0
    )
    piece_rows = height // col_count
    raw_panel = front_local[:, :PANEL]
    piece = jnp.where(col_index == 0, raw_panel[:piece_rows], 0.0)
    for k in range(1, col_count):
        pairs = [(r * col_count, r * col_count + k) for r in range(row_count)]
        piece = piece + lax.ppermute(
            raw_panel[k * piece_rows:(k + 1) * piece_rows], ("row", "col"), pairs
        )
    factor_piece = jnp.dot(
        piece,
        panel_inverse.T,
        precision=lax.Precision.HIGHEST,
        preferred_element_type=jnp.float32,
    )
    factor_panel = lax.all_gather(factor_piece, "col", axis=0, tiled=True)
    ratio = col_count // row_count
    pairs = [
        (r * col_count + k, (k % row_count) * col_count + r * ratio + k // row_count)
        for r in range(row_count)
        for k in range(col_count)
    ]
    moved = lax.ppermute(factor_piece, ("row", "col"), pairs)
    across = lax.all_gather(moved, "row", axis=0, tiled=True)
    update_term = lax.dot_general(
        factor_panel,
        across,
        (((1,), (1,)), ((), ())),
        precision=lax.Precision.HIGHEST,
        preferred_element_type=jnp.float32,
    )
    trailing = front_local - update_term
    return (factor_panel, trailing)


def solution(mesh):
    return jax.shard_map(
        on_device,
        mesh=mesh,
        in_specs=(P("col", "row"), P(), P("row"), P()),
        out_specs=(P("row", None), P("row", "col")),
        check_vma=False,
    )
```

time: 315 us -> 313 us (level)
  waiting for transfers between devices: 136 us -> 180 us
  local copies, waits for them, and re-layouts: 81.5 us -> 49.8 us
  other arithmetic: 28.9 us -> 14.8 us
    all_to_all x1, waiting for transfers between devices: 51.9 us -> 95.6 us  [on_device(): lax.all_to_all(outgoing, ('row', 'col'), split_axis=0, concat_axis=0, til...]
    scatter x2 -> x4, local copies, waits for them, and re-layouts: 42.7 us -> 2.75 us  [the longest x2 1.55 us: on_device(): inverse = jnp.full((front_blocks,), -1, jnp.int32).at[block_map[child_id]...]
    scatter-add x1 -> x0, other arithmetic: 26 us -> none  [on_device(): assembled = jnp.zeros((dump_slot + 1, BLK, BLK), jnp.float32).at[slot_tar...]
    gather x13 -> x10, local copies, waits for them, and re-layouts: 16.7 us -> 36.5 us  [the longest x3 15.7 us: on_device(): jnp.take(updates.reshape(row_items, BLK, local_cols), inv_k, axis=0)]
    select_n x10 -> x12, other arithmetic: 1 us -> 13.2 us  [the longest x2 4.86 us: on_device(): jnp.take(updates.reshape(row_items, BLK, local_cols), inv_k, axis=0)]
    broadcast_in_dim x2 -> x0, local copies, waits for them, and re-layouts: 6.43 us -> none  [the longest x1 4.28 us: on_device(): jnp.zeros((slot_total, BLK, BLK), jnp.float32)]
    select_n x1, local copies, waits for them, and re-layouts: 0.1 us -> 3.81 us  [on_device(): picked = jnp.where((inv_l >= 0)[None, None, :, None], picked, 0.0)]
    unnamed x14 -> x15, local copies, waits for them, and re-layouts: 7.07 us -> 4.42 us
  transfers between devices with their start and end apart: 19 -> 19, of which waited for: 9 -> 9; matrix products, arithmetic and copies ran while one was open for 15% -> 2% of each run, Pallas kernels for 0% -> 0%
where the time goes in v3:
time: 313 us; the launch traced here: 312 us
  waiting for transfers between devices  180 us (58%)
  local copies, waits for them, and re-layouts  49.8 us (16%)
  starting transfers between devices  39.9 us (13%)
  other arithmetic  14.8 us (5%)
  between operations  14.5 us (5%)
  matrix products  13.3 us (4%)
    all_to_all x1, waiting for transfers between devices, on_device(): lax.all_to_all(outgoing, ('row', 'col'), split_axis=0, concat_axis=0, til...  95.6 us
    all_gather x1, waiting for transfers between devices, on_device(): factor_panel = lax.all_gather(factor_piece, 'col', axis=0, tiled=True)  37.4 us
    all_gather x1, waiting for transfers between devices, on_device(): across = lax.all_gather(moved, 'row', axis=0, tiled=True)  26.8 us
    ppermute x15, starting transfers between devices, on_device(): lax.ppermute(raw_panel[k * piece_rows:(k + 1) * piece_rows], ('row', 'col...  26 us
    gather x3, local copies, waits for them, and re-layouts, on_device(): jnp.take(updates.reshape(row_items, BLK, local_cols), inv_k, axis=0)  15.7 us
    ppermute x15, waiting for transfers between devices, on_device(): lax.ppermute(raw_panel[k * piece_rows:(k + 1) * piece_rows], ('row', 'col...  12.8 us
    all_to_all x1, starting transfers between devices, on_device(): lax.all_to_all(outgoing, ('row', 'col'), split_axis=0, concat_axis=0, til...  11.9 us
    gather x2, local copies, waits for them, and re-layouts, on_device(): jnp.take(incoming, source.reshape(-1), axis=0)  11.7 us
  transfers between devices with their start and end apart: 19, of which 9 were waited for; matrix products, arithmetic and copies ran while one was open for 2% of the time, Pallas kernels for 0%

profile of v3, /device:TPU:1, one launch (start us, length us, event | category | flops | bytes accessed | tf_op | source)
XLA Modules:
  0.0 312.0 jit_solution(4391737214700540643)
XLA Ops:
  9.4 5.0 %gather_fusion = f32[8,128,1024]{2,1,0:T(8,128)} fusion(f32[8,128,1024]{2,1,0:T(8,128)} %bitcast.48, s32[1024]{0:T(1024)S(1)} %pad_clamp_fusion.3), kind=kCustom, calls=%fused_computation.6 | custom fusion | bytes 8388640 | tf_op jit(solution)/shard_map/jit(_take)/gather | solution.py:47
  14.4 5.3 %copy.15 = f32[8,128,1024]{1,2,0:T(8,128)} copy(f32[8,128,1024]{2,1,0:T(8,128)} %gather_fusion) | data formatting | bytes 8388608 | tf_op jit(solution)/shard_map/jit(_take)/gather | solution.py:47
  19.7 5.4 %copy.16 = f32[8,128,8,128]{3,1,2,0:T(8,128)} copy(f32[8,128,8,128]{1,3,2,0:T(8,128)} %bitcast.45) | data formatting | bytes 8388608 | tf_op jit(solution)/shard_map/jit(_take)/gather | solution.py:47
  25.1 4.9 %broadcast_select_fusion = f32[8,128,8,128]{3,1,2,0:T(8,128)} fusion(f32[8,128,8,128]{3,1,2,0:T(8,128)} %copy.16, pred[8]{0:T(512)(128)(4,1)S(1)} %compare_and_fusion.4), kind=kLoop, calls=%fused_computation.16 | loop fusion | flops 1048576 | bytes 8388616 | tf_op jit(solution)/shard_map/jit(_take)/select_n | solution.py:47
  29.9 6.5 %gather_fusion.1 = f32[16,8,128,128]{3,2,1,0:T(8,128)} fusion(f32[8,128,8,128]{3,1,2,0:T(8,128)} %broadcast_select_fusion, s32[1024]{0:T(1024)S(1)} %pad_clamp_fusion.2), kind=kCustom, calls=%fused_computation.7 | custom fusion | bytes 16777280 | tf_op jit(solution)/shard_map/jit(_take)/gather | solution.py:48
  36.5 4.8 %select_bitcast_fusion = f32[8,16,128,128]{3,2,0,1:T(8,128)S(1)} fusion(f32[16,8,128,128]{3,2,1,0:T(8,128)} %gather_fusion.1, pred[16]{0:T(512)(128)(4,1)S(1)} %get-tuple-element.34, pred[16]{0:T(512)(128)(4,1)S(1)} %get-tuple-element.33), kind=kLoop, calls=%fused_computation.12 | loop fusion | flops 4194304 | bytes 16777248 | tf_op jit(solution)/shard_map/jit(_where)/select_n | solution.py:51
  41.3 3.8 %copy.17 = f32[8,16,128,128]{3,2,1,0:T(8,128)} copy(f32[8,16,128,128]{3,2,0,1:T(8,128)S(1)} %select_bitcast_fusion) | data formatting | bytes 16777216 | tf_op jit(solution)/shard_map/jit(_where)/select_n | solution.py:51
  45.1 11.9 %all-to-all-start = ((f32[128,1,128,128]{3,2,1,0:T(8,128)}), f32[128,1,128,128]{3,2,1,0:T(8,128)}, u32[]{:S(2)}, u32[]{:S(2)}) async-start(f32[128,1,128,128]{3,2,1,0:T(8,128)} %bitcast.43), calls=%async_computation | async-start | bytes 16777216 | tf_op jit(solution)/shard_map/all_to_all | solution.py:53
  62.0 95.6 %all-to-all-done = f32[128,1,128,128]{3,2,1,0:T(8,128)} async-done(((f32[128,1,128,128]{3,2,1,0:T(8,128)}), f32[128,1,128,128]{3,2,1,0:T(8,128)}, u32[]{:S(2)}, u32[]{:S(2)}) %all-to-all-start) | async-done | bytes 8388640 | tf_op jit(solution)/shard_map/all_to_all | solution.py:53
  157.6 5.8 %gather_fusion.4 = f32[50,128,128]{2,1,0:T(8,128)} fusion(f32[128,128,128]{2,1,0:T(8,128)} %bitcast.11, s32[1024]{0:T(1024)S(1)} %pad_clamp_fusion.1), kind=kCustom, calls=%fused_computation.2.clone | custom fusion | bytes 6553800 | tf_op jit(solution)/shard_map/jit(_take)/gather | solution.py:72
  163.4 5.8 %gather_fusion.7 = f32[50,128,128]{2,1,0:T(8,128)} fusion(f32[128,128,128]{2,1,0:T(8,128)} %bitcast.11, s32[1024]{0:T(1024)S(1)} %pad_clamp_fusion), kind=kCustom, calls=%fused_computation.5.clone | custom fusion | bytes 6553800 | tf_op jit(solution)/shard_map/jit(_take)/gather | solution.py:72
  169.3 2.4 broadcast_select_fusion.2
  180.2 4.5 %collective-permute-start.10 = (f32[80,512]{1,0:T(8,128)S(1)}, f32[80,512]{1,0:T(8,128)S(1)}, u32[]{:S(2)}, u32[]{:S(2)}) collective-permute-start(f32[80,512]{1,0:T(8,128)S(1)} %get-tuple-element.21), channel_id=1, source_target_pairs={{0,11},{16,27},{32,43},{48,59},{64,75},{80,91},{96,107},{112,123}} | collective-permute-start | bytes 491528 | tf_op jit(solution)/shard_map/ppermute | solution.py:88
  195.8 2.0 collective-permute-start.5
  201.3 2.0 collective-permute-start.7
  205.2 2.0 collective-permute-start.9
  207.2 2.3 collective-permute-done.7
  209.4 3.5 %collective-permute-done.8 = f32[80,512]{1,0:T(8,128)} collective-permute-done((f32[80,512]{1,0:T(8,128)S(1)}, f32[80,512]{1,0:T(8,128)}, u32[]{:S(2)}, u32[]{:S(2)}) %collective-permute-start.8) | collective-permute-done | bytes 163872 | tf_op jit(solution)/shard_map/ppermute | solution.py:88
  213.0 3.5 %collective-permute-done.9 = f32[80,512]{1,0:T(8,128)} collective-permute-done((f32[80,512]{1,0:T(8,128)S(1)}, f32[80,512]{1,0:T(8,128)}, u32[]{:S(2)}, u32[]{:S(2)}) %collective-permute-start.9) | collective-permute-done | bytes 163872 | tf_op jit(solution)/shard_map/ppermute | solution.py:88
  216.5 3.1 fusion.15
  221.6 7.0 %collective-permute-done.15 = f32[80,512]{1,0:T(8,128)S(1)} collective-permute-done((f32[80,512]{1,0:T(8,128)}, f32[80,512]{1,0:T(8,128)S(1)}, u32[]{:S(2)}, u32[]{:S(2)}) %collective-permute-start.15) | collective-permute-done | bytes 163872 | tf_op jit(solution)/shard_map/ppermute | solution.py:104
  229.3 37.4 %all-gather.3.cloned.1.call-done = f32[1280,512]{1,0:T(8,128)} async-done(((f32[80,512]{1,0:T(8,128)}), f32[1280,512]{1,0:T(8,128)}) %all-gather.3.cloned.1.call-update) | async-done | bytes 2621456 | tf_op jit(solution)/shard_map/all_gather | solution.py:97
  266.7 26.8 %all-gather.5.cloned.1.call-done = f32[640,512]{1,0:T(8,128)} async-done(((f32[80,512]{1,0:T(8,128)}), f32[640,512]{1,0:T(8,128)}) %all-gather.5.cloned.1.call-update) | async-done | bytes 1310736 | tf_op jit(solution)/shard_map/all_gather | solution.py:105
  293.5 10.2 %convolution_subtract_fusion = f32[1280,640]{1,0:T(8,128)} fusion(f32[1280,640]{1,0:T(8,128)} %copy-done.1, f32[1280,512]{1,0:T(8,128)} %all-gather.3.cloned.1.call-done, f32[640,512]{1,0:T(8,128)} %all-gather.5.cloned.1.call-done), kind=kOutput, calls=%fused_computation.13 | convolution fusion | flops 5033984000 | bytes 10485760 | tf_op jit(solution)/shard_map/dot_general | solution.py:106
  (91 shorter events, 36.0 us)
Async XLA Ops:
  7.2 209.3 %copy-start = (f32[512,512]{1,0:T(8,128)S(1)}, f32[512,512]{1,0:T(8,128)}, u32[]{:S(2)}) copy-start(f32[512,512]{1,0:T(8,128)} %param.13) | copy-start | bytes 3145732
  45.1 12.0 %copy-start.6 = (s32[2,64]{1,0:T(2,128)S(1)}, s32[2,64]{1,0:T(2,128)}, u32[]{:S(2)}) copy-start(s32[2,64]{1,0:T(2,128)} %param.11) | copy-start | bytes 1540
  45.1 112.5 %all-to-all-start = ((f32[128,1,128,128]{3,2,1,0:T(8,128)}), f32[128,1,128,128]{3,2,1,0:T(8,128)}, u32[]{:S(2)}, u32[]{:S(2)}) async-start(f32[128,1,128,128]{3,2,1,0:T(8,128)} %bitcast.43), calls=%async_computation | async-start | bytes 16777216 | tf_op jit(solution)/shard_map/all_to_all | solution.py:53
  57.0 209.7 %all-gather.3.cloned.1.call-start = ((), (), s32[]{:S(2)}) async-start(), calls=%async_computation.1 | async-start | bytes 2785280 | tf_op jit(solution)/shard_map/all_gather | solution.py:97
  169.3 2.9 copy-start.2
  172.9 2.0 copy-start.5
  177.6 9.8 %collective-permute-start = (f32[80,512]{1,0:T(8,128)S(1)}, f32[80,512]{1,0:T(8,128)S(1)}, u32[]{:S(2)}, u32[]{:S(2)}) collective-permute-start(f32[80,512]{1,0:T(8,128)S(1)} %get-tuple-element.16), channel_id=1, source_target_pairs={{0,1},{16,17},{32,33},{48,49},{64,65},{80,81},{96,97},{112,113}} | collective-permute-start | bytes 491528 | tf_op jit(solution)/shard_map/ppermute | solution.py:88
  178.9 9.8 %collective-permute-start.1 = (f32[80,512]{1,0:T(8,128)S(1)}, f32[80,512]{1,0:T(8,128)S(1)}, u32[]{:S(2)}, u32[]{:S(2)}) collective-permute-start(f32[80,512]{1,0:T(8,128)S(1)} %get-tuple-element.30), channel_id=1, source_target_pairs={{0,2},{16,18},{32,34},{48,50},{64,66},{80,82},{96,98},{112,114}} | collective-permute-start | bytes 491528 | tf_op jit(solution)/shard_map/ppermute | solution.py:88
  180.2 9.8 %collective-permute-start.10 = (f32[80,512]{1,0:T(8,128)S(1)}, f32[80,512]{1,0:T(8,128)S(1)}, u32[]{:S(2)}, u32[]{:S(2)}) collective-permute-start(f32[80,512]{1,0:T(8,128)S(1)} %get-tuple-element.21), channel_id=1, source_target_pairs={{0,11},{16,27},{32,43},{48,59},{64,75},{80,91},{96,107},{112,123}} | collective-permute-start | bytes 491528 | tf_op jit(solution)/shard_map/ppermute | solution.py:88
  184.7 6.6 %collective-permute-start.11 = (f32[80,512]{1,0:T(8,128)S(1)}, f32[80,512]{1,0:T(8,128)S(1)}, u32[]{:S(2)}, u32[]{:S(2)}) collective-permute-start(f32[80,512]{1,0:T(8,128)S(1)} %get-tuple-element.20), channel_id=1, source_target_pairs={{0,12},{16,28},{32,44},{48,60},{64,76},{80,92},{96,108},{112,124}} | collective-permute-start | bytes 491528 | tf_op jit(solution)/shard_map/ppermute | solution.py:88
  186.0 6.6 %collective-permute-start.12 = (f32[80,512]{1,0:T(8,128)S(1)}, f32[80,512]{1,0:T(8,128)S(1)}, u32[]{:S(2)}, u32[]{:S(2)}) collective-permute-start(f32[80,512]{1,0:T(8,128)S(1)} %get-tuple-element.19), channel_id=1, source_target_pairs={{0,13},{16,29},{32,45},{48,61},{64,77},{80,93},{96,109},{112,125}} | collective-permute-start | bytes 491528 | tf_op jit(solution)/shard_map/ppermute | solution.py:88
  187.3 8.5 %collective-permute-start.13 = (f32[80,512]{1,0:T(8,128)S(1)}, f32[80,512]{1,0:T(8,128)S(1)}, u32[]{:S(2)}, u32[]{:S(2)}) collective-permute-start(f32[80,512]{1,0:T(8,128)S(1)} %get-tuple-element.18), channel_id=1, source_target_pairs={{0,14},{16,30},{32,46},{48,62},{64,78},{80,94},{96,110},{112,126}} | collective-permute-start | bytes 491528 | tf_op jit(solution)/shard_map/ppermute | solution.py:88
  188.7 10.7 %collective-permute-start.14 = (f32[80,512]{1,0:T(8,128)S(1)}, f32[80,512]{1,0:T(8,128)S(1)}, u32[]{:S(2)}, u32[]{:S(2)}) collective-permute-start(f32[80,512]{1,0:T(8,128)S(1)} %get-tuple-element.17), channel_id=1, source_target_pairs={{0,15},{16,31},{32,47},{48,63},{64,79},{80,95},{96,111},{112,127}} | collective-permute-start | bytes 491528 | tf_op jit(solution)/shard_map/ppermute | solution.py:88
  190.0 11.3 %collective-permute-start.2 = (f32[80,512]{1,0:T(8,128)S(1)}, f32[80,512]{1,0:T(8,128)S(1)}, u32[]{:S(2)}, u32[]{:S(2)}) collective-permute-start(f32[80,512]{1,0:T(8,128)S(1)} %get-tuple-element.29), channel_id=1, source_target_pairs={{0,3},{16,19},{32,35},{48,51},{64,67},{80,83},{96,99},{112,115}} | collective-permute-start | bytes 491528 | tf_op jit(solution)/shard_map/ppermute | solution.py:88
  191.3 11.9 %collective-permute-start.3 = (f32[80,512]{1,0:T(8,128)S(1)}, f32[80,512]{1,0:T(8,128)S(1)}, u32[]{:S(2)}, u32[]{:S(2)}) collective-permute-start(f32[80,512]{1,0:T(8,128)S(1)} %get-tuple-element.28), channel_id=1, source_target_pairs={{0,4},{16,20},{32,36},{48,52},{64,68},{80,84},{96,100},{112,116}} | collective-permute-start | bytes 491528 | tf_op jit(solution)/shard_map/ppermute | solution.py:88
  192.6 12.6 %collective-permute-start.4 = (f32[80,512]{1,0:T(8,128)S(1)}, f32[80,512]{1,0:T(8,128)S(1)}, u32[]{:S(2)}, u32[]{:S(2)}) collective-permute-start(f32[80,512]{1,0:T(8,128)S(1)} %get-tuple-element.27), channel_id=1, source_target_pairs={{0,5},{16,21},{32,37},{48,53},{64,69},{80,85},{96,101},{112,117}} | collective-permute-start | bytes 491528 | tf_op jit(solution)/shard_map/ppermute | solution.py:88
  195.8 11.3 %collective-permute-start.5 = (f32[80,512]{1,0:T(8,128)S(1)}, f32[80,512]{1,0:T(8,128)}, u32[]{:S(2)}, u32[]{:S(2)}) collective-permute-start(f32[80,512]{1,0:T(8,128)S(1)} %get-tuple-element.26), channel_id=1, source_target_pairs={{0,6},{16,22},{32,38},{48,54},{64,70},{80,86},{96,102},{112,118}} | collective-permute-start | bytes 491528 | tf_op jit(solution)/shard_map/ppermute | solution.py:88
  199.3 7.8 %collective-permute-start.6 = (f32[80,512]{1,0:T(8,128)S(1)}, f32[80,512]{1,0:T(8,128)}, u32[]{:S(2)}, u32[]{:S(2)}) collective-permute-start(f32[80,512]{1,0:T(8,128)S(1)} %get-tuple-element.25), channel_id=1, source_target_pairs={{0,7},{16,23},{32,39},{48,55},{64,71},{80,87},{96,103},{112,119}} | collective-permute-start | bytes 491528 | tf_op jit(solution)/shard_map/ppermute | solution.py:88
  201.3 8.1 %collective-permute-start.7 = (f32[80,512]{1,0:T(8,128)S(1)}, f32[80,512]{1,0:T(8,128)}, u32[]{:S(2)}, u32[]{:S(2)}) collective-permute-start(f32[80,512]{1,0:T(8,128)S(1)} %get-tuple-element.24), channel_id=1, source_target_pairs={{0,8},{16,24},{32,40},{48,56},{64,72},{80,88},{96,104},{112,120}} | collective-permute-start | bytes 491528 | tf_op jit(solution)/shard_map/ppermute | solution.py:88
  203.3 9.7 %collective-permute-start.8 = (f32[80,512]{1,0:T(8,128)S(1)}, f32[80,512]{1,0:T(8,128)}, u32[]{:S(2)}, u32[]{:S(2)}) collective-permute-start(f32[80,512]{1,0:T(8,128)S(1)} %get-tuple-element.23), channel_id=1, source_target_pairs={{0,9},{16,25},{32,41},{48,57},{64,73},{80,89},{96,105},{112,121}} | collective-permute-start | bytes 491528 | tf_op jit(solution)/shard_map/ppermute | solution.py:88
  205.2 11.3 %collective-permute-start.9 = (f32[80,512]{1,0:T(8,128)S(1)}, f32[80,512]{1,0:T(8,128)}, u32[]{:S(2)}, u32[]{:S(2)}) collective-permute-start(f32[80,512]{1,0:T(8,128)S(1)} %get-tuple-element.22), channel_id=1, source_target_pairs={{0,10},{16,26},{32,42},{48,58},{64,74},{80,90},{96,106},{112,122}} | collective-permute-start | bytes 491528 | tf_op jit(solution)/shard_map/ppermute | solution.py:88
  219.6 73.9 %all-gather.5.cloned.1.call-start = ((), (), s32[]{:S(2)}) async-start(), calls=%async_computation.2 | async-start | bytes 1474560 | tf_op jit(solution)/shard_map/all_gather | solution.py:105
  219.7 8.9 %collective-permute-start.15 = (f32[80,512]{1,0:T(8,128)}, f32[80,512]{1,0:T(8,128)S(1)}, u32[]{:S(2)}, u32[]{:S(2)}) collective-permute-start(f32[80,512]{1,0:T(8,128)} %fusion.15), channel_id=1, source_target_pairs={{0,0},{1,16},{2,32},{3,48},{4,64},{5,80},{6,96},{7,112},{8,1},{9,1... | collective-permute-start | bytes 491528 | tf_op jit(solution)/shard_map/ppermute | solution.py:104
  293.5 10.2 %copy-start.3 = (f32[1280,512]{1,0:T(8,128)S(1)}, f32[1280,512]{1,0:T(8,128)}, u32[]{:S(2)}) copy-start(f32[1280,512]{1,0:T(8,128)} %all-gather.3.cloned.1.call-done) | copy-start | bytes 7864324
  (2 other events, 2.4 us)
Sparse Core Ops, SparseCore 0:
  219.7 46.9 all-gather.2
  268.4 25.0 all-gather.4

commit v4 on v3

v4 whole, which is shorter than its diff:
```python
import jax
import jax.numpy as jnp
from jax import lax
from jax.sharding import PartitionSpec as P

F = 10240
M = 8192
BLK = 128
PANEL = 512


def on_device(updates, block_map, own_diag, panel_inverse):
    row_count = lax.axis_size("row")
    col_count = lax.axis_size("col")
    row_index = lax.axis_index("row")
    col_index = lax.axis_index("col")
    local_rows, local_cols = updates.shape
    row_items = local_rows // BLK
    col_items = local_cols // BLK
    assert row_items == row_count
    half_cols = col_count // 2
    front_blocks = F // BLK
    front_rows = front_blocks // row_count
    front_cols = front_blocks // col_count
    height = front_rows * BLK
    col_width = front_cols * BLK
    panel_blocks = PANEL // BLK
    child_blocks = block_map.shape[1]
    block_map = block_map.astype(jnp.int32)
    child = col_index // half_cols
    child_map = jnp.take(block_map, child, axis=0)
    row_parent = lax.dynamic_slice_in_dim(child_map, col_index % half_cols * row_items, row_items)
    inv_k = (
        jnp.zeros((row_count,), jnp.int32)
        .at[row_parent // front_rows]
        .set(jnp.arange(row_items, dtype=jnp.int32))
    )
    sorted_rows = jnp.take(updates.reshape(row_items, BLK, local_cols), inv_k, axis=0)
    row_block = lax.all_to_all(sorted_rows, "row", split_axis=0, concat_axis=0, tiled=True)
    tiles = (
        row_block.reshape(row_count, BLK, col_items, BLK)
        .transpose(0, 2, 1, 3)
        .reshape(row_count * col_items, BLK, BLK)
    )
    inverses = [
        jnp.full((front_blocks,), child_blocks, jnp.int32)
        .at[block_map[c]]
        .set(jnp.arange(child_blocks, dtype=jnp.int32))
        for c in range(2)
    ]
    my_inverse = jnp.where(child == 0, inverses[0], inverses[1])
    by_front_col = jnp.take(tiles, my_inverse, axis=0, mode="fill", fill_value=0.0)
    panel_part = by_front_col[:panel_blocks].transpose(1, 0, 2).reshape(BLK, PANEL)
    panel_parts = lax.all_gather(panel_part, "col", axis=0, tiled=False)
    outgoing = by_front_col.reshape(col_count, front_cols, BLK, BLK)
    incoming = lax.all_to_all(outgoing, "col", split_axis=0, concat_axis=0, tiled=True)
    my_rows = row_index * front_rows + jnp.arange(front_rows, dtype=jnp.int32)
    sources = []
    for c in range(2):
        a = jnp.take(inverses[c], my_rows)
        sources.append(jnp.where(a < child_blocks, c * half_cols + a // row_items, col_count))
    row_global = row_index * height + jnp.arange(height, dtype=jnp.int32)
    panel_raw = None
    for src in sources:
        part = jnp.take(panel_parts, src, axis=0, mode="fill", fill_value=0.0)
        panel_raw = part if panel_raw is None else panel_raw + part
    panel_raw = panel_raw.reshape(height, PANEL)
    panel_raw = panel_raw + jnp.where(
        row_global[:, None] == jnp.arange(PANEL, dtype=jnp.int32)[None, :], own_diag[:, None], 0.0
    )
    factor_panel = jnp.dot(
        panel_raw,
        panel_inverse.T,
        precision=lax.Precision.HIGHEST,
        preferred_element_type=jnp.float32,
    )
    piece_rows = col_width // row_count
    ratio = col_count // row_count
    received = []
    for q in range(row_count):
        chunk = lax.dynamic_slice_in_dim(
            factor_panel, (col_index // row_count) * col_width + q * piece_rows, piece_rows, 0
        )
        pairs = [
            (
                r * col_count + t,
                ((t % row_count - q) % row_count) * col_count + r * ratio + t // row_count,
            )
            for r in range(row_count)
            for t in range(col_count)
        ]
        received.append(lax.ppermute(chunk, ("row", "col"), pairs))
    across = jnp.concatenate(received, axis=0)
    incoming = incoming.reshape(col_count, front_cols, BLK, BLK)
    front_tiles = None
    for src in sources:
        part = jnp.take(incoming, src, axis=0, mode="fill", fill_value=0.0)
        front_tiles = part if front_tiles is None else front_tiles + part
    front_local = front_tiles.transpose(0, 2, 1, 3).reshape(height, col_width)
    col_global = col_index * col_width + jnp.arange(col_width, dtype=jnp.int32)
    front_local = front_local + jnp.where(
        row_global[:, None] == col_global[None, :], own_diag[:, None], 0.0
    )
    update_term = lax.dot_general(
        factor_panel,
        across,
        (((1,), (1,)), ((), ())),
        precision=lax.Precision.HIGHEST,
        preferred_element_type=jnp.float32,
    )
    trailing = front_local - update_term
    return (factor_panel, trailing)


def solution(mesh):
    return jax.shard_map(
        on_device,
        mesh=mesh,
        in_specs=(P("col", "row"), P(), P("row"), P()),
        out_specs=(P("row", None), P("row", "col")),
        check_vma=False,
    )
```

time: 313 us -> 315 us (level)
  the two profiles are of different devices: /device:TPU:1 before, /device:TPU:43 now
where the time goes in v4:
time: 315 us; the launch traced here: 314 us
  waiting for transfers between devices  125 us (40%)
  blocking collectives  53.7 us (17%)
  local copies, waits for them, and re-layouts  46.5 us (15%)
  starting transfers between devices  44.7 us (14%)
  other arithmetic  15.8 us (5%)
  between operations  14.5 us (5%)
  matrix products  13.2 us (4%)
    all_to_all x1, waiting for transfers between devices, on_device(): lax.all_to_all(outgoing, 'col', split_axis=0, concat_axis=0, tiled=True)  67.3 us
    all_to_all x1, blocking collectives, on_device(): lax.all_to_all(sorted_rows, 'row', split_axis=0, concat_axis=0, tiled=True)  53.7 us
    ppermute x8, starting transfers between devices, on_device(): received.append(lax.ppermute(chunk, ('row', 'col'), pairs))  37.9 us
    ppermute x8, waiting for transfers between devices, on_device(): received.append(lax.ppermute(chunk, ('row', 'col'), pairs))  35.3 us
    all_gather x1, waiting for transfers between devices, on_device(): panel_parts = lax.all_gather(panel_part, 'col', axis=0, tiled=False)  22.7 us
    gather x2, local copies, waits for them, and re-layouts, on_device(): part = jnp.take(incoming, src, axis=0, mode='fill', fill_value=0.0)  9.93 us
    gather x2, local copies, waits for them, and re-layouts, on_device(): part = jnp.take(panel_parts, src, axis=0, mode='fill', fill_value=0.0)  8.79 us
    dot_general x1, matrix products, on_device(): lax.dot_general(factor_panel, across, (((1,), (1,)), ((), ())), precision...  8.62 us
  transfers between devices with their start and end apart: 10, of which 6 were waited for; matrix products, arithmetic and copies ran while one was open for 6% of the time, Pallas kernels for 0%

profile of v4, /device:TPU:43, one launch (start us, length us, event | category | flops | bytes accessed | tf_op | source)
XLA Modules:
  0.0 313.7 jit_solution(10839079553388574987)
XLA Ops:
  11.1 5.0 %gather_fusion = f32[8,128,1024]{2,1,0:T(8,128)} fusion(f32[8,128,1024]{2,1,0:T(8,128)} %bitcast.44, s32[1024]{0:T(1024)S(1)} %get-tuple-element.35), kind=kCustom, calls=%fused_computation.6 | custom fusion | bytes 8388640 | tf_op jit(solution)/shard_map/jit(_take)/gather | solution.py:38
  18.7 53.7 %all_to_all.10 = f32[8,128,1024]{2,1,0:T(8,128)} all-to-all(f32[8,128,1024]{2,1,0:T(8,128)S(1)} %broadcast_select_fusion.1), channel_id=1, replica_groups=mesh['row'=8,'col'=16] {'row'}, dimensions={0} | all-to-all | bytes 8388608 | tf_op jit(solution)/shard_map/all_to_all | solution.py:39
  72.4 5.3 %copy.17 = f32[8,128,1024]{1,2,0:T(8,128)} copy(f32[8,128,1024]{2,1,0:T(8,128)} %all_to_all.10) | data formatting | bytes 8388608 | tf_op jit(solution)/shard_map/all_to_all | solution.py:39
  77.8 5.4 %copy.18 = f32[8,8,128,128]{3,2,1,0:T(8,128)} copy(f32[8,8,128,128]{2,3,1,0:T(8,128)} %bitcast.42) | data formatting | bytes 8388608 | tf_op jit(solution)/shard_map/transpose | solution.py:42
  83.2 5.4 %gather_fusion.1 = f32[80,128,128]{2,1,0:T(8,128)} fusion(f32[64,128,128]{2,1,0:T(8,128)} %bitcast.41, s32[1024]{0:T(1024)S(1)} %get-tuple-element.34), kind=kCustom, calls=%fused_computation.7 | custom fusion | bytes 10486080 | tf_op jit(solution)/shard_map/jit(_take)/gather | solution.py:52
  90.7 5.3 %broadcast_select_fusion = f32[16,5,128,128]{3,2,1,0:T(8,128)} fusion(f32[16,5,128,128]{3,2,1,0:T(8,128)} %bitcast.40, pred[16,5]{1,0:T(8,128)(4,1)S(1)} %broadcast_in_dim.116), kind=kLoop, calls=%fused_computation.17 | loop fusion | flops 1310720 | bytes 10485840 | tf_op jit(solution)/shard_map/jit(_take)/select_n | solution.py:52
  96.0 6.8 %all-to-all-start.1 = ((f32[16,5,128,128]{3,2,1,0:T(8,128)}), f32[16,5,128,128]{3,2,1,0:T(8,128)}, u32[]{:S(2)}, u32[]{:S(2)}) async-start(f32[16,5,128,128]{3,2,1,0:T(8,128)} %broadcast_select_fusion), calls=%async_computation.1 | async-start | bytes 10485760 | tf_op jit(solution)/shard_map/all_to_all | solution.py:56
  104.2 67.3 %all-to-all-done.1 = f32[16,5,128,128]{3,2,1,0:T(8,128)} async-done(((f32[16,5,128,128]{3,2,1,0:T(8,128)}), f32[16,5,128,128]{3,2,1,0:T(8,128)}, u32[]{:S(2)}, u32[]{:S(2)}) %all-to-all-start.1) | async-done | bytes 5242912 | tf_op jit(solution)/shard_map/all_to_all | solution.py:56
  171.5 4.9 %gather_fusion.7 = f32[10,5,128,128]{3,2,1,0:T(8,128)} fusion(f32[16,5,128,128]{3,2,1,0:T(8,128)} %all-to-all-done.1, s32[1024]{0:T(1024)S(1)} %pad_clamp_fusion), kind=kCustom, calls=%fused_computation.5.clone | custom fusion | bytes 6553640 | tf_op jit(solution)/shard_map/jit(_take)/gather | solution.py:97
  176.5 5.0 %gather_fusion.6 = f32[10,5,128,128]{3,2,1,0:T(8,128)} fusion(f32[16,5,128,128]{3,2,1,0:T(8,128)} %all-to-all-done.1, s32[1024]{0:T(1024)S(1)} %pad_clamp_fusion.1), kind=kCustom, calls=%fused_computation.2.clone | custom fusion | bytes 6553640 | tf_op jit(solution)/shard_map/jit(_take)/gather | solution.py:97
  181.5 22.7 %all-gather.2.cloned.1.call-done = f32[16,128,512]{2,1,0:T(8,128)} async-done(((f32[1,128,512]{2,1,0:T(8,128)}), f32[16,128,512]{2,1,0:T(8,128)}) %all-gather.2.cloned.1.call-update) | async-done | bytes 4194320 | tf_op jit(solution)/shard_map/all_gather | solution.py:54
  204.2 4.4 %gather_fusion.5 = f32[10,128,512]{2,1,0:T(8,128)} fusion(f32[16,128,512]{2,1,0:T(8,128)} %all-gather.2.cloned.1.call-done, s32[1024]{0:T(1024)S(1)} %pad_clamp_fusion), kind=kCustom, calls=%fused_computation.4.clone | custom fusion | bytes 5242920 | tf_op jit(solution)/shard_map/jit(_take)/gather | solution.py:65
  208.5 4.4 %gather_fusion.3 = f32[10,128,512]{2,1,0:T(8,128)} fusion(f32[16,128,512]{2,1,0:T(8,128)} %all-gather.2.cloned.1.call-done, s32[1024]{0:T(1024)S(1)} %pad_clamp_fusion.1), kind=kCustom, calls=%fused_computation.1.clone | custom fusion | bytes 5242920 | tf_op jit(solution)/shard_map/jit(_take)/gather | solution.py:65
  217.1 4.5 %fusion.10 = f32[1280,512]{1,0:T(8,128)S(1)} fusion(f32[1280,512]{1,0:T(8,128)S(1)} %bitcast_add_fusion.1, f32[512,512]{1,0:T(8,128)S(1)} %copy-done), kind=kOutput, calls=%fused_computation.81 | convolution fusion | flops 4026531840 | bytes 6291456 | tf_op jit(solution)/shard_map/dot_general | solution.py:71
  221.8 3.4 %collective-permute-start = (f32[80,512]{1,0:T(8,128)S(1)}, f32[80,512]{1,0:T(8,128)S(1)}, u32[]{:S(2)}, u32[]{:S(2)}) collective-permute-start(f32[80,512]{1,0:T(8,128)S(1)} %get-tuple-element.29), channel_id=1, source_target_pairs={{0,0},{1,16},{2,32},{3,48},{4,64},{5,80},{6,96},{7,112},{8,1},{9,1... | collective-permute-start | bytes 491528 | tf_op jit(solution)/shard_map/ppermute | solution.py:92
  225.2 8.2 %collective-permute-start.1 = (f32[80,512]{1,0:T(8,128)S(1)}, f32[80,512]{1,0:T(8,128)S(1)}, u32[]{:S(2)}, u32[]{:S(2)}) collective-permute-start(f32[80,512]{1,0:T(8,128)S(1)} %get-tuple-element.28), channel_id=1, source_target_pairs={{0,112},{1,0},{2,16},{3,32},{4,48},{5,64},{6,80},{7,96},{8,113},{9... | collective-permute-start | bytes 491528 | tf_op jit(solution)/shard_map/ppermute | solution.py:92
  241.9 4.9 %collective-permute-start.4 = (f32[80,512]{1,0:T(8,128)S(1)}, f32[80,512]{1,0:T(8,128)S(1)}, u32[]{:S(2)}, u32[]{:S(2)}) collective-permute-start(f32[80,512]{1,0:T(8,128)S(1)} %get-tuple-element.25), channel_id=1, source_target_pairs={{0,64},{1,80},{2,96},{3,112},{4,0},{5,16},{6,32},{7,48},{8,65},{9,... | collective-permute-start | bytes 491528 | tf_op jit(solution)/shard_map/ppermute | solution.py:92
  246.8 6.1 %collective-permute-start.5 = (f32[80,512]{1,0:T(8,128)S(1)}, f32[80,512]{1,0:T(8,128)S(1)}, u32[]{:S(2)}, u32[]{:S(2)}) collective-permute-start(f32[80,512]{1,0:T(8,128)S(1)} %get-tuple-element.24), channel_id=1, source_target_pairs={{0,48},{1,64},{2,80},{3,96},{4,112},{5,0},{6,16},{7,32},{8,49},{9,... | collective-permute-start | bytes 491528 | tf_op jit(solution)/shard_map/ppermute | solution.py:92
  254.9 7.9 %collective-permute-start.7 = (f32[80,512]{1,0:T(8,128)S(1)}, f32[80,512]{1,0:T(8,128)S(1)}, u32[]{:S(2)}, u32[]{:S(2)}) collective-permute-start(f32[80,512]{1,0:T(8,128)S(1)} %get-tuple-element.22), channel_id=1, source_target_pairs={{0,16},{1,32},{2,48},{3,64},{4,80},{5,96},{6,112},{7,0},{8,17},{9,... | collective-permute-start | bytes 491528 | tf_op jit(solution)/shard_map/ppermute | solution.py:92
  262.9 6.3 %collective-permute-done.4 = f32[80,512]{1,0:T(8,128)S(1)} collective-permute-done((f32[80,512]{1,0:T(8,128)S(1)}, f32[80,512]{1,0:T(8,128)S(1)}, u32[]{:S(2)}, u32[]{:S(2)}) %collective-permute-start.4) | collective-permute-done | bytes 163872 | tf_op jit(solution)/shard_map/ppermute | solution.py:92
  269.2 10.4 %collective-permute-done.5 = f32[80,512]{1,0:T(8,128)S(1)} collective-permute-done((f32[80,512]{1,0:T(8,128)S(1)}, f32[80,512]{1,0:T(8,128)S(1)}, u32[]{:S(2)}, u32[]{:S(2)}) %collective-permute-start.5) | collective-permute-done | bytes 163872 | tf_op jit(solution)/shard_map/ppermute | solution.py:92
  279.6 9.4 %collective-permute-done.6 = f32[80,512]{1,0:T(8,128)S(1)} collective-permute-done((f32[80,512]{1,0:T(8,128)S(1)}, f32[80,512]{1,0:T(8,128)S(1)}, u32[]{:S(2)}, u32[]{:S(2)}) %collective-permute-start.6) | collective-permute-done | bytes 163872 | tf_op jit(solution)/shard_map/ppermute | solution.py:92
  289.0 9.2 %collective-permute-done.7 = f32[80,512]{1,0:T(8,128)S(1)} collective-permute-done((f32[80,512]{1,0:T(8,128)S(1)}, f32[80,512]{1,0:T(8,128)S(1)}, u32[]{:S(2)}, u32[]{:S(2)}) %collective-permute-start.7) | collective-permute-done | bytes 163872 | tf_op jit(solution)/shard_map/ppermute | solution.py:92
  298.3 8.6 %convolution_subtract_fusion = f32[1280,640]{1,0:T(8,128)} fusion(f32[1280,512]{1,0:T(8,128)S(1)} %fusion.10, f32[640,512]{1,0:T(8,128)S(1)} %constant_dynamic-update-slice_fusion, f32[160,8,5,128]{3,2,1,0:T(8,128)S(1)} %bitcast.43, f32[1280]{0:T(1024)S(1)} %copy-done.4, s32[640]{0:T(1024)S(1)} %iota_add_fusion.1, s32[1280]{0:T(1024)S(1)} %iota_add_fusion), kind=kOutput, calls=%fused_computation.11 | convolution fusion | flops 5036441600 | bytes 10498560 | tf_op jit(solution)/shard_map/dot_general | solution.py:104
  (59 shorter events, 24.7 us)
Async XLA Ops:
  7.2 209.9 %copy-start = (f32[512,512]{1,0:T(8,128)S(1)}, f32[512,512]{1,0:T(8,128)}, u32[]{:S(2)}) copy-start(f32[512,512]{1,0:T(8,128)} %param.13) | copy-start | bytes 3145732
  7.2 197.0 %all-gather.2.cloned.1.call-start = ((), (), s32[]{:S(2)}) async-start(), calls=%async_computation.2 | async-start | bytes 4456448 | tf_op jit(solution)/shard_map/all_gather | solution.py:54
  96.0 75.6 %all-to-all-start.1 = ((f32[16,5,128,128]{3,2,1,0:T(8,128)}), f32[16,5,128,128]{3,2,1,0:T(8,128)}, u32[]{:S(2)}, u32[]{:S(2)}) async-start(f32[16,5,128,128]{3,2,1,0:T(8,128)} %broadcast_select_fusion), calls=%async_computation.1 | async-start | bytes 10485760 | tf_op jit(solution)/shard_map/all_to_all | solution.py:56
  212.9 3.3 %copy-start.4 = (f32[1280]{0:T(1024)S(1)}, f32[1280]{0:T(1024)}, u32[]{:S(2)}) copy-start(f32[1280]{0:T(1024)} %param.12) | copy-start | bytes 15364
  217.1 16.3 %copy-start.2 = (f32[10,5,128,128]{3,2,1,0:T(8,128)S(1)}, f32[10,5,128,128]{3,2,1,0:T(8,128)}, u32[]{:S(2)}) copy-start(f32[10,5,128,128]{3,2,1,0:T(8,128)} %gather_fusion.7) | copy-start | bytes 9830404
  217.1 16.3 %copy-start.3 = (f32[10,5,128,128]{3,2,1,0:T(8,128)S(1)}, f32[10,5,128,128]{3,2,1,0:T(8,128)}, u32[]{:S(2)}) copy-start(f32[10,5,128,128]{3,2,1,0:T(8,128)} %gather_fusion.6) | copy-start | bytes 9830404
  221.7 76.6 %copy-start.1 = (f32[1280,512]{1,0:T(8,128)}, f32[1280,512]{1,0:T(8,128)S(1)}, u32[]{:S(2)}) copy-start(f32[1280,512]{1,0:T(8,128)S(1)} %fusion.10) | copy-start | bytes 7864324
  221.8 24.9 %collective-permute-start = (f32[80,512]{1,0:T(8,128)S(1)}, f32[80,512]{1,0:T(8,128)S(1)}, u32[]{:S(2)}, u32[]{:S(2)}) collective-permute-start(f32[80,512]{1,0:T(8,128)S(1)} %get-tuple-element.29), channel_id=1, source_target_pairs={{0,0},{1,16},{2,32},{3,48},{4,64},{5,80},{6,96},{7,112},{8,1},{9,1... | collective-permute-start | bytes 491528 | tf_op jit(solution)/shard_map/ppermute | solution.py:92
  225.2 27.7 %collective-permute-start.1 = (f32[80,512]{1,0:T(8,128)S(1)}, f32[80,512]{1,0:T(8,128)S(1)}, u32[]{:S(2)}, u32[]{:S(2)}) collective-permute-start(f32[80,512]{1,0:T(8,128)S(1)} %get-tuple-element.28), channel_id=1, source_target_pairs={{0,112},{1,0},{2,16},{3,32},{4,48},{5,64},{6,80},{7,96},{8,113},{9... | collective-permute-start | bytes 491528 | tf_op jit(solution)/shard_map/ppermute | solution.py:92
  236.4 18.5 %collective-permute-start.2 = (f32[80,512]{1,0:T(8,128)S(1)}, f32[80,512]{1,0:T(8,128)S(1)}, u32[]{:S(2)}, u32[]{:S(2)}) collective-permute-start(f32[80,512]{1,0:T(8,128)S(1)} %get-tuple-element.27), channel_id=1, source_target_pairs={{0,96},{1,112},{2,0},{3,16},{4,32},{5,48},{6,64},{7,80},{8,97},{9,... | collective-permute-start | bytes 491528 | tf_op jit(solution)/shard_map/ppermute | solution.py:92
  238.7 24.2 %collective-permute-start.3 = (f32[80,512]{1,0:T(8,128)S(1)}, f32[80,512]{1,0:T(8,128)S(1)}, u32[]{:S(2)}, u32[]{:S(2)}) collective-permute-start(f32[80,512]{1,0:T(8,128)S(1)} %get-tuple-element.26), channel_id=1, source_target_pairs={{0,80},{1,96},{2,112},{3,0},{4,16},{5,32},{6,48},{7,64},{8,81},{9,... | collective-permute-start | bytes 491528 | tf_op jit(solution)/shard_map/ppermute | solution.py:92
  241.9 27.3 %collective-permute-start.4 = (f32[80,512]{1,0:T(8,128)S(1)}, f32[80,512]{1,0:T(8,128)S(1)}, u32[]{:S(2)}, u32[]{:S(2)}) collective-permute-start(f32[80,512]{1,0:T(8,128)S(1)} %get-tuple-element.25), channel_id=1, source_target_pairs={{0,64},{1,80},{2,96},{3,112},{4,0},{5,16},{6,32},{7,48},{8,65},{9,... | collective-permute-start | bytes 491528 | tf_op jit(solution)/shard_map/ppermute | solution.py:92
  246.8 32.8 %collective-permute-start.5 = (f32[80,512]{1,0:T(8,128)S(1)}, f32[80,512]{1,0:T(8,128)S(1)}, u32[]{:S(2)}, u32[]{:S(2)}) collective-permute-start(f32[80,512]{1,0:T(8,128)S(1)} %get-tuple-element.24), channel_id=1, source_target_pairs={{0,48},{1,64},{2,80},{3,96},{4,112},{5,0},{6,16},{7,32},{8,49},{9,... | collective-permute-start | bytes 491528 | tf_op jit(solution)/shard_map/ppermute | solution.py:92
  252.9 36.1 %collective-permute-start.6 = (f32[80,512]{1,0:T(8,128)S(1)}, f32[80,512]{1,0:T(8,128)S(1)}, u32[]{:S(2)}, u32[]{:S(2)}) collective-permute-start(f32[80,512]{1,0:T(8,128)S(1)} %get-tuple-element.23), channel_id=1, source_target_pairs={{0,32},{1,48},{2,64},{3,80},{4,96},{5,112},{6,0},{7,16},{8,33},{9,... | collective-permute-start | bytes 491528 | tf_op jit(solution)/shard_map/ppermute | solution.py:92
  254.9 43.4 %collective-permute-start.7 = (f32[80,512]{1,0:T(8,128)S(1)}, f32[80,512]{1,0:T(8,128)S(1)}, u32[]{:S(2)}, u32[]{:S(2)}) collective-permute-start(f32[80,512]{1,0:T(8,128)S(1)} %get-tuple-element.22), channel_id=1, source_target_pairs={{0,16},{1,32},{2,48},{3,64},{4,80},{5,96},{6,112},{7,0},{8,17},{9,... | collective-permute-start | bytes 491528 | tf_op jit(solution)/shard_map/ppermute | solution.py:92
Sparse Core Ops, SparseCore 0:
  90.7 113.3 all-gather.1

commit v5 on v3

--- a/solution.py
+++ b/solution.py
@@ -7,11 +7,6 @@
 M = 8192
 BLK = 128
 PANEL = 512
-
-
-def broadcast(shard, axis, root):
-    mine = lax.axis_index(axis) == root
-    return lax.psum(jnp.where(mine, shard, jnp.zeros_like(shard)), axis)
 
 
 def on_device(updates, block_map, own_diag, panel_inverse):
@@ -44,18 +39,19 @@
         .at[col_parent // front_cols]
         .set(jnp.arange(col_items, dtype=jnp.int32))
     )
-    row_sorted = jnp.take(updates.reshape(row_items, BLK, local_cols), inv_k, axis=0)
-    picked = jnp.take(
-        row_sorted.reshape(row_count, BLK, col_items, BLK), jnp.maximum(inv_l, 0), axis=2
+    fill_l = jnp.where(inv_l >= 0, inv_l, col_items)
+    outgoing = (
+        updates.reshape(row_items, BLK, col_items, BLK)
+        .at[inv_k[:, None], :, fill_l[None, :], :]
+        .get(mode="fill", fill_value=0.0)
+        .reshape(devices_all, 1, BLK, BLK)
     )
-    picked = jnp.where((inv_l >= 0)[None, None, :, None], picked, 0.0)
-    outgoing = picked.transpose(0, 2, 1, 3).reshape(devices_all, 1, BLK, BLK)
     incoming = lax.all_to_all(
         outgoing, ("row", "col"), split_axis=0, concat_axis=0, tiled=True
     ).reshape(devices_all, BLK, BLK)
-    slots = jnp.arange(front_blocks, dtype=jnp.int32)
     my_rows = row_index * front_rows + jnp.arange(front_rows, dtype=jnp.int32)
     my_cols = col_index * front_cols + jnp.arange(front_cols, dtype=jnp.int32)
+    lanes = jnp.arange(BLK, dtype=jnp.int32)
     front_local = None
     for child_id in range(2):
         inverse = (
@@ -69,12 +65,12 @@
             child_id * half_cols + jnp.maximum(a, 0) // row_items
         )[:, None]
         valid = (a >= 0)[:, None] & (b >= 0)[None, :]
-        part = jnp.take(incoming, source.reshape(-1), axis=0).reshape(
-            front_rows, front_cols, BLK, BLK
+        source = jnp.where(valid, source, devices_all)
+        part = incoming.at[source[:, None, :], lanes[None, :, None], :].get(
+            mode="fill", fill_value=0.0
         )
-        part = jnp.where(valid[:, :, None, None], part, 0.0)
         front_local = part if front_local is None else front_local + part
-    front_local = front_local.transpose(0, 2, 1, 3).reshape(height, col_width)
+    front_local = front_local.reshape(height, col_width)
     row_global = row_index * height + jnp.arange(height, dtype=jnp.int32)
     col_global = col_index * col_width + jnp.arange(col_width, dtype=jnp.int32)
     front_local = front_local + jnp.where(
@@ -102,7 +98,12 @@
         for k in range(col_count)
     ]
     moved = lax.ppermute(factor_piece, ("row", "col"), pairs)
-    across = lax.all_gather(moved, "row", axis=0, tiled=True)
+    stack = [moved]
+    for q in range(1, row_count):
+        shift = [(r, (r + q) % row_count) for r in range(row_count)]
+        stack.append(lax.ppermute(moved, "row", shift))
+    order = (row_index - jnp.arange(row_count, dtype=jnp.int32)) % row_count
+    across = jnp.take(jnp.stack(stack), order, axis=0).reshape(col_width, PANEL)
     update_term = lax.dot_general(
         factor_panel,
         across,

time: 313 us -> 393 us (1.26)
  local copies, waits for them, and re-layouts: 49.8 us -> 159 us
  waiting for transfers between devices: 180 us -> 136 us
  starting transfers between devices: 39.9 us -> 51.8 us
    gather x6, local copies, waits for them, and re-layouts: 33.9 us -> 141 us  [the longest x4 133 us: on_device(): incoming.at[source[:, None, :], lanes[None, :, None], :]]
    all_gather x1 -> x0, waiting for transfers between devices: 26.8 us -> none  [on_device(): across = lax.all_gather(moved, 'row', axis=0, tiled=True)]
    all_gather x1, waiting for transfers between devices: 37.4 us -> 11 us  [on_device(): factor_panel = lax.all_gather(factor_piece, 'col', axis=0, tiled=True)]
    ppermute x0 -> x7, waiting for transfers between devices: none -> 12 us  [on_device(): stack.append(lax.ppermute(moved, 'row', shift))]
    ppermute x0 -> x7, starting transfers between devices: none -> 11.7 us  [on_device(): stack.append(lax.ppermute(moved, 'row', shift))]
    add x3 -> x1, other arithmetic: 0.16 us -> 5.55 us  [on_device(): front_local = part if front_local is None else front_local + part]
  transfers between devices with their start and end apart: 19 -> 25, of which waited for: 9 -> 14; matrix products, arithmetic and copies ran while one was open for 2% -> 3% of each run, Pallas kernels for 0% -> 0%
where the time goes in v5:
time: 393 us; the launch traced here: 390 us
  local copies, waits for them, and re-layouts  159 us (40%)
  waiting for transfers between devices  136 us (35%)
  starting transfers between devices  51.8 us (13%)
  other arithmetic  16.6 us (4%)
  between operations  14.6 us (4%)
  matrix products  12.9 us (3%)
    gather x4, local copies, waits for them, and re-layouts, on_device(): incoming.at[source[:, None, :], lanes[None, :, None], :]  133 us
    all_to_all x1, waiting for transfers between devices, on_device(): lax.all_to_all(outgoing, ('row', 'col'), split_axis=0, concat_axis=0, til...  93.1 us
    ppermute x15, starting transfers between devices, on_device(): lax.ppermute(raw_panel[k * piece_rows:(k + 1) * piece_rows], ('row', 'col...  26.2 us
    ppermute x15, waiting for transfers between devices, on_device(): lax.ppermute(raw_panel[k * piece_rows:(k + 1) * piece_rows], ('row', 'col...  12.6 us
    ppermute x7, waiting for transfers between devices, on_device(): stack.append(lax.ppermute(moved, 'row', shift))  12 us
    all_to_all x1, starting transfers between devices, on_device(): lax.all_to_all(outgoing, ('row', 'col'), split_axis=0, concat_axis=0, til...  11.9 us
    ppermute x7, starting transfers between devices, on_device(): stack.append(lax.ppermute(moved, 'row', shift))  11.7 us
    all_gather x1, waiting for transfers between devices, on_device(): factor_panel = lax.all_gather(factor_piece, 'col', axis=0, tiled=True)  11 us
  transfers between devices with their start and end apart: 25, of which 14 were waited for; matrix products, arithmetic and copies ran while one was open for 3% of the time, Pallas kernels for 0%

profile of v5, /device:TPU:1, one launch (start us, length us, event | category | flops | bytes accessed | tf_op | source)
XLA Modules:
  0.0 390.4 jit_solution(3016989263311851734)
XLA Ops:
  9.5 3.2 copy.17
  12.7 2.7 copy.12
  15.6 6.5 %gather_fusion = f32[128,128,128]{2,1,0:T(8,128)} fusion(f32[8,128,8,128]{3,1,2,0:T(8,128)} %copy.12, s32[128]{0:T(128)S(1)} %reshape.345), kind=kCustom, calls=%fused_computation.4 | custom fusion | bytes 16778240 | tf_op jit(solution)/shard_map/gather | solution.py:46
  22.1 7.2 %fusion = f32[128,1,128,128]{3,2,1,0:T(8,128)} fusion(f32[128,128,128]{2,1,0:T(8,128)} %gather_fusion, pred[128]{0:T(512)(128)(4,1)S(1)} %broadcast_in_dim.136), kind=kLoop, calls=%fused_computation.13 | loop fusion | flops 2097152 | bytes 16777344 | tf_op jit(solution)/shard_map/select_n | solution.py:46
  29.3 11.9 %all-to-all-start = ((f32[128,1,128,128]{3,2,1,0:T(8,128)}), f32[128,1,128,128]{3,2,1,0:T(8,128)}, u32[]{:S(2)}, u32[]{:S(2)}) async-start(f32[128,1,128,128]{3,2,1,0:T(8,128)} %fusion), calls=%async_computation | async-start | bytes 16777216 | tf_op jit(solution)/shard_map/all_to_all | solution.py:49
  48.7 93.1 %all-to-all-done = f32[128,1,128,128]{3,2,1,0:T(8,128)} async-done(((f32[128,1,128,128]{3,2,1,0:T(8,128)}), f32[128,1,128,128]{3,2,1,0:T(8,128)}, u32[]{:S(2)}, u32[]{:S(2)}) %all-to-all-start) | async-done | bytes 8388640 | tf_op jit(solution)/shard_map/all_to_all | solution.py:49
  141.8 61.6 %gather_fusion.1 = f32[6400,128]{1,0:T(8,128)} fusion(f32[128,128,128]{2,1,0:T(8,128)} %bitcast.8, s32[6400]{0:T(1024)S(1)} %reshape.351), kind=kCustom, calls=%fused_computation.5 | custom fusion | bytes 6604800 | tf_op jit(solution)/shard_map/gather | solution.py:69
  203.4 4.9 %reshape.354 = f32[10,128,5,128]{3,2,1,0:T(8,128)} reshape(f32[6400,128]{1,0:T(8,128)} %gather_fusion.1) | data formatting | bytes 6553600 | tf_op jit(solution)/shard_map/gather | solution.py:69
  208.3 61.7 %gather_fusion.2 = f32[6400,128]{1,0:T(8,128)} fusion(f32[128,128,128]{2,1,0:T(8,128)} %bitcast.8, s32[6400]{0:T(1024)S(1)} %reshape.357), kind=kCustom, calls=%fused_computation.6 | custom fusion | bytes 6604800 | tf_op jit(solution)/shard_map/gather | solution.py:69
  270.0 4.9 %reshape.360 = f32[10,128,5,128]{3,2,1,0:T(8,128)} reshape(f32[6400,128]{1,0:T(8,128)} %gather_fusion.2) | data formatting | bytes 6553600 | tf_op jit(solution)/shard_map/gather | solution.py:69
  274.9 5.5 %select_add_fusion = f32[10,128,5,128]{3,2,1,0:T(8,128)S(1)} fusion(f32[10,128,5,128]{3,2,1,0:T(8,128)} %reshape.360, f32[10,128,5,128]{3,2,1,0:T(8,128)} %reshape.354, pred[10,128,5]{2,1,0:T(8,128)(4,1)S(1)} %copy.15, pred[10,128,5]{2,1,0:T(8,128)(4,1)S(1)} %copy.11), kind=kLoop, calls=%fused_computation.14 | loop fusion | flops 2457600 | bytes 9843200 | tf_op jit(solution)/shard_map/add | solution.py:72
  285.7 4.5 %collective-permute-start.10 = (f32[80,512]{1,0:T(8,128)S(1)}, f32[80,512]{1,0:T(8,128)S(1)}, u32[]{:S(2)}, u32[]{:S(2)}) collective-permute-start(f32[80,512]{1,0:T(8,128)S(1)} %get-tuple-element.24), channel_id=1, source_target_pairs={{0,11},{16,27},{32,43},{48,59},{64,75},{80,91},{96,107},{112,123}} | collective-permute-start | bytes 491528 | tf_op jit(solution)/shard_map/ppermute | solution.py:84
  304.9 2.1 collective-permute-start.6
  315.0 3.5 collective-permute-done.8
  318.5 3.5 collective-permute-done.9
  322.0 3.1 fusion.16
  327.3 6.9 %collective-permute-done.15 = f32[80,512]{1,0:T(8,128)S(1)} collective-permute-done((f32[80,512]{1,0:T(8,128)}, f32[80,512]{1,0:T(8,128)S(1)}, u32[]{:S(2)}, u32[]{:S(2)}) %collective-permute-start.15) | collective-permute-done | bytes 163872 | tf_op jit(solution)/shard_map/ppermute | solution.py:100
  334.2 7.3 %collective-permute-start.16 = (f32[80,512]{1,0:T(8,128)S(1)}, f32[80,512]{1,0:T(8,128)S(1)}, u32[]{:S(2)}, u32[]{:S(2)}) collective-permute-start(f32[80,512]{1,0:T(8,128)S(1)} %collective-permute-done.15), channel_id=1, source_target_pairs={{0,16},{16,32},{32,48},{48,64},{64,80},{80,96},{96,112},{112,0},{1... | collective-permute-start | bytes 491528 | tf_op jit(solution)/shard_map/ppermute | solution.py:104
  342.5 2.2 collective-permute-start.19
  346.0 2.4 collective-permute-done.17
  348.5 3.5 collective-permute-done.18
  352.0 4.7 %collective-permute-done.19 = f32[80,512]{1,0:T(8,128)S(1)} collective-permute-done((f32[80,512]{1,0:T(8,128)S(1)}, f32[80,512]{1,0:T(8,128)S(1)}, u32[]{:S(2)}, u32[]{:S(2)}) %collective-permute-start.19) | collective-permute-done | bytes 163872 | tf_op jit(solution)/shard_map/ppermute | solution.py:104
  361.2 11.0 %all-gather.2.cloned.1.call-done = f32[1280,512]{1,0:T(8,128)} async-done(((f32[80,512]{1,0:T(8,128)}), f32[1280,512]{1,0:T(8,128)}) %all-gather.2.cloned.1.call-update) | async-done | bytes 2621456 | tf_op jit(solution)/shard_map/all_gather | solution.py:93
  372.2 9.8 %convolution_subtract_fusion = f32[1280,640]{1,0:T(8,128)} fusion(f32[1280,640]{1,0:T(8,128)} %copy-done.1, f32[1280,512]{1,0:T(8,128)} %all-gather.2.cloned.1.call-done, f32[640,512]{1,0:T(8,128)S(1)} %bitcast_select_fusion.1), kind=kOutput, calls=%fused_computation.15 | convolution fusion | flops 5033984000 | bytes 10485760 | tf_op jit(solution)/shard_map/dot_general | solution.py:107
  (113 shorter events, 47.8 us)
Async XLA Ops:
  29.3 112.5 %all-to-all-start = ((f32[128,1,128,128]{3,2,1,0:T(8,128)}), f32[128,1,128,128]{3,2,1,0:T(8,128)}, u32[]{:S(2)}, u32[]{:S(2)}) async-start(f32[128,1,128,128]{3,2,1,0:T(8,128)} %fusion), calls=%async_computation | async-start | bytes 16777216 | tf_op jit(solution)/shard_map/all_to_all | solution.py:49
  41.2 331.0 %all-gather.2.cloned.1.call-start = ((), (), s32[]{:S(2)}) async-start(), calls=%async_computation.1 | async-start | bytes 2785280 | tf_op jit(solution)/shard_map/all_gather | solution.py:93
  283.1 9.8 %collective-permute-start = (f32[80,512]{1,0:T(8,128)S(1)}, f32[80,512]{1,0:T(8,128)S(1)}, u32[]{:S(2)}, u32[]{:S(2)}) collective-permute-start(f32[80,512]{1,0:T(8,128)S(1)} %get-tuple-element.19), channel_id=1, source_target_pairs={{0,1},{16,17},{32,33},{48,49},{64,65},{80,81},{96,97},{112,113}} | collective-permute-start | bytes 491528 | tf_op jit(solution)/shard_map/ppermute | solution.py:84
  284.4 9.8 %collective-permute-start.1 = (f32[80,512]{1,0:T(8,128)S(1)}, f32[80,512]{1,0:T(8,128)S(1)}, u32[]{:S(2)}, u32[]{:S(2)}) collective-permute-start(f32[80,512]{1,0:T(8,128)S(1)} %get-tuple-element.33), channel_id=1, source_target_pairs={{0,2},{16,18},{32,34},{48,50},{64,66},{80,82},{96,98},{112,114}} | collective-permute-start | bytes 491528 | tf_op jit(solution)/shard_map/ppermute | solution.py:84
  285.7 9.8 %collective-permute-start.10 = (f32[80,512]{1,0:T(8,128)S(1)}, f32[80,512]{1,0:T(8,128)S(1)}, u32[]{:S(2)}, u32[]{:S(2)}) collective-permute-start(f32[80,512]{1,0:T(8,128)S(1)} %get-tuple-element.24), channel_id=1, source_target_pairs={{0,11},{16,27},{32,43},{48,59},{64,75},{80,91},{96,107},{112,123}} | collective-permute-start | bytes 491528 | tf_op jit(solution)/shard_map/ppermute | solution.py:84
  291.6 6.6 %collective-permute-start.12 = (f32[80,512]{1,0:T(8,128)S(1)}, f32[80,512]{1,0:T(8,128)S(1)}, u32[]{:S(2)}, u32[]{:S(2)}) collective-permute-start(f32[80,512]{1,0:T(8,128)S(1)} %get-tuple-element.22), channel_id=1, source_target_pairs={{0,13},{16,29},{32,45},{48,61},{64,77},{80,93},{96,109},{112,125}} | collective-permute-start | bytes 491528 | tf_op jit(solution)/shard_map/ppermute | solution.py:84
  292.9 8.5 %collective-permute-start.13 = (f32[80,512]{1,0:T(8,128)S(1)}, f32[80,512]{1,0:T(8,128)S(1)}, u32[]{:S(2)}, u32[]{:S(2)}) collective-permute-start(f32[80,512]{1,0:T(8,128)S(1)} %get-tuple-element.21), channel_id=1, source_target_pairs={{0,14},{16,30},{32,46},{48,62},{64,78},{80,94},{96,110},{112,126}} | collective-permute-start | bytes 491528 | tf_op jit(solution)/shard_map/ppermute | solution.py:84
  294.2 10.7 %collective-permute-start.14 = (f32[80,512]{1,0:T(8,128)S(1)}, f32[80,512]{1,0:T(8,128)S(1)}, u32[]{:S(2)}, u32[]{:S(2)}) collective-permute-start(f32[80,512]{1,0:T(8,128)S(1)} %get-tuple-element.20), channel_id=1, source_target_pairs={{0,15},{16,31},{32,47},{48,63},{64,79},{80,95},{96,111},{112,127}} | collective-permute-start | bytes 491528 | tf_op jit(solution)/shard_map/ppermute | solution.py:84
  295.6 11.5 %collective-permute-start.2 = (f32[80,512]{1,0:T(8,128)S(1)}, f32[80,512]{1,0:T(8,128)S(1)}, u32[]{:S(2)}, u32[]{:S(2)}) collective-permute-start(f32[80,512]{1,0:T(8,128)S(1)} %get-tuple-element.32), channel_id=1, source_target_pairs={{0,3},{16,19},{32,35},{48,51},{64,67},{80,83},{96,99},{112,115}} | collective-permute-start | bytes 491528 | tf_op jit(solution)/shard_map/ppermute | solution.py:84
  296.9 12.1 %collective-permute-start.3 = (f32[80,512]{1,0:T(8,128)S(1)}, f32[80,512]{1,0:T(8,128)S(1)}, u32[]{:S(2)}, u32[]{:S(2)}) collective-permute-start(f32[80,512]{1,0:T(8,128)S(1)} %get-tuple-element.31), channel_id=1, source_target_pairs={{0,4},{16,20},{32,36},{48,52},{64,68},{80,84},{96,100},{112,116}} | collective-permute-start | bytes 491528 | tf_op jit(solution)/shard_map/ppermute | solution.py:84
  298.2 12.8 %collective-permute-start.4 = (f32[80,512]{1,0:T(8,128)S(1)}, f32[80,512]{1,0:T(8,128)S(1)}, u32[]{:S(2)}, u32[]{:S(2)}) collective-permute-start(f32[80,512]{1,0:T(8,128)S(1)} %get-tuple-element.30), channel_id=1, source_target_pairs={{0,5},{16,21},{32,37},{48,53},{64,69},{80,85},{96,101},{112,117}} | collective-permute-start | bytes 491528 | tf_op jit(solution)/shard_map/ppermute | solution.py:84
  301.4 11.5 %collective-permute-start.5 = (f32[80,512]{1,0:T(8,128)S(1)}, f32[80,512]{1,0:T(8,128)}, u32[]{:S(2)}, u32[]{:S(2)}) collective-permute-start(f32[80,512]{1,0:T(8,128)S(1)} %get-tuple-element.29), channel_id=1, source_target_pairs={{0,6},{16,22},{32,38},{48,54},{64,70},{80,86},{96,102},{112,118}} | collective-permute-start | bytes 491528 | tf_op jit(solution)/shard_map/ppermute | solution.py:84
  304.9 8.0 %collective-permute-start.6 = (f32[80,512]{1,0:T(8,128)S(1)}, f32[80,512]{1,0:T(8,128)}, u32[]{:S(2)}, u32[]{:S(2)}) collective-permute-start(f32[80,512]{1,0:T(8,128)S(1)} %get-tuple-element.28), channel_id=1, source_target_pairs={{0,7},{16,23},{32,39},{48,55},{64,71},{80,87},{96,103},{112,119}} | collective-permute-start | bytes 491528 | tf_op jit(solution)/shard_map/ppermute | solution.py:84
  307.0 8.0 %collective-permute-start.7 = (f32[80,512]{1,0:T(8,128)S(1)}, f32[80,512]{1,0:T(8,128)}, u32[]{:S(2)}, u32[]{:S(2)}) collective-permute-start(f32[80,512]{1,0:T(8,128)S(1)} %get-tuple-element.27), channel_id=1, source_target_pairs={{0,8},{16,24},{32,40},{48,56},{64,72},{80,88},{96,104},{112,120}} | collective-permute-start | bytes 491528 | tf_op jit(solution)/shard_map/ppermute | solution.py:84
  309.0 9.5 %collective-permute-start.8 = (f32[80,512]{1,0:T(8,128)S(1)}, f32[80,512]{1,0:T(8,128)}, u32[]{:S(2)}, u32[]{:S(2)}) collective-permute-start(f32[80,512]{1,0:T(8,128)S(1)} %get-tuple-element.26), channel_id=1, source_target_pairs={{0,9},{16,25},{32,41},{48,57},{64,73},{80,89},{96,105},{112,121}} | collective-permute-start | bytes 491528 | tf_op jit(solution)/shard_map/ppermute | solution.py:84
  311.0 11.1 %collective-permute-start.9 = (f32[80,512]{1,0:T(8,128)S(1)}, f32[80,512]{1,0:T(8,128)}, u32[]{:S(2)}, u32[]{:S(2)}) collective-permute-start(f32[80,512]{1,0:T(8,128)S(1)} %get-tuple-element.25), channel_id=1, source_target_pairs={{0,10},{16,26},{32,42},{48,58},{64,74},{80,90},{96,106},{112,122}} | collective-permute-start | bytes 491528 | tf_op jit(solution)/shard_map/ppermute | solution.py:84
  325.2 9.0 %collective-permute-start.15 = (f32[80,512]{1,0:T(8,128)}, f32[80,512]{1,0:T(8,128)S(1)}, u32[]{:S(2)}, u32[]{:S(2)}) collective-permute-start(f32[80,512]{1,0:T(8,128)} %fusion.16), channel_id=1, source_target_pairs={{0,0},{1,16},{2,32},{3,48},{4,64},{5,80},{6,96},{7,112},{8,1},{9,1... | collective-permute-start | bytes 491528 | tf_op jit(solution)/shard_map/ppermute | solution.py:100
  334.2 10.7 %collective-permute-start.16 = (f32[80,512]{1,0:T(8,128)S(1)}, f32[80,512]{1,0:T(8,128)S(1)}, u32[]{:S(2)}, u32[]{:S(2)}) collective-permute-start(f32[80,512]{1,0:T(8,128)S(1)} %collective-permute-done.15), channel_id=1, source_target_pairs={{0,16},{16,32},{32,48},{48,64},{64,80},{80,96},{96,112},{112,0},{1... | collective-permute-start | bytes 491528 | tf_op jit(solution)/shard_map/ppermute | solution.py:104
  341.5 6.9 %collective-permute-start.17 = (f32[80,512]{1,0:T(8,128)S(1)}, f32[80,512]{1,0:T(8,128)S(1)}, u32[]{:S(2)}, u32[]{:S(2)}) collective-permute-start(f32[80,512]{1,0:T(8,128)S(1)} %collective-permute-done.15), channel_id=1, source_target_pairs={{0,32},{16,48},{32,64},{48,80},{64,96},{80,112},{96,0},{112,16},{1... | collective-permute-start | bytes 491528 | tf_op jit(solution)/shard_map/ppermute | solution.py:104
  341.5 10.5 %collective-permute-start.18 = (f32[80,512]{1,0:T(8,128)S(1)}, f32[80,512]{1,0:T(8,128)S(1)}, u32[]{:S(2)}, u32[]{:S(2)}) collective-permute-start(f32[80,512]{1,0:T(8,128)S(1)} %collective-permute-done.15), channel_id=1, source_target_pairs={{0,48},{16,64},{32,80},{48,96},{64,112},{80,0},{96,16},{112,32},{1... | collective-permute-start | bytes 491528 | tf_op jit(solution)/shard_map/ppermute | solution.py:104
  342.5 14.1 %collective-permute-start.19 = (f32[80,512]{1,0:T(8,128)S(1)}, f32[80,512]{1,0:T(8,128)S(1)}, u32[]{:S(2)}, u32[]{:S(2)}) collective-permute-start(f32[80,512]{1,0:T(8,128)S(1)} %collective-permute-done.15), channel_id=1, source_target_pairs={{0,64},{16,80},{32,96},{48,112},{64,0},{80,16},{96,32},{112,48},{1... | collective-permute-start | bytes 491528 | tf_op jit(solution)/shard_map/ppermute | solution.py:104
  344.8 12.5 %collective-permute-start.20 = (f32[80,512]{1,0:T(8,128)S(1)}, f32[80,512]{1,0:T(8,128)S(1)}, u32[]{:S(2)}, u32[]{:S(2)}) collective-permute-start(f32[80,512]{1,0:T(8,128)S(1)} %collective-permute-done.15), channel_id=1, source_target_pairs={{0,80},{16,96},{32,112},{48,0},{64,16},{80,32},{96,48},{112,64},{1... | collective-permute-start | bytes 491528 | tf_op jit(solution)/shard_map/ppermute | solution.py:104
  344.9 12.3 %collective-permute-start.21 = (f32[80,512]{1,0:T(8,128)S(1)}, f32[80,512]{1,0:T(8,128)S(1)}, u32[]{:S(2)}, u32[]{:S(2)}) collective-permute-start(f32[80,512]{1,0:T(8,128)S(1)} %collective-permute-done.15), channel_id=1, source_target_pairs={{0,96},{16,112},{32,0},{48,16},{64,32},{80,48},{96,64},{112,80},{1... | collective-permute-start | bytes 491528 | tf_op jit(solution)/shard_map/ppermute | solution.py:104
  348.4 9.6 %collective-permute-start.22 = (f32[80,512]{1,0:T(8,128)S(1)}, f32[80,512]{1,0:T(8,128)S(1)}, u32[]{:S(2)}, u32[]{:S(2)}) collective-permute-start(f32[80,512]{1,0:T(8,128)S(1)} %collective-permute-done.15), channel_id=1, source_target_pairs={{0,112},{16,0},{32,16},{48,32},{64,48},{80,64},{96,80},{112,96},{1... | collective-permute-start | bytes 491528 | tf_op jit(solution)/shard_map/ppermute | solution.py:104
  (6 other events, 350.5 us)
Sparse Core Ops, SparseCore 0:
  325.3 46.8 all-gather.1

commit v6 on v5

--- a/solution.py
+++ b/solution.py
@@ -39,19 +39,22 @@
         .at[col_parent // front_cols]
         .set(jnp.arange(col_items, dtype=jnp.int32))
     )
-    fill_l = jnp.where(inv_l >= 0, inv_l, col_items)
-    outgoing = (
+    local_tiles = (
         updates.reshape(row_items, BLK, col_items, BLK)
-        .at[inv_k[:, None], :, fill_l[None, :], :]
-        .get(mode="fill", fill_value=0.0)
-        .reshape(devices_all, 1, BLK, BLK)
+        .transpose(0, 2, 1, 3)
+        .reshape(row_items * col_items, BLK, BLK)
     )
+    slot_tile = jnp.where(
+        (inv_l >= 0)[None, :], inv_k[:, None] * col_items + inv_l[None, :], row_items * col_items
+    )
+    outgoing = jnp.take(
+        local_tiles, slot_tile.reshape(-1), axis=0, mode="fill", fill_value=0.0
+    ).reshape(devices_all, 1, BLK, BLK)
     incoming = lax.all_to_all(
         outgoing, ("row", "col"), split_axis=0, concat_axis=0, tiled=True
     ).reshape(devices_all, BLK, BLK)
     my_rows = row_index * front_rows + jnp.arange(front_rows, dtype=jnp.int32)
     my_cols = col_index * front_cols + jnp.arange(front_cols, dtype=jnp.int32)
-    lanes = jnp.arange(BLK, dtype=jnp.int32)
     front_local = None
     for child_id in range(2):
         inverse = (
@@ -66,11 +69,13 @@
         )[:, None]
         valid = (a >= 0)[:, None] & (b >= 0)[None, :]
         source = jnp.where(valid, source, devices_all)
-        part = incoming.at[source[:, None, :], lanes[None, :, None], :].get(
-            mode="fill", fill_value=0.0
-        )
+        part = jnp.take(incoming, source.reshape(-1), axis=0, mode="fill", fill_value=0.0)
         front_local = part if front_local is None else front_local + part
-    front_local = front_local.reshape(height, col_width)
+    front_local = (
+        front_local.reshape(front_rows, front_cols, BLK, BLK)
+        .transpose(0, 2, 1, 3)
+        .reshape(height, col_width)
+    )
     row_global = row_index * height + jnp.arange(height, dtype=jnp.int32)
     col_global = col_index * col_width + jnp.arange(col_width, dtype=jnp.int32)
     front_local = front_local + jnp.where(

time: 393 us -> 270 us (0.69)
  local copies, waits for them, and re-layouts: 159 us -> 37.3 us
    gather x5 -> x3, local copies, waits for them, and re-layouts: 140 us -> 18.2 us  [the longest x2 11.7 us: on_device(): jnp.take(incoming, source.reshape(-1), axis=0, mode='fill', fill_value=0.0)]
    transpose x0 -> x3, local copies, waits for them, and re-layouts: none -> 4.9 us  [the longest x2 2.97 us: on_device(): local_tiles = updates.reshape(row_items, BLK, col_items, BLK).transpose(0...]
where the time goes in v6:
time: 270 us; the launch traced here: 269 us
  waiting for transfers between devices  138 us (51%)
  starting transfers between devices  51.7 us (19%)
  local copies, waits for them, and re-layouts  37.3 us (14%)
  between operations  14.6 us (5%)
  other arithmetic  14.1 us (5%)
  matrix products  12.9 us (5%)
    all_to_all x1, waiting for transfers between devices, on_device(): lax.all_to_all(outgoing, ('row', 'col'), split_axis=0, concat_axis=0, til...  95.7 us
    ppermute x15, starting transfers between devices, on_device(): lax.ppermute(raw_panel[k * piece_rows:(k + 1) * piece_rows], ('row', 'col...  26 us
    ppermute x15, waiting for transfers between devices, on_device(): lax.ppermute(raw_panel[k * piece_rows:(k + 1) * piece_rows], ('row', 'col...  12.8 us
    ppermute x7, waiting for transfers between devices, on_device(): stack.append(lax.ppermute(moved, 'row', shift))  12 us
    all_to_all x1, starting transfers between devices, on_device(): lax.all_to_all(outgoing, ('row', 'col'), split_axis=0, concat_axis=0, til...  11.9 us
    ppermute x7, starting transfers between devices, on_device(): stack.append(lax.ppermute(moved, 'row', shift))  11.8 us
    gather x2, local copies, waits for them, and re-layouts, on_device(): jnp.take(incoming, source.reshape(-1), axis=0, mode='fill', fill_value=0.0)  11.7 us
    all_gather x1, waiting for transfers between devices, on_device(): factor_panel = lax.all_gather(factor_piece, 'col', axis=0, tiled=True)  11.1 us
  transfers between devices with their start and end apart: 25, of which 14 were waited for; matrix products, arithmetic and copies ran while one was open for 3% of the time, Pallas kernels for 0%

profile of v6, /device:TPU:1, one launch (start us, length us, event | category | flops | bytes accessed | tf_op | source)
XLA Modules:
  0.0 269.0 jit_solution(17393022413816814904)
XLA Ops:
  9.6 3.2 %copy.12 = f32[128,8,8,128]{3,2,1,0:T(8,128)S(1)} copy(f32[128,8,8,128]{3,1,2,0:T(8,128)} %bitcast.75) | data formatting | bytes 8388608
  13.1 2.7 %copy.9 = f32[8,8,128,128]{3,2,1,0:T(8,128)} copy(f32[8,8,128,128]{3,1,2,0:T(8,128)S(1)} %bitcast_bitcast_fusion) | data formatting | bytes 8388608 | tf_op jit(solution)/shard_map/transpose | solution.py:44
  15.8 6.5 %gather_fusion = f32[128,128,128]{2,1,0:T(8,128)} fusion(f32[64,128,128]{2,1,0:T(8,128)} %bitcast.71, s32[1024]{0:T(1024)S(1)} %pad_clamp_fusion.3), kind=kCustom, calls=%fused_computation.6 | custom fusion | bytes 16777728 | tf_op jit(solution)/shard_map/jit(_take)/gather | solution.py:50
  22.3 7.2 %fusion = f32[128,1,128,128]{3,2,1,0:T(8,128)} fusion(f32[128,128,128]{2,1,0:T(8,128)} %gather_fusion, pred[128]{0:T(512)(128)(4,1)S(1)} %compare_and_fusion.5), kind=kLoop, calls=%fused_computation.13 | loop fusion | flops 2097152 | bytes 16777344 | tf_op jit(solution)/shard_map/jit(_take)/select_n | solution.py:50
  29.5 11.9 %all-to-all-start = ((f32[128,1,128,128]{3,2,1,0:T(8,128)}), f32[128,1,128,128]{3,2,1,0:T(8,128)}, u32[]{:S(2)}, u32[]{:S(2)}) async-start(f32[128,1,128,128]{3,2,1,0:T(8,128)} %fusion), calls=%async_computation | async-start | bytes 16777216 | tf_op jit(solution)/shard_map/all_to_all | solution.py:53
  46.3 95.7 %all-to-all-done = f32[128,1,128,128]{3,2,1,0:T(8,128)} async-done(((f32[128,1,128,128]{3,2,1,0:T(8,128)}), f32[128,1,128,128]{3,2,1,0:T(8,128)}, u32[]{:S(2)}, u32[]{:S(2)}) %all-to-all-start) | async-done | bytes 8388640 | tf_op jit(solution)/shard_map/all_to_all | solution.py:53
  142.0 5.8 %gather_fusion.4 = f32[50,128,128]{2,1,0:T(8,128)} fusion(f32[128,128,128]{2,1,0:T(8,128)} %bitcast.11, s32[1024]{0:T(1024)S(1)} %pad_clamp_fusion.2), kind=kCustom, calls=%fused_computation.2.clone | custom fusion | bytes 6553800 | tf_op jit(solution)/shard_map/jit(_take)/gather | solution.py:72
  147.8 5.8 %gather_fusion.7 = f32[50,128,128]{2,1,0:T(8,128)} fusion(f32[128,128,128]{2,1,0:T(8,128)} %bitcast.11, s32[1024]{0:T(1024)S(1)} %pad_clamp_fusion.1), kind=kCustom, calls=%fused_computation.5.clone | custom fusion | bytes 6553800 | tf_op jit(solution)/shard_map/jit(_take)/gather | solution.py:72
  153.7 3.4 %select_add_fusion = f32[50,128,128]{2,1,0:T(8,128)S(1)} fusion(f32[50,128,128]{2,1,0:T(8,128)} %gather_fusion.7, f32[50,128,128]{2,1,0:T(8,128)} %gather_fusion.4, pred[50]{0:T(512)(128)(4,1)S(1)} %get-tuple-element.37, pred[50]{0:T(512)(128)(4,1)S(1)} %get-tuple-element.38), kind=kLoop, calls=%fused_computation.17 | loop fusion | flops 2457600 | bytes 9830500 | tf_op jit(solution)/shard_map/add | solution.py:73
  164.3 4.5 %collective-permute-start.10 = (f32[80,512]{1,0:T(8,128)S(1)}, f32[80,512]{1,0:T(8,128)S(1)}, u32[]{:S(2)}, u32[]{:S(2)}) collective-permute-start(f32[80,512]{1,0:T(8,128)S(1)} %get-tuple-element.21), channel_id=1, source_target_pairs={{0,11},{16,27},{32,43},{48,59},{64,75},{80,91},{96,107},{112,123}} | collective-permute-start | bytes 491528 | tf_op jit(solution)/shard_map/ppermute | solution.py:89
  180.0 2.0 collective-permute-start.5
  189.3 2.0 collective-permute-start.9
  191.3 2.3 collective-permute-done.7
  193.6 3.5 %collective-permute-done.8 = f32[80,512]{1,0:T(8,128)} collective-permute-done((f32[80,512]{1,0:T(8,128)S(1)}, f32[80,512]{1,0:T(8,128)}, u32[]{:S(2)}, u32[]{:S(2)}) %collective-permute-start.8) | collective-permute-done | bytes 163872 | tf_op jit(solution)/shard_map/ppermute | solution.py:89
  197.1 3.5 %collective-permute-done.9 = f32[80,512]{1,0:T(8,128)} collective-permute-done((f32[80,512]{1,0:T(8,128)S(1)}, f32[80,512]{1,0:T(8,128)}, u32[]{:S(2)}, u32[]{:S(2)}) %collective-permute-start.9) | collective-permute-done | bytes 163872 | tf_op jit(solution)/shard_map/ppermute | solution.py:89
  200.6 3.1 %fusion.16 = f32[80,512]{1,0:T(8,128)} fusion(f32[512,512]{1,0:T(8,128)S(1)} %copy-done, f32[80,512]{1,0:T(8,128)S(1)} %collective-permute-done.14, f32[80,512]{1,0:T(8,128)S(1)} %collective-permute-done.13, f32[80,512]{1,0:T(8,128)S(1)} %collective-permute-done.12, f32[80,512]{1,0:T(8,128)S(1)} %collective-permute-done.11, ...), kind=kOutput, calls=%fused_computation.35 | convolution fusion | flops 252313600 | bytes 3833857 | tf_op jit(solution)/shard_map/dot_general | solution.py:92
  205.9 6.8 %collective-permute-done.15 = f32[80,512]{1,0:T(8,128)S(1)} collective-permute-done((f32[80,512]{1,0:T(8,128)}, f32[80,512]{1,0:T(8,128)S(1)}, u32[]{:S(2)}, u32[]{:S(2)}) %collective-permute-start.15) | collective-permute-done | bytes 163872 | tf_op jit(solution)/shard_map/ppermute | solution.py:105
  212.7 7.4 %collective-permute-start.16 = (f32[80,512]{1,0:T(8,128)S(1)}, f32[80,512]{1,0:T(8,128)S(1)}, u32[]{:S(2)}, u32[]{:S(2)}) collective-permute-start(f32[80,512]{1,0:T(8,128)S(1)} %collective-permute-done.15), channel_id=1, source_target_pairs={{0,16},{16,32},{32,48},{48,64},{64,80},{80,96},{96,112},{112,0},{1... | collective-permute-start | bytes 491528 | tf_op jit(solution)/shard_map/ppermute | solution.py:109
  221.1 2.2 collective-permute-start.19
  224.6 2.4 collective-permute-done.17
  227.0 3.5 %collective-permute-done.18 = f32[80,512]{1,0:T(8,128)S(1)} collective-permute-done((f32[80,512]{1,0:T(8,128)S(1)}, f32[80,512]{1,0:T(8,128)S(1)}, u32[]{:S(2)}, u32[]{:S(2)}) %collective-permute-start.18) | collective-permute-done | bytes 163872 | tf_op jit(solution)/shard_map/ppermute | solution.py:109
  230.5 4.7 %collective-permute-done.19 = f32[80,512]{1,0:T(8,128)S(1)} collective-permute-done((f32[80,512]{1,0:T(8,128)S(1)}, f32[80,512]{1,0:T(8,128)S(1)}, u32[]{:S(2)}, u32[]{:S(2)}) %collective-permute-start.19) | collective-permute-done | bytes 163872 | tf_op jit(solution)/shard_map/ppermute | solution.py:109
  239.8 11.1 %all-gather.2.cloned.1.call-done = f32[1280,512]{1,0:T(8,128)} async-done(((f32[80,512]{1,0:T(8,128)}), f32[1280,512]{1,0:T(8,128)}) %all-gather.2.cloned.1.call-update) | async-done | bytes 2621456 | tf_op jit(solution)/shard_map/all_gather | solution.py:98
  250.8 9.8 %convolution_subtract_fusion = f32[1280,640]{1,0:T(8,128)} fusion(f32[1280,640]{1,0:T(8,128)} %copy-done.1, f32[1280,512]{1,0:T(8,128)} %all-gather.2.cloned.1.call-done, f32[640,512]{1,0:T(8,128)S(1)} %bitcast_select_fusion.1), kind=kOutput, calls=%fused_computation.15 | convolution fusion | flops 5033984000 | bytes 10485760 | tf_op jit(solution)/shard_map/dot_general | solution.py:112
  (111 shorter events, 43.4 us)
Async XLA Ops:
  29.5 112.5 %all-to-all-start = ((f32[128,1,128,128]{3,2,1,0:T(8,128)}), f32[128,1,128,128]{3,2,1,0:T(8,128)}, u32[]{:S(2)}, u32[]{:S(2)}) async-start(f32[128,1,128,128]{3,2,1,0:T(8,128)} %fusion), calls=%async_computation | async-start | bytes 16777216 | tf_op jit(solution)/shard_map/all_to_all | solution.py:53
  41.4 209.4 %all-gather.2.cloned.1.call-start = ((), (), s32[]{:S(2)}) async-start(), calls=%async_computation.1 | async-start | bytes 2785280 | tf_op jit(solution)/shard_map/all_gather | solution.py:98
  161.7 9.8 %collective-permute-start = (f32[80,512]{1,0:T(8,128)S(1)}, f32[80,512]{1,0:T(8,128)S(1)}, u32[]{:S(2)}, u32[]{:S(2)}) collective-permute-start(f32[80,512]{1,0:T(8,128)S(1)} %get-tuple-element.16), channel_id=1, source_target_pairs={{0,1},{16,17},{32,33},{48,49},{64,65},{80,81},{96,97},{112,113}} | collective-permute-start | bytes 491528 | tf_op jit(solution)/shard_map/ppermute | solution.py:89
  163.0 9.8 %collective-permute-start.1 = (f32[80,512]{1,0:T(8,128)S(1)}, f32[80,512]{1,0:T(8,128)S(1)}, u32[]{:S(2)}, u32[]{:S(2)}) collective-permute-start(f32[80,512]{1,0:T(8,128)S(1)} %get-tuple-element.30), channel_id=1, source_target_pairs={{0,2},{16,18},{32,34},{48,50},{64,66},{80,82},{96,98},{112,114}} | collective-permute-start | bytes 491528 | tf_op jit(solution)/shard_map/ppermute | solution.py:89
  164.3 9.8 %collective-permute-start.10 = (f32[80,512]{1,0:T(8,128)S(1)}, f32[80,512]{1,0:T(8,128)S(1)}, u32[]{:S(2)}, u32[]{:S(2)}) collective-permute-start(f32[80,512]{1,0:T(8,128)S(1)} %get-tuple-element.21), channel_id=1, source_target_pairs={{0,11},{16,27},{32,43},{48,59},{64,75},{80,91},{96,107},{112,123}} | collective-permute-start | bytes 491528 | tf_op jit(solution)/shard_map/ppermute | solution.py:89
  170.2 6.6 %collective-permute-start.12 = (f32[80,512]{1,0:T(8,128)S(1)}, f32[80,512]{1,0:T(8,128)S(1)}, u32[]{:S(2)}, u32[]{:S(2)}) collective-permute-start(f32[80,512]{1,0:T(8,128)S(1)} %get-tuple-element.19), channel_id=1, source_target_pairs={{0,13},{16,29},{32,45},{48,61},{64,77},{80,93},{96,109},{112,125}} | collective-permute-start | bytes 491528 | tf_op jit(solution)/shard_map/ppermute | solution.py:89
  171.5 8.5 %collective-permute-start.13 = (f32[80,512]{1,0:T(8,128)S(1)}, f32[80,512]{1,0:T(8,128)S(1)}, u32[]{:S(2)}, u32[]{:S(2)}) collective-permute-start(f32[80,512]{1,0:T(8,128)S(1)} %get-tuple-element.18), channel_id=1, source_target_pairs={{0,14},{16,30},{32,46},{48,62},{64,78},{80,94},{96,110},{112,126}} | collective-permute-start | bytes 491528 | tf_op jit(solution)/shard_map/ppermute | solution.py:89
  172.8 10.7 %collective-permute-start.14 = (f32[80,512]{1,0:T(8,128)S(1)}, f32[80,512]{1,0:T(8,128)S(1)}, u32[]{:S(2)}, u32[]{:S(2)}) collective-permute-start(f32[80,512]{1,0:T(8,128)S(1)} %get-tuple-element.17), channel_id=1, source_target_pairs={{0,15},{16,31},{32,47},{48,63},{64,79},{80,95},{96,111},{112,127}} | collective-permute-start | bytes 491528 | tf_op jit(solution)/shard_map/ppermute | solution.py:89
  174.1 11.3 %collective-permute-start.2 = (f32[80,512]{1,0:T(8,128)S(1)}, f32[80,512]{1,0:T(8,128)S(1)}, u32[]{:S(2)}, u32[]{:S(2)}) collective-permute-start(f32[80,512]{1,0:T(8,128)S(1)} %get-tuple-element.29), channel_id=1, source_target_pairs={{0,3},{16,19},{32,35},{48,51},{64,67},{80,83},{96,99},{112,115}} | collective-permute-start | bytes 491528 | tf_op jit(solution)/shard_map/ppermute | solution.py:89
  175.4 12.0 %collective-permute-start.3 = (f32[80,512]{1,0:T(8,128)S(1)}, f32[80,512]{1,0:T(8,128)S(1)}, u32[]{:S(2)}, u32[]{:S(2)}) collective-permute-start(f32[80,512]{1,0:T(8,128)S(1)} %get-tuple-element.28), channel_id=1, source_target_pairs={{0,4},{16,20},{32,36},{48,52},{64,68},{80,84},{96,100},{112,116}} | collective-permute-start | bytes 491528 | tf_op jit(solution)/shard_map/ppermute | solution.py:89
  176.7 12.6 %collective-permute-start.4 = (f32[80,512]{1,0:T(8,128)S(1)}, f32[80,512]{1,0:T(8,128)S(1)}, u32[]{:S(2)}, u32[]{:S(2)}) collective-permute-start(f32[80,512]{1,0:T(8,128)S(1)} %get-tuple-element.27), channel_id=1, source_target_pairs={{0,5},{16,21},{32,37},{48,53},{64,69},{80,85},{96,101},{112,117}} | collective-permute-start | bytes 491528 | tf_op jit(solution)/shard_map/ppermute | solution.py:89
  180.0 11.3 %collective-permute-start.5 = (f32[80,512]{1,0:T(8,128)S(1)}, f32[80,512]{1,0:T(8,128)}, u32[]{:S(2)}, u32[]{:S(2)}) collective-permute-start(f32[80,512]{1,0:T(8,128)S(1)} %get-tuple-element.26), channel_id=1, source_target_pairs={{0,6},{16,22},{32,38},{48,54},{64,70},{80,86},{96,102},{112,118}} | collective-permute-start | bytes 491528 | tf_op jit(solution)/shard_map/ppermute | solution.py:89
  183.5 7.8 %collective-permute-start.6 = (f32[80,512]{1,0:T(8,128)S(1)}, f32[80,512]{1,0:T(8,128)}, u32[]{:S(2)}, u32[]{:S(2)}) collective-permute-start(f32[80,512]{1,0:T(8,128)S(1)} %get-tuple-element.25), channel_id=1, source_target_pairs={{0,7},{16,23},{32,39},{48,55},{64,71},{80,87},{96,103},{112,119}} | collective-permute-start | bytes 491528 | tf_op jit(solution)/shard_map/ppermute | solution.py:89
  185.4 8.1 %collective-permute-start.7 = (f32[80,512]{1,0:T(8,128)S(1)}, f32[80,512]{1,0:T(8,128)}, u32[]{:S(2)}, u32[]{:S(2)}) collective-permute-start(f32[80,512]{1,0:T(8,128)S(1)} %get-tuple-element.24), channel_id=1, source_target_pairs={{0,8},{16,24},{32,40},{48,56},{64,72},{80,88},{96,104},{112,120}} | collective-permute-start | bytes 491528 | tf_op jit(solution)/shard_map/ppermute | solution.py:89
  187.4 9.7 %collective-permute-start.8 = (f32[80,512]{1,0:T(8,128)S(1)}, f32[80,512]{1,0:T(8,128)}, u32[]{:S(2)}, u32[]{:S(2)}) collective-permute-start(f32[80,512]{1,0:T(8,128)S(1)} %get-tuple-element.23), channel_id=1, source_target_pairs={{0,9},{16,25},{32,41},{48,57},{64,73},{80,89},{96,105},{112,121}} | collective-permute-start | bytes 491528 | tf_op jit(solution)/shard_map/ppermute | solution.py:89
  189.3 11.3 %collective-permute-start.9 = (f32[80,512]{1,0:T(8,128)S(1)}, f32[80,512]{1,0:T(8,128)}, u32[]{:S(2)}, u32[]{:S(2)}) collective-permute-start(f32[80,512]{1,0:T(8,128)S(1)} %get-tuple-element.22), channel_id=1, source_target_pairs={{0,10},{16,26},{32,42},{48,58},{64,74},{80,90},{96,106},{112,122}} | collective-permute-start | bytes 491528 | tf_op jit(solution)/shard_map/ppermute | solution.py:89
  203.7 8.9 %collective-permute-start.15 = (f32[80,512]{1,0:T(8,128)}, f32[80,512]{1,0:T(8,128)S(1)}, u32[]{:S(2)}, u32[]{:S(2)}) collective-permute-start(f32[80,512]{1,0:T(8,128)} %fusion.16), channel_id=1, source_target_pairs={{0,0},{1,16},{2,32},{3,48},{4,64},{5,80},{6,96},{7,112},{8,1},{9,1... | collective-permute-start | bytes 491528 | tf_op jit(solution)/shard_map/ppermute | solution.py:105
  212.7 10.8 %collective-permute-start.16 = (f32[80,512]{1,0:T(8,128)S(1)}, f32[80,512]{1,0:T(8,128)S(1)}, u32[]{:S(2)}, u32[]{:S(2)}) collective-permute-start(f32[80,512]{1,0:T(8,128)S(1)} %collective-permute-done.15), channel_id=1, source_target_pairs={{0,16},{16,32},{32,48},{48,64},{64,80},{80,96},{96,112},{112,0},{1... | collective-permute-start | bytes 491528 | tf_op jit(solution)/shard_map/ppermute | solution.py:109
  220.0 6.9 %collective-permute-start.17 = (f32[80,512]{1,0:T(8,128)S(1)}, f32[80,512]{1,0:T(8,128)S(1)}, u32[]{:S(2)}, u32[]{:S(2)}) collective-permute-start(f32[80,512]{1,0:T(8,128)S(1)} %collective-permute-done.15), channel_id=1, source_target_pairs={{0,32},{16,48},{32,64},{48,80},{64,96},{80,112},{96,0},{112,16},{1... | collective-permute-start | bytes 491528 | tf_op jit(solution)/shard_map/ppermute | solution.py:109
  220.1 10.5 %collective-permute-start.18 = (f32[80,512]{1,0:T(8,128)S(1)}, f32[80,512]{1,0:T(8,128)S(1)}, u32[]{:S(2)}, u32[]{:S(2)}) collective-permute-start(f32[80,512]{1,0:T(8,128)S(1)} %collective-permute-done.15), channel_id=1, source_target_pairs={{0,48},{16,64},{32,80},{48,96},{64,112},{80,0},{96,16},{112,32},{1... | collective-permute-start | bytes 491528 | tf_op jit(solution)/shard_map/ppermute | solution.py:109
  221.1 14.1 %collective-permute-start.19 = (f32[80,512]{1,0:T(8,128)S(1)}, f32[80,512]{1,0:T(8,128)S(1)}, u32[]{:S(2)}, u32[]{:S(2)}) collective-permute-start(f32[80,512]{1,0:T(8,128)S(1)} %collective-permute-done.15), channel_id=1, source_target_pairs={{0,64},{16,80},{32,96},{48,112},{64,0},{80,16},{96,32},{112,48},{1... | collective-permute-start | bytes 491528 | tf_op jit(solution)/shard_map/ppermute | solution.py:109
  223.3 12.5 %collective-permute-start.20 = (f32[80,512]{1,0:T(8,128)S(1)}, f32[80,512]{1,0:T(8,128)S(1)}, u32[]{:S(2)}, u32[]{:S(2)}) collective-permute-start(f32[80,512]{1,0:T(8,128)S(1)} %collective-permute-done.15), channel_id=1, source_target_pairs={{0,80},{16,96},{32,112},{48,0},{64,16},{80,32},{96,48},{112,64},{1... | collective-permute-start | bytes 491528 | tf_op jit(solution)/shard_map/ppermute | solution.py:109
  223.5 12.3 %collective-permute-start.21 = (f32[80,512]{1,0:T(8,128)S(1)}, f32[80,512]{1,0:T(8,128)S(1)}, u32[]{:S(2)}, u32[]{:S(2)}) collective-permute-start(f32[80,512]{1,0:T(8,128)S(1)} %collective-permute-done.15), channel_id=1, source_target_pairs={{0,96},{16,112},{32,0},{48,16},{64,32},{80,48},{96,64},{112,80},{1... | collective-permute-start | bytes 491528 | tf_op jit(solution)/shard_map/ppermute | solution.py:109
  227.0 9.6 %collective-permute-start.22 = (f32[80,512]{1,0:T(8,128)S(1)}, f32[80,512]{1,0:T(8,128)S(1)}, u32[]{:S(2)}, u32[]{:S(2)}) collective-permute-start(f32[80,512]{1,0:T(8,128)S(1)} %collective-permute-done.15), channel_id=1, source_target_pairs={{0,112},{16,0},{32,16},{48,32},{64,48},{80,64},{96,80},{112,96},{1... | collective-permute-start | bytes 491528 | tf_op jit(solution)/shard_map/ppermute | solution.py:109
  (6 other events, 225.5 us)
Sparse Core Ops, SparseCore 0:
  203.9 46.9 all-gather.1

commit v7 on v6

--- a/solution.py
+++ b/solution.py
@@ -47,15 +47,16 @@
     slot_tile = jnp.where(
         (inv_l >= 0)[None, :], inv_k[:, None] * col_items + inv_l[None, :], row_items * col_items
     )
-    outgoing = jnp.take(
-        local_tiles, slot_tile.reshape(-1), axis=0, mode="fill", fill_value=0.0
-    ).reshape(devices_all, 1, BLK, BLK)
+    local_tiles = jnp.concatenate([local_tiles, jnp.zeros((1, BLK, BLK), jnp.float32)], axis=0)
+    outgoing = jnp.take(local_tiles, slot_tile.reshape(-1), axis=0, mode="clip").reshape(
+        devices_all, 1, BLK, BLK
+    )
     incoming = lax.all_to_all(
         outgoing, ("row", "col"), split_axis=0, concat_axis=0, tiled=True
     ).reshape(devices_all, BLK, BLK)
     my_rows = row_index * front_rows + jnp.arange(front_rows, dtype=jnp.int32)
     my_cols = col_index * front_cols + jnp.arange(front_cols, dtype=jnp.int32)
-    front_local = None
+    sources = []
     for child_id in range(2):
         inverse = (
             jnp.full((front_blocks,), -1, jnp.int32)
@@ -68,21 +69,28 @@
             child_id * half_cols + jnp.maximum(a, 0) // row_items
         )[:, None]
         valid = (a >= 0)[:, None] & (b >= 0)[None, :]
-        source = jnp.where(valid, source, devices_all)
-        part = jnp.take(incoming, source.reshape(-1), axis=0, mode="fill", fill_value=0.0)
-        front_local = part if front_local is None else front_local + part
-    front_local = (
-        front_local.reshape(front_rows, front_cols, BLK, BLK)
-        .transpose(0, 2, 1, 3)
-        .reshape(height, col_width)
-    )
+        sources.append(jnp.where(valid, source, devices_all))
+
+    def assemble(width):
+        total = None
+        for source in sources:
+            part = jnp.take(
+                incoming, source[:, :width].reshape(-1), axis=0, mode="fill", fill_value=0.0
+            )
+            total = part if total is None else total + part
+        return (
+            total.reshape(front_rows, width, BLK, BLK)
+            .transpose(0, 2, 1, 3)
+            .reshape(height, width * BLK)
+        )
+
     row_global = row_index * height + jnp.arange(height, dtype=jnp.int32)
     col_global = col_index * col_width + jnp.arange(col_width, dtype=jnp.int32)
-    front_local = front_local + jnp.where(
-        row_global[:, None] == col_global[None, :], own_diag[:, None], 0.0
-    )
+    diag = jnp.where(row_global[:, None] == col_global[None, :], own_diag[:, None], 0.0)
+    raw_panel = assemble(PANEL // BLK) + diag[:, :PANEL]
+    front_local = assemble(front_cols) + diag
     piece_rows = height // col_count
-    raw_panel = front_local[:, :PANEL]
+    piece_rows = height // col_count
     piece = jnp.where(col_index == 0, raw_panel[:piece_rows], 0.0)
     for k in range(1, col_count):
         pairs = [(r * col_count, r * col_count + k) for r in range(row_count)]

time: 270 us -> 268 us (level)
  waiting for transfers between devices: 138 us -> 116 us
  local copies, waits for them, and re-layouts: 37.3 us -> 53.2 us
  starting transfers between devices: 51.7 us -> 55.7 us
    gather x3 -> x5, local copies, waits for them, and re-layouts: 18.2 us -> 29.5 us  [the longest x4 22.9 us: assemble(): jnp.take(incoming, source[:, :width].reshape(-1), axis=0, mode='fill', fi...]
    all_gather x1, waiting for transfers between devices: 11.1 us -> 0.02 us  [on_device(): factor_panel = lax.all_gather(factor_piece, 'col', axis=0, tiled=True)]
    ppermute x1, waiting for transfers between devices: 6.81 us -> 0.59 us  [on_device(): moved = lax.ppermute(factor_piece, ('row', 'col'), pairs)]
    select_n x5, other arithmetic: 7.39 us -> 2.28 us  [the longest x1 2.12 us: on_device(): jnp.where(row_global[:, None] == col_global[None, :], own_diag[:, None],...]
    transpose x1 -> x2, local copies, waits for them, and re-layouts: 1.93 us -> 5.97 us  [assemble(): return total.reshape(front_rows, width, BLK, BLK).transpose(0, 2, 1, 3).r...]
    ppermute x7, starting transfers between devices: 11.8 us -> 15.6 us  [on_device(): stack.append(lax.ppermute(moved, 'row', shift))]
    add x2 -> x3, other arithmetic: 4.1 us -> 6.73 us  [the longest x2 6.3 us: assemble(): total = part if total is None else total + part]
    unnamed x19 -> x23, local copies, waits for them, and re-layouts: 6.5 us -> 6.51 us
  transfers between devices with their start and end apart: 25 -> 25, of which waited for: 14 -> 12; matrix products, arithmetic and copies ran while one was open for 3% -> 11% of each run, Pallas kernels for 0% -> 0%
where the time goes in v7:
time: 268 us; the launch traced here: 265 us
  waiting for transfers between devices  116 us (43%)
  starting transfers between devices  55.7 us (21%)
  local copies, waits for them, and re-layouts  53.2 us (20%)
  between operations  14.6 us (5%)
  matrix products  14.1 us (5%)
  other arithmetic  11.6 us (4%)
    all_to_all x1, waiting for transfers between devices, on_device(): lax.all_to_all(outgoing, ('row', 'col'), split_axis=0, concat_axis=0, til...  93.6 us
    ppermute x15, starting transfers between devices, on_device(): lax.ppermute(raw_panel[k * piece_rows:(k + 1) * piece_rows], ('row', 'col...  26 us
    gather x4, local copies, waits for them, and re-layouts, assemble(): jnp.take(incoming, source[:, :width].reshape(-1), axis=0, mode='fill', fi...  22.9 us
    ppermute x7, starting transfers between devices, on_device(): stack.append(lax.ppermute(moved, 'row', shift))  15.6 us
    ppermute x15, waiting for transfers between devices, on_device(): lax.ppermute(raw_panel[k * piece_rows:(k + 1) * piece_rows], ('row', 'col...  12.8 us
    all_to_all x1, starting transfers between devices, on_device(): lax.all_to_all(outgoing, ('row', 'col'), split_axis=0, concat_axis=0, til...  11.9 us
    dot_general x1, matrix products, on_device(): lax.dot_general(factor_panel, across, (((1,), (1,)), ((), ())), precision...  10.9 us
    ppermute x7, waiting for transfers between devices, on_device(): stack.append(lax.ppermute(moved, 'row', shift))  9.26 us
  transfers between devices with their start and end apart: 25, of which 12 were waited for; matrix products, arithmetic and copies ran while one was open for 11% of the time, Pallas kernels for 0%

profile of v7, /device:TPU:1, one launch (start us, length us, event | category | flops | bytes accessed | tf_op | source)
XLA Modules:
  0.0 265.5 jit_solution(8856378728418606486)
XLA Ops:
  9.5 3.2 %copy.15 = f32[128,8,8,128]{3,2,1,0:T(8,128)S(1)} copy(f32[128,8,8,128]{3,1,2,0:T(8,128)} %bitcast.84) | data formatting | bytes 8388608
  13.7 2.3 concatenate.3
  16.0 6.5 %gather_fusion = f32[128,128,128]{2,1,0:T(8,128)} fusion(f32[65,128,128]{2,1,0:T(8,128)} %concatenate.3, s32[1024]{0:T(1024)S(1)} %pad_clamp_fusion.5), kind=kCustom, calls=%fused_computation.8 | custom fusion | bytes 16777728 | tf_op jit(solution)/shard_map/jit(_take)/gather | solution.py:51
  22.6 11.9 %all-to-all-start = ((f32[128,1,128,128]{3,2,1,0:T(8,128)}), f32[128,1,128,128]{3,2,1,0:T(8,128)}, u32[]{:S(2)}, u32[]{:S(2)}) async-start(f32[128,1,128,128]{3,2,1,0:T(8,128)} %bitcast.77), calls=%async_computation | async-start | bytes 16777216 | tf_op jit(solution)/shard_map/all_to_all | solution.py:54
  39.4 2.1 compare_select_fusion
  41.5 93.6 %all-to-all-done = f32[128,1,128,128]{3,2,1,0:T(8,128)} async-done(((f32[128,1,128,128]{3,2,1,0:T(8,128)}), f32[128,1,128,128]{3,2,1,0:T(8,128)}, u32[]{:S(2)}, u32[]{:S(2)}) %all-to-all-start) | async-done | bytes 8388640 | tf_op jit(solution)/shard_map/all_to_all | solution.py:54
  135.1 5.6 %gather_fusion.4 = f32[40,128,128]{2,1,0:T(8,128)} fusion(f32[128,128,128]{2,1,0:T(8,128)} %bitcast.10, s32[1024]{0:T(1024)S(1)} %pad_clamp_fusion.4), kind=kCustom, calls=%fused_computation.2.clone | custom fusion | bytes 5243040 | tf_op jit(solution)/shard_map/jit(_take)/gather | solution.py:77
  140.8 5.6 %gather_fusion.7 = f32[40,128,128]{2,1,0:T(8,128)} fusion(f32[128,128,128]{2,1,0:T(8,128)} %bitcast.10, s32[1024]{0:T(1024)S(1)} %pad_clamp_fusion.3), kind=kCustom, calls=%fused_computation.6.clone | custom fusion | bytes 5243040 | tf_op jit(solution)/shard_map/jit(_take)/gather | solution.py:77
  146.3 2.9 %select_add_fusion.1 = f32[40,128,128]{2,1,0:T(8,128)S(1)} fusion(f32[40,128,128]{2,1,0:T(8,128)} %gather_fusion.7, f32[40,128,128]{2,1,0:T(8,128)} %gather_fusion.4, pred[40]{0:T(512)(128)(4,1)S(1)} %get-tuple-element.42, pred[40]{0:T(512)(128)(4,1)S(1)} %get-tuple-element.43), kind=kLoop, calls=%fused_computation.20 | loop fusion | flops 1966080 | bytes 7864400 | tf_op jit(solution)/shard_map/add | solution.py:80
  156.0 4.5 %collective-permute-start.10 = (f32[80,512]{1,0:T(8,128)S(1)}, f32[80,512]{1,0:T(8,128)S(1)}, u32[]{:S(2)}, u32[]{:S(2)}) collective-permute-start(f32[80,512]{1,0:T(8,128)S(1)} %get-tuple-element.22), channel_id=1, source_target_pairs={{0,11},{16,27},{32,43},{48,59},{64,75},{80,91},{96,107},{112,123}} | collective-permute-start | bytes 491528 | tf_op jit(solution)/shard_map/ppermute | solution.py:97
  183.0 2.3 collective-permute-done.7
  185.3 3.5 %collective-permute-done.8 = f32[80,512]{1,0:T(8,128)} collective-permute-done((f32[80,512]{1,0:T(8,128)S(1)}, f32[80,512]{1,0:T(8,128)}, u32[]{:S(2)}, u32[]{:S(2)}) %collective-permute-start.8) | collective-permute-done | bytes 163872 | tf_op jit(solution)/shard_map/ppermute | solution.py:97
  188.8 3.5 %collective-permute-done.9 = f32[80,512]{1,0:T(8,128)} collective-permute-done((f32[80,512]{1,0:T(8,128)S(1)}, f32[80,512]{1,0:T(8,128)}, u32[]{:S(2)}, u32[]{:S(2)}) %collective-permute-start.9) | collective-permute-done | bytes 163872 | tf_op jit(solution)/shard_map/ppermute | solution.py:97
  192.3 3.1 %fusion.15 = f32[80,512]{1,0:T(8,128)} fusion(f32[512,512]{1,0:T(8,128)S(1)} %copy-done, f32[80,512]{1,0:T(8,128)S(1)} %collective-permute-done.14, f32[80,512]{1,0:T(8,128)S(1)} %collective-permute-done.13, f32[80,512]{1,0:T(8,128)S(1)} %collective-permute-done.12, f32[80,512]{1,0:T(8,128)S(1)} %collective-permute-done.11, ...), kind=kOutput, calls=%fused_computation.38 | convolution fusion | flops 252313600 | bytes 3833857 | tf_op jit(solution)/shard_map/dot_general | solution.py:100
  195.9 5.8 %gather_fusion.8 = f32[50,128,128]{2,1,0:T(8,128)} fusion(f32[128,128,128]{2,1,0:T(8,128)} %bitcast.10, s32[1024]{0:T(1024)S(1)} %pad_clamp_fusion.2), kind=kCustom, calls=%fused_computation.3.clone | custom fusion | bytes 6553800 | tf_op jit(solution)/shard_map/jit(_take)/gather | solution.py:77
  201.7 5.9 %gather_fusion.9 = f32[50,128,128]{2,1,0:T(8,128)} fusion(f32[128,128,128]{2,1,0:T(8,128)} %bitcast.10, s32[1024]{0:T(1024)S(1)} %pad_clamp_fusion.1), kind=kCustom, calls=%fused_computation.7.clone | custom fusion | bytes 6553800 | tf_op jit(solution)/shard_map/jit(_take)/gather | solution.py:77
  209.7 3.4 %select_add_fusion = f32[50,128,128]{2,1,0:T(8,128)S(1)} fusion(f32[50,128,128]{2,1,0:T(8,128)} %gather_fusion.9, f32[50,128,128]{2,1,0:T(8,128)} %gather_fusion.8, pred[50]{0:T(512)(128)(4,1)S(1)} %get-tuple-element.40, pred[50]{0:T(512)(128)(4,1)S(1)} %get-tuple-element.41), kind=kLoop, calls=%fused_computation.17 | loop fusion | flops 2457600 | bytes 9830500 | tf_op jit(solution)/shard_map/add | solution.py:80
  213.1 4.3 %copy.14 = f32[10,128,5,128]{3,2,1,0:T(8,128)} copy(f32[10,128,5,128]{3,1,2,0:T(8,128)S(1)} %bitcast.81) | data formatting | bytes 6553600 | tf_op jit(solution)/shard_map/transpose | solution.py:83
  218.0 7.1 %collective-permute-start.16 = (f32[80,512]{1,0:T(8,128)S(1)}, f32[80,512]{1,0:T(8,128)S(1)}, u32[]{:S(2)}, u32[]{:S(2)}) collective-permute-start(f32[80,512]{1,0:T(8,128)S(1)} %collective-permute-done.15), channel_id=1, source_target_pairs={{0,16},{16,32},{32,48},{48,64},{64,80},{80,96},{96,112},{112,0},{1... | collective-permute-start | bytes 491528 | tf_op jit(solution)/shard_map/ppermute | solution.py:117
  225.0 3.1 %collective-permute-start.18 = (f32[80,512]{1,0:T(8,128)S(1)}, f32[80,512]{1,0:T(8,128)S(1)}, u32[]{:S(2)}, u32[]{:S(2)}) collective-permute-start(f32[80,512]{1,0:T(8,128)S(1)} %collective-permute-done.15), channel_id=1, source_target_pairs={{0,48},{16,64},{32,80},{48,96},{64,112},{80,0},{96,16},{112,32},{1... | collective-permute-start | bytes 491528 | tf_op jit(solution)/shard_map/ppermute | solution.py:117
  228.3 2.5 collective-permute-start.20
  232.0 2.3 collective-permute-start.22
  235.5 6.6 %collective-permute-done.19 = f32[80,512]{1,0:T(8,128)S(1)} collective-permute-done((f32[80,512]{1,0:T(8,128)S(1)}, f32[80,512]{1,0:T(8,128)S(1)}, u32[]{:S(2)}, u32[]{:S(2)}) %collective-permute-start.19) | collective-permute-done | bytes 163872 | tf_op jit(solution)/shard_map/ppermute | solution.py:117
  246.2 10.9 %convolution_subtract_fusion = f32[1280,640]{1,0:T(8,128)} fusion(f32[1280,512]{1,0:T(8,128)} %all-gather.2.cloned.1.call-done, f32[640,512]{1,0:T(8,128)S(1)} %bitcast_select_fusion, f32[160,8,5,128]{3,2,1,0:T(8,128)} %bitcast.80, f32[1280]{0:T(1024)S(1)} %copy-done.5, s32[640]{0:T(1024)S(1)} %iota_add_fusion.1, s32[1280]{0:T(1024)S(1)} %iota_add_fusion), kind=kOutput, calls=%fused_computation.15 | convolution fusion | flops 5036441600 | bytes 10498560 | tf_op jit(solution)/shard_map/dot_general | solution.py:120
  (123 shorter events, 48.2 us)
Async XLA Ops:
  22.6 112.5 %all-to-all-start = ((f32[128,1,128,128]{3,2,1,0:T(8,128)}), f32[128,1,128,128]{3,2,1,0:T(8,128)}, u32[]{:S(2)}, u32[]{:S(2)}) async-start(f32[128,1,128,128]{3,2,1,0:T(8,128)} %bitcast.77), calls=%async_computation | async-start | bytes 16777216 | tf_op jit(solution)/shard_map/all_to_all | solution.py:54
  34.5 211.7 %all-gather.2.cloned.1.call-start = ((), (), s32[]{:S(2)}) async-start(), calls=%async_computation.1 | async-start | bytes 2785280 | tf_op jit(solution)/shard_map/all_gather | solution.py:106
  153.4 9.8 %collective-permute-start = (f32[80,512]{1,0:T(8,128)S(1)}, f32[80,512]{1,0:T(8,128)S(1)}, u32[]{:S(2)}, u32[]{:S(2)}) collective-permute-start(f32[80,512]{1,0:T(8,128)S(1)} %get-tuple-element.17), channel_id=1, source_target_pairs={{0,1},{16,17},{32,33},{48,49},{64,65},{80,81},{96,97},{112,113}} | collective-permute-start | bytes 491528 | tf_op jit(solution)/shard_map/ppermute | solution.py:97
  154.7 9.8 %collective-permute-start.1 = (f32[80,512]{1,0:T(8,128)S(1)}, f32[80,512]{1,0:T(8,128)S(1)}, u32[]{:S(2)}, u32[]{:S(2)}) collective-permute-start(f32[80,512]{1,0:T(8,128)S(1)} %get-tuple-element.31), channel_id=1, source_target_pairs={{0,2},{16,18},{32,34},{48,50},{64,66},{80,82},{96,98},{112,114}} | collective-permute-start | bytes 491528 | tf_op jit(solution)/shard_map/ppermute | solution.py:97
  156.0 9.8 %collective-permute-start.10 = (f32[80,512]{1,0:T(8,128)S(1)}, f32[80,512]{1,0:T(8,128)S(1)}, u32[]{:S(2)}, u32[]{:S(2)}) collective-permute-start(f32[80,512]{1,0:T(8,128)S(1)} %get-tuple-element.22), channel_id=1, source_target_pairs={{0,11},{16,27},{32,43},{48,59},{64,75},{80,91},{96,107},{112,123}} | collective-permute-start | bytes 491528 | tf_op jit(solution)/shard_map/ppermute | solution.py:97
  161.9 6.6 %collective-permute-start.12 = (f32[80,512]{1,0:T(8,128)S(1)}, f32[80,512]{1,0:T(8,128)S(1)}, u32[]{:S(2)}, u32[]{:S(2)}) collective-permute-start(f32[80,512]{1,0:T(8,128)S(1)} %get-tuple-element.20), channel_id=1, source_target_pairs={{0,13},{16,29},{32,45},{48,61},{64,77},{80,93},{96,109},{112,125}} | collective-permute-start | bytes 491528 | tf_op jit(solution)/shard_map/ppermute | solution.py:97
  163.2 8.5 %collective-permute-start.13 = (f32[80,512]{1,0:T(8,128)S(1)}, f32[80,512]{1,0:T(8,128)S(1)}, u32[]{:S(2)}, u32[]{:S(2)}) collective-permute-start(f32[80,512]{1,0:T(8,128)S(1)} %get-tuple-element.19), channel_id=1, source_target_pairs={{0,14},{16,30},{32,46},{48,62},{64,78},{80,94},{96,110},{112,126}} | collective-permute-start | bytes 491528 | tf_op jit(solution)/shard_map/ppermute | solution.py:97
  164.5 10.7 %collective-permute-start.14 = (f32[80,512]{1,0:T(8,128)S(1)}, f32[80,512]{1,0:T(8,128)S(1)}, u32[]{:S(2)}, u32[]{:S(2)}) collective-permute-start(f32[80,512]{1,0:T(8,128)S(1)} %get-tuple-element.18), channel_id=1, source_target_pairs={{0,15},{16,31},{32,47},{48,63},{64,79},{80,95},{96,111},{112,127}} | collective-permute-start | bytes 491528 | tf_op jit(solution)/shard_map/ppermute | solution.py:97
  165.8 11.3 %collective-permute-start.2 = (f32[80,512]{1,0:T(8,128)S(1)}, f32[80,512]{1,0:T(8,128)S(1)}, u32[]{:S(2)}, u32[]{:S(2)}) collective-permute-start(f32[80,512]{1,0:T(8,128)S(1)} %get-tuple-element.30), channel_id=1, source_target_pairs={{0,3},{16,19},{32,35},{48,51},{64,67},{80,83},{96,99},{112,115}} | collective-permute-start | bytes 491528 | tf_op jit(solution)/shard_map/ppermute | solution.py:97
  167.1 12.0 %collective-permute-start.3 = (f32[80,512]{1,0:T(8,128)S(1)}, f32[80,512]{1,0:T(8,128)S(1)}, u32[]{:S(2)}, u32[]{:S(2)}) collective-permute-start(f32[80,512]{1,0:T(8,128)S(1)} %get-tuple-element.29), channel_id=1, source_target_pairs={{0,4},{16,20},{32,36},{48,52},{64,68},{80,84},{96,100},{112,116}} | collective-permute-start | bytes 491528 | tf_op jit(solution)/shard_map/ppermute | solution.py:97
  168.5 12.6 %collective-permute-start.4 = (f32[80,512]{1,0:T(8,128)S(1)}, f32[80,512]{1,0:T(8,128)S(1)}, u32[]{:S(2)}, u32[]{:S(2)}) collective-permute-start(f32[80,512]{1,0:T(8,128)S(1)} %get-tuple-element.28), channel_id=1, source_target_pairs={{0,5},{16,21},{32,37},{48,53},{64,69},{80,85},{96,101},{112,117}} | collective-permute-start | bytes 491528 | tf_op jit(solution)/shard_map/ppermute | solution.py:97
  171.7 11.3 %collective-permute-start.5 = (f32[80,512]{1,0:T(8,128)S(1)}, f32[80,512]{1,0:T(8,128)}, u32[]{:S(2)}, u32[]{:S(2)}) collective-permute-start(f32[80,512]{1,0:T(8,128)S(1)} %get-tuple-element.27), channel_id=1, source_target_pairs={{0,6},{16,22},{32,38},{48,54},{64,70},{80,86},{96,102},{112,118}} | collective-permute-start | bytes 491528 | tf_op jit(solution)/shard_map/ppermute | solution.py:97
  175.2 7.8 %collective-permute-start.6 = (f32[80,512]{1,0:T(8,128)S(1)}, f32[80,512]{1,0:T(8,128)}, u32[]{:S(2)}, u32[]{:S(2)}) collective-permute-start(f32[80,512]{1,0:T(8,128)S(1)} %get-tuple-element.26), channel_id=1, source_target_pairs={{0,7},{16,23},{32,39},{48,55},{64,71},{80,87},{96,103},{112,119}} | collective-permute-start | bytes 491528 | tf_op jit(solution)/shard_map/ppermute | solution.py:97
  177.1 8.1 %collective-permute-start.7 = (f32[80,512]{1,0:T(8,128)S(1)}, f32[80,512]{1,0:T(8,128)}, u32[]{:S(2)}, u32[]{:S(2)}) collective-permute-start(f32[80,512]{1,0:T(8,128)S(1)} %get-tuple-element.25), channel_id=1, source_target_pairs={{0,8},{16,24},{32,40},{48,56},{64,72},{80,88},{96,104},{112,120}} | collective-permute-start | bytes 491528 | tf_op jit(solution)/shard_map/ppermute | solution.py:97
  179.1 9.7 %collective-permute-start.8 = (f32[80,512]{1,0:T(8,128)S(1)}, f32[80,512]{1,0:T(8,128)}, u32[]{:S(2)}, u32[]{:S(2)}) collective-permute-start(f32[80,512]{1,0:T(8,128)S(1)} %get-tuple-element.24), channel_id=1, source_target_pairs={{0,9},{16,25},{32,41},{48,57},{64,73},{80,89},{96,105},{112,121}} | collective-permute-start | bytes 491528 | tf_op jit(solution)/shard_map/ppermute | solution.py:97
  181.1 11.2 %collective-permute-start.9 = (f32[80,512]{1,0:T(8,128)S(1)}, f32[80,512]{1,0:T(8,128)}, u32[]{:S(2)}, u32[]{:S(2)}) collective-permute-start(f32[80,512]{1,0:T(8,128)S(1)} %get-tuple-element.23), channel_id=1, source_target_pairs={{0,10},{16,26},{32,42},{48,58},{64,74},{80,90},{96,106},{112,122}} | collective-permute-start | bytes 491528 | tf_op jit(solution)/shard_map/ppermute | solution.py:97
  207.6 10.4 %collective-permute-start.15 = (f32[80,512]{1,0:T(8,128)S(1)}, f32[80,512]{1,0:T(8,128)S(1)}, u32[]{:S(2)}, u32[]{:S(2)}) collective-permute-start(f32[80,512]{1,0:T(8,128)S(1)} %copy-done.4), channel_id=1, source_target_pairs={{0,0},{1,16},{2,32},{3,48},{4,64},{5,80},{6,96},{7,112},{8,1},{9,1... | collective-permute-start | bytes 491528 | tf_op jit(solution)/shard_map/ppermute | solution.py:113
  218.0 12.8 %collective-permute-start.16 = (f32[80,512]{1,0:T(8,128)S(1)}, f32[80,512]{1,0:T(8,128)S(1)}, u32[]{:S(2)}, u32[]{:S(2)}) collective-permute-start(f32[80,512]{1,0:T(8,128)S(1)} %collective-permute-done.15), channel_id=1, source_target_pairs={{0,16},{16,32},{32,48},{48,64},{64,80},{80,96},{96,112},{112,0},{1... | collective-permute-start | bytes 491528 | tf_op jit(solution)/shard_map/ppermute | solution.py:117
  225.0 6.9 %collective-permute-start.17 = (f32[80,512]{1,0:T(8,128)S(1)}, f32[80,512]{1,0:T(8,128)S(1)}, u32[]{:S(2)}, u32[]{:S(2)}) collective-permute-start(f32[80,512]{1,0:T(8,128)S(1)} %collective-permute-done.15), channel_id=1, source_target_pairs={{0,32},{16,48},{32,64},{48,80},{64,96},{80,112},{96,0},{112,16},{1... | collective-permute-start | bytes 491528 | tf_op jit(solution)/shard_map/ppermute | solution.py:117
  225.0 10.5 %collective-permute-start.18 = (f32[80,512]{1,0:T(8,128)S(1)}, f32[80,512]{1,0:T(8,128)S(1)}, u32[]{:S(2)}, u32[]{:S(2)}) collective-permute-start(f32[80,512]{1,0:T(8,128)S(1)} %collective-permute-done.15), channel_id=1, source_target_pairs={{0,48},{16,64},{32,80},{48,96},{64,112},{80,0},{96,16},{112,32},{1... | collective-permute-start | bytes 491528 | tf_op jit(solution)/shard_map/ppermute | solution.py:117
  228.1 14.0 %collective-permute-start.19 = (f32[80,512]{1,0:T(8,128)S(1)}, f32[80,512]{1,0:T(8,128)S(1)}, u32[]{:S(2)}, u32[]{:S(2)}) collective-permute-start(f32[80,512]{1,0:T(8,128)S(1)} %collective-permute-done.15), channel_id=1, source_target_pairs={{0,64},{16,80},{32,96},{48,112},{64,0},{80,16},{96,32},{112,48},{1... | collective-permute-start | bytes 491528 | tf_op jit(solution)/shard_map/ppermute | solution.py:117
  228.3 14.5 %collective-permute-start.20 = (f32[80,512]{1,0:T(8,128)S(1)}, f32[80,512]{1,0:T(8,128)S(1)}, u32[]{:S(2)}, u32[]{:S(2)}) collective-permute-start(f32[80,512]{1,0:T(8,128)S(1)} %collective-permute-done.15), channel_id=1, source_target_pairs={{0,80},{16,96},{32,112},{48,0},{64,16},{80,32},{96,48},{112,64},{1... | collective-permute-start | bytes 491528 | tf_op jit(solution)/shard_map/ppermute | solution.py:117
  230.8 12.0 %collective-permute-start.21 = (f32[80,512]{1,0:T(8,128)S(1)}, f32[80,512]{1,0:T(8,128)S(1)}, u32[]{:S(2)}, u32[]{:S(2)}) collective-permute-start(f32[80,512]{1,0:T(8,128)S(1)} %collective-permute-done.15), channel_id=1, source_target_pairs={{0,96},{16,112},{32,0},{48,16},{64,32},{80,48},{96,64},{112,80},{1... | collective-permute-start | bytes 491528 | tf_op jit(solution)/shard_map/ppermute | solution.py:117
  232.0 11.0 %collective-permute-start.22 = (f32[80,512]{1,0:T(8,128)S(1)}, f32[80,512]{1,0:T(8,128)S(1)}, u32[]{:S(2)}, u32[]{:S(2)}) collective-permute-start(f32[80,512]{1,0:T(8,128)S(1)} %collective-permute-done.15), channel_id=1, source_target_pairs={{0,112},{16,0},{32,16},{48,32},{64,48},{80,64},{96,80},{112,96},{1... | collective-permute-start | bytes 491528 | tf_op jit(solution)/shard_map/ppermute | solution.py:117
  (8 other events, 240.8 us)
Sparse Core Ops, SparseCore 0:
  195.6 49.4 all-gather.1

commit v8 on v7

--- a/solution.py
+++ b/solution.py
@@ -90,20 +90,28 @@
     raw_panel = assemble(PANEL // BLK) + diag[:, :PANEL]
     front_local = assemble(front_cols) + diag
     piece_rows = height // col_count
-    piece_rows = height // col_count
-    piece = jnp.where(col_index == 0, raw_panel[:piece_rows], 0.0)
-    for k in range(1, col_count):
-        pairs = [(r * col_count, r * col_count + k) for r in range(row_count)]
-        piece = piece + lax.ppermute(
-            raw_panel[k * piece_rows:(k + 1) * piece_rows], ("row", "col"), pairs
+    half_rows = piece_rows // 2
+    factor_halves = []
+    gathered_halves = []
+    for h in range(2):
+        lo = h * half_rows
+        piece = jnp.where(col_index == 0, raw_panel[lo:lo + half_rows], 0.0)
+        for k in range(1, col_count):
+            pairs = [(r * col_count, r * col_count + k) for r in range(row_count)]
+            start = k * piece_rows + lo
+            piece = piece + lax.ppermute(
+                raw_panel[start:start + half_rows], ("row", "col"), pairs
+            )
+        factor_half = jnp.dot(
+            piece,
+            panel_inverse.T,
+            precision=lax.Precision.HIGHEST,
+            preferred_element_type=jnp.float32,
         )
-    factor_piece = jnp.dot(
-        piece,
-        panel_inverse.T,
-        precision=lax.Precision.HIGHEST,
-        preferred_element_type=jnp.float32,
-    )
-    factor_panel = lax.all_gather(factor_piece, "col", axis=0, tiled=True)
+        factor_halves.append(factor_half)
+        gathered_halves.append(lax.all_gather(factor_half, "col", axis=0, tiled=False))
+    factor_piece = jnp.concatenate(factor_halves, axis=0)
+    factor_panel = jnp.stack(gathered_halves, axis=1).reshape(height, PANEL)
     ratio = col_count // row_count
     pairs = [
         (r * col_count + k, (k % row_count) * col_count + r * ratio + k // row_count)

time: 268 us -> 296 us (1.10)
  starting transfers between devices: 55.7 us -> 71.2 us
  waiting for transfers between devices: 116 us -> 129 us
    all_gather x1 -> x2, waiting for transfers between devices: 0.02 us -> 20.5 us  [on_device(): lax.all_gather(factor_half, 'col', axis=0, tiled=False)]
    ppermute x15 -> x30, starting transfers between devices: 26 us -> 44.6 us  [on_device(): lax.ppermute(raw_panel[start:start + half_rows], ('row', 'col'), pairs)]
    ppermute x15 -> x30, waiting for transfers between devices: 12.8 us -> 1.67 us  [on_device(): lax.ppermute(raw_panel[start:start + half_rows], ('row', 'col'), pairs)]
    ppermute x7, starting transfers between devices: 15.6 us -> 12.6 us  [on_device(): stack.append(lax.ppermute(moved, 'row', shift))]
    unnamed x23 -> x28, local copies, waits for them, and re-layouts: 6.51 us -> 4.1 us
  transfers between devices with their start and end apart: 25 -> 41, of which waited for: 12 -> 10; matrix products, arithmetic and copies ran while one was open for 11% -> 11% of each run, Pallas kernels for 0% -> 0%
where the time goes in v8:
time: 296 us; the launch traced here: 293 us
  waiting for transfers between devices  129 us (44%)
  starting transfers between devices  71.2 us (24%)
  local copies, waits for them, and re-layouts  50.8 us (17%)
  between operations  15 us (5%)
  other arithmetic  14 us (5%)
  matrix products  13.4 us (5%)
    all_to_all x1, waiting for transfers between devices, on_device(): lax.all_to_all(outgoing, ('row', 'col'), split_axis=0, concat_axis=0, til...  93.6 us
    ppermute x30, starting transfers between devices, on_device(): lax.ppermute(raw_panel[start:start + half_rows], ('row', 'col'), pairs)  44.6 us
    gather x4, local copies, waits for them, and re-layouts, assemble(): jnp.take(incoming, source[:, :width].reshape(-1), axis=0, mode='fill', fi...  22.9 us
    all_gather x2, waiting for transfers between devices, on_device(): lax.all_gather(factor_half, 'col', axis=0, tiled=False)  20.5 us
    ppermute x7, starting transfers between devices, on_device(): stack.append(lax.ppermute(moved, 'row', shift))  12.6 us
    all_to_all x1, starting transfers between devices, on_device(): lax.all_to_all(outgoing, ('row', 'col'), split_axis=0, concat_axis=0, til...  11.9 us
    ppermute x7, waiting for transfers between devices, on_device(): stack.append(lax.ppermute(moved, 'row', shift))  11 us
    dot_general x1, matrix products, on_device(): lax.dot_general(factor_panel, across, (((1,), (1,)), ((), ())), precision...  8.61 us
  transfers between devices with their start and end apart: 41, of which 10 were waited for; matrix products, arithmetic and copies ran while one was open for 11% of the time, Pallas kernels for 0%

profile of v8, /device:TPU:1, one launch (start us, length us, event | category | flops | bytes accessed | tf_op | source)
XLA Modules:
  0.0 293.3 jit_solution(6854774810062246213)
XLA Ops:
  9.5 3.2 %copy.19 = f32[128,8,8,128]{3,2,1,0:T(8,128)S(1)} copy(f32[128,8,8,128]{3,1,2,0:T(8,128)} %bitcast.92) | data formatting | bytes 8388608
  13.7 2.4 concatenate.6
  16.1 6.6 %gather_fusion = f32[128,128,128]{2,1,0:T(8,128)} fusion(f32[65,128,128]{2,1,0:T(8,128)} %concatenate.6, s32[1024]{0:T(1024)S(1)} %pad_clamp_fusion.5), kind=kCustom, calls=%fused_computation.8 | custom fusion | bytes 16777728 | tf_op jit(solution)/shard_map/jit(_take)/gather | solution.py:51
  22.6 11.9 %all-to-all-start = ((f32[128,1,128,128]{3,2,1,0:T(8,128)}), f32[128,1,128,128]{3,2,1,0:T(8,128)}, u32[]{:S(2)}, u32[]{:S(2)}) async-start(f32[128,1,128,128]{3,2,1,0:T(8,128)} %bitcast.80), calls=%async_computation | async-start | bytes 16777216 | tf_op jit(solution)/shard_map/all_to_all | solution.py:54
  39.5 2.1 compare_select_fusion
  41.6 93.6 %all-to-all-done = f32[128,1,128,128]{3,2,1,0:T(8,128)} async-done(((f32[128,1,128,128]{3,2,1,0:T(8,128)}), f32[128,1,128,128]{3,2,1,0:T(8,128)}, u32[]{:S(2)}, u32[]{:S(2)}) %all-to-all-start) | async-done | bytes 8388640 | tf_op jit(solution)/shard_map/all_to_all | solution.py:54
  135.2 5.6 %gather_fusion.4 = f32[40,128,128]{2,1,0:T(8,128)} fusion(f32[128,128,128]{2,1,0:T(8,128)} %bitcast.10, s32[1024]{0:T(1024)S(1)} %pad_clamp_fusion.4), kind=kCustom, calls=%fused_computation.2.clone | custom fusion | bytes 5243040 | tf_op jit(solution)/shard_map/jit(_take)/gather | solution.py:77
  140.8 5.6 %gather_fusion.7 = f32[40,128,128]{2,1,0:T(8,128)} fusion(f32[128,128,128]{2,1,0:T(8,128)} %bitcast.10, s32[1024]{0:T(1024)S(1)} %pad_clamp_fusion.3), kind=kCustom, calls=%fused_computation.6.clone | custom fusion | bytes 5243040 | tf_op jit(solution)/shard_map/jit(_take)/gather | solution.py:77
  146.3 2.9 select_add_fusion.1
  154.4 2.4 collective-permute-start.13
  177.5 2.8 fusion.32
  192.4 2.5 collective-permute-start.24
  201.7 5.8 %gather_fusion.8 = f32[50,128,128]{2,1,0:T(8,128)} fusion(f32[128,128,128]{2,1,0:T(8,128)} %bitcast.10, s32[1024]{0:T(1024)S(1)} %pad_clamp_fusion.2), kind=kCustom, calls=%fused_computation.3.clone | custom fusion | bytes 6553800 | tf_op jit(solution)/shard_map/jit(_take)/gather | solution.py:77
  207.5 5.9 %gather_fusion.9 = f32[50,128,128]{2,1,0:T(8,128)} fusion(f32[128,128,128]{2,1,0:T(8,128)} %bitcast.10, s32[1024]{0:T(1024)S(1)} %pad_clamp_fusion.1), kind=kCustom, calls=%fused_computation.7.clone | custom fusion | bytes 6553800 | tf_op jit(solution)/shard_map/jit(_take)/gather | solution.py:77
  213.4 2.0 fusion.15
  217.4 3.4 %select_add_fusion = f32[50,128,128]{2,1,0:T(8,128)S(1)} fusion(f32[50,128,128]{2,1,0:T(8,128)} %gather_fusion.9, f32[50,128,128]{2,1,0:T(8,128)} %gather_fusion.8, pred[50]{0:T(512)(128)(4,1)S(1)} %get-tuple-element.55, pred[50]{0:T(512)(128)(4,1)S(1)} %get-tuple-element.56), kind=kLoop, calls=%fused_computation.17 | loop fusion | flops 2457600 | bytes 9830500 | tf_op jit(solution)/shard_map/add | solution.py:80
  220.8 4.3 %copy.18 = f32[10,128,5,128]{3,2,1,0:T(8,128)} copy(f32[10,128,5,128]{3,1,2,0:T(8,128)S(1)} %bitcast.86) | data formatting | bytes 6553600 | tf_op jit(solution)/shard_map/transpose | solution.py:83
  225.1 2.3 collective-permute-done.30
  227.3 5.6 %collective-permute-start.31 = (f32[80,512]{1,0:T(8,128)S(1)}, f32[80,512]{1,0:T(8,128)S(1)}, u32[]{:S(2)}, u32[]{:S(2)}) collective-permute-start(f32[80,512]{1,0:T(8,128)S(1)} %collective-permute-done.30), channel_id=1, source_target_pairs={{0,16},{16,32},{32,48},{48,64},{64,80},{80,96},{96,112},{112,0},{1... | collective-permute-start | bytes 491528 | tf_op jit(solution)/shard_map/ppermute | solution.py:125
  234.4 3.0 %collective-permute-start.34 = (f32[80,512]{1,0:T(8,128)S(1)}, f32[80,512]{1,0:T(8,128)S(1)}, u32[]{:S(2)}, u32[]{:S(2)}) collective-permute-start(f32[80,512]{1,0:T(8,128)S(1)} %collective-permute-done.30), channel_id=1, source_target_pairs={{0,64},{16,80},{32,96},{48,112},{64,0},{80,16},{96,32},{112,48},{1... | collective-permute-start | bytes 491528 | tf_op jit(solution)/shard_map/ppermute | solution.py:125
  242.2 6.2 %collective-permute-done.34 = f32[80,512]{1,0:T(8,128)S(1)} collective-permute-done((f32[80,512]{1,0:T(8,128)S(1)}, f32[80,512]{1,0:T(8,128)S(1)}, u32[]{:S(2)}, u32[]{:S(2)}) %collective-permute-start.34) | collective-permute-done | bytes 163872 | tf_op jit(solution)/shard_map/ppermute | solution.py:125
  254.4 20.5 %all-gather.7.cloned.1.call-done = f32[640,512]{1,0:T(8,128)} async-done(((f32[40,512]{1,0:T(8,128)}), f32[640,512]{1,0:T(8,128)}) %all-gather.7.cloned.1.call-update) | async-done | bytes 1310736 | tf_op jit(solution)/shard_map/all_gather | solution.py:112
  274.9 2.1 pad_maximum_fusion
  277.9 8.6 %convolution_subtract_fusion = f32[1280,640]{1,0:T(8,128)} fusion(f32[1280,512]{1,0:T(8,128)S(1)} %bitcast.88, f32[640,512]{1,0:T(8,128)S(1)} %bitcast.91, f32[160,8,5,128]{3,2,1,0:T(8,128)S(1)} %bitcast.85, f32[1280]{0:T(1024)S(1)} %copy-done.6, s32[640]{0:T(1024)S(1)} %iota_add_fusion.1, s32[1280]{0:T(1024)S(1)} %iota_add_fusion), kind=kOutput, calls=%fused_computation.15 | convolution fusion | flops 5036441600 | bytes 10498560 | tf_op jit(solution)/shard_map/dot_general | solution.py:128
  (165 shorter events, 67.3 us)
Async XLA Ops:
  22.6 112.5 %all-to-all-start = ((f32[128,1,128,128]{3,2,1,0:T(8,128)}), f32[128,1,128,128]{3,2,1,0:T(8,128)}, u32[]{:S(2)}, u32[]{:S(2)}) async-start(f32[128,1,128,128]{3,2,1,0:T(8,128)} %bitcast.80), calls=%async_computation | async-start | bytes 16777216 | tf_op jit(solution)/shard_map/all_to_all | solution.py:54
  34.6 219.8 %all-gather.5.cloned.1.call-start = ((), (), s32[]{:S(2)}) async-start(), calls=%async_computation.1 | async-start | bytes 1392640 | tf_op jit(solution)/shard_map/all_gather | solution.py:112
  153.1 8.0 %collective-permute-start.12 = (f32[40,512]{1,0:T(8,128)S(1)}, f32[40,512]{1,0:T(8,128)S(1)}, u32[]{:S(2)}, u32[]{:S(2)}) collective-permute-start(f32[40,512]{1,0:T(8,128)S(1)} %get-tuple-element.35), channel_id=1, source_target_pairs={{0,13},{16,29},{32,45},{48,61},{64,77},{80,93},{96,109},{112,125}} | collective-permute-start | bytes 245768 | tf_op jit(solution)/shard_map/ppermute | solution.py:102
  154.4 8.0 %collective-permute-start.13 = (f32[40,512]{1,0:T(8,128)S(1)}, f32[40,512]{1,0:T(8,128)S(1)}, u32[]{:S(2)}, u32[]{:S(2)}) collective-permute-start(f32[40,512]{1,0:T(8,128)S(1)} %get-tuple-element.34), channel_id=1, source_target_pairs={{0,14},{16,30},{32,46},{48,62},{64,78},{80,94},{96,110},{112,126}} | collective-permute-start | bytes 245768 | tf_op jit(solution)/shard_map/ppermute | solution.py:102
  162.4 7.8 %collective-permute-start.2 = (f32[40,512]{1,0:T(8,128)S(1)}, f32[40,512]{1,0:T(8,128)S(1)}, u32[]{:S(2)}, u32[]{:S(2)}) collective-permute-start(f32[40,512]{1,0:T(8,128)S(1)} %get-tuple-element.46), channel_id=1, source_target_pairs={{0,3},{16,19},{32,35},{48,51},{64,67},{80,83},{96,99},{112,115}} | collective-permute-start | bytes 245768 | tf_op jit(solution)/shard_map/ppermute | solution.py:102
  163.7 8.4 %collective-permute-start.3 = (f32[40,512]{1,0:T(8,128)S(1)}, f32[40,512]{1,0:T(8,128)S(1)}, u32[]{:S(2)}, u32[]{:S(2)}) collective-permute-start(f32[40,512]{1,0:T(8,128)S(1)} %get-tuple-element.45), channel_id=1, source_target_pairs={{0,4},{16,20},{32,36},{48,52},{64,68},{80,84},{96,100},{112,116}} | collective-permute-start | bytes 245768 | tf_op jit(solution)/shard_map/ppermute | solution.py:102
  165.0 9.0 %collective-permute-start.4 = (f32[40,512]{1,0:T(8,128)S(1)}, f32[40,512]{1,0:T(8,128)S(1)}, u32[]{:S(2)}, u32[]{:S(2)}) collective-permute-start(f32[40,512]{1,0:T(8,128)S(1)} %get-tuple-element.44), channel_id=1, source_target_pairs={{0,5},{16,21},{32,37},{48,53},{64,69},{80,85},{96,101},{112,117}} | collective-permute-start | bytes 245768 | tf_op jit(solution)/shard_map/ppermute | solution.py:102
  166.3 9.6 %collective-permute-start.5 = (f32[40,512]{1,0:T(8,128)S(1)}, f32[40,512]{1,0:T(8,128)}, u32[]{:S(2)}, u32[]{:S(2)}) collective-permute-start(f32[40,512]{1,0:T(8,128)S(1)} %get-tuple-element.43), channel_id=1, source_target_pairs={{0,6},{16,22},{32,38},{48,54},{64,70},{80,86},{96,102},{112,118}} | collective-permute-start | bytes 245768 | tf_op jit(solution)/shard_map/ppermute | solution.py:102
  180.3 94.6 %all-gather.7.cloned.1.call-start = ((), (), s32[]{:S(2)}) async-start(), calls=%async_computation.2 | async-start | bytes 1392640 | tf_op jit(solution)/shard_map/all_gather | solution.py:112
  187.2 7.7 %collective-permute-start.20 = (f32[40,512]{1,0:T(8,128)S(1)}, f32[40,512]{1,0:T(8,128)S(1)}, u32[]{:S(2)}, u32[]{:S(2)}) collective-permute-start(f32[40,512]{1,0:T(8,128)S(1)} %get-tuple-element.27), channel_id=1, source_target_pairs={{0,6},{16,22},{32,38},{48,54},{64,70},{80,86},{96,102},{112,118}} | collective-permute-start | bytes 245768 | tf_op jit(solution)/shard_map/ppermute | solution.py:102
  188.5 7.7 %collective-permute-start.21 = (f32[40,512]{1,0:T(8,128)S(1)}, f32[40,512]{1,0:T(8,128)S(1)}, u32[]{:S(2)}, u32[]{:S(2)}) collective-permute-start(f32[40,512]{1,0:T(8,128)S(1)} %get-tuple-element.26), channel_id=1, source_target_pairs={{0,7},{16,23},{32,39},{48,55},{64,71},{80,87},{96,103},{112,119}} | collective-permute-start | bytes 245768 | tf_op jit(solution)/shard_map/ppermute | solution.py:102
  191.1 7.7 %collective-permute-start.23 = (f32[40,512]{1,0:T(8,128)S(1)}, f32[40,512]{1,0:T(8,128)S(1)}, u32[]{:S(2)}, u32[]{:S(2)}) collective-permute-start(f32[40,512]{1,0:T(8,128)S(1)} %get-tuple-element.24), channel_id=1, source_target_pairs={{0,9},{16,25},{32,41},{48,57},{64,73},{80,89},{96,105},{112,121}} | collective-permute-start | bytes 245768 | tf_op jit(solution)/shard_map/ppermute | solution.py:102
  194.9 18.4 %collective-permute-start.25 = (f32[40,512]{1,0:T(8,128)S(1)}, f32[40,512]{1,0:T(8,128)S(1)}, u32[]{:S(2)}, u32[]{:S(2)}) collective-permute-start(f32[40,512]{1,0:T(8,128)S(1)} %get-tuple-element.22), channel_id=1, source_target_pairs={{0,11},{16,27},{32,43},{48,59},{64,75},{80,91},{96,107},{112,123}} | collective-permute-start | bytes 245768 | tf_op jit(solution)/shard_map/ppermute | solution.py:102
  196.2 17.1 %collective-permute-start.26 = (f32[40,512]{1,0:T(8,128)S(1)}, f32[40,512]{1,0:T(8,128)S(1)}, u32[]{:S(2)}, u32[]{:S(2)}) collective-permute-start(f32[40,512]{1,0:T(8,128)S(1)} %get-tuple-element.21), channel_id=1, source_target_pairs={{0,12},{16,28},{32,44},{48,60},{64,76},{80,92},{96,108},{112,124}} | collective-permute-start | bytes 245768 | tf_op jit(solution)/shard_map/ppermute | solution.py:102
  197.5 15.8 %collective-permute-start.27 = (f32[40,512]{1,0:T(8,128)S(1)}, f32[40,512]{1,0:T(8,128)S(1)}, u32[]{:S(2)}, u32[]{:S(2)}) collective-permute-start(f32[40,512]{1,0:T(8,128)S(1)} %get-tuple-element.20), channel_id=1, source_target_pairs={{0,13},{16,29},{32,45},{48,61},{64,77},{80,93},{96,109},{112,125}} | collective-permute-start | bytes 245768 | tf_op jit(solution)/shard_map/ppermute | solution.py:102
  198.8 14.5 %collective-permute-start.28 = (f32[40,512]{1,0:T(8,128)S(1)}, f32[40,512]{1,0:T(8,128)S(1)}, u32[]{:S(2)}, u32[]{:S(2)}) collective-permute-start(f32[40,512]{1,0:T(8,128)S(1)} %get-tuple-element.19), channel_id=1, source_target_pairs={{0,14},{16,30},{32,46},{48,62},{64,78},{80,94},{96,110},{112,126}} | collective-permute-start | bytes 245768 | tf_op jit(solution)/shard_map/ppermute | solution.py:102
  200.2 13.2 %collective-permute-start.29 = (f32[40,512]{1,0:T(8,128)S(1)}, f32[40,512]{1,0:T(8,128)S(1)}, u32[]{:S(2)}, u32[]{:S(2)}) collective-permute-start(f32[40,512]{1,0:T(8,128)S(1)} %get-tuple-element.18), channel_id=1, source_target_pairs={{0,15},{16,31},{32,47},{48,63},{64,79},{80,95},{96,111},{112,127}} | collective-permute-start | bytes 245768 | tf_op jit(solution)/shard_map/ppermute | solution.py:102
  215.4 11.9 %collective-permute-start.30 = (f32[80,512]{1,0:T(8,128)S(1)}, f32[80,512]{1,0:T(8,128)S(1)}, u32[]{:S(2)}, u32[]{:S(2)}) collective-permute-start(f32[80,512]{1,0:T(8,128)S(1)} %pad_maximum_fusion.1), channel_id=1, source_target_pairs={{0,0},{1,16},{2,32},{3,48},{4,64},{5,80},{6,96},{7,112},{8,1},{9,1... | collective-permute-start | bytes 491528 | tf_op jit(solution)/shard_map/ppermute | solution.py:121
  227.3 10.1 %collective-permute-start.31 = (f32[80,512]{1,0:T(8,128)S(1)}, f32[80,512]{1,0:T(8,128)S(1)}, u32[]{:S(2)}, u32[]{:S(2)}) collective-permute-start(f32[80,512]{1,0:T(8,128)S(1)} %collective-permute-done.30), channel_id=1, source_target_pairs={{0,16},{16,32},{32,48},{48,64},{64,80},{80,96},{96,112},{112,0},{1... | collective-permute-start | bytes 491528 | tf_op jit(solution)/shard_map/ppermute | solution.py:125
  233.8 8.4 %collective-permute-start.33 = (f32[80,512]{1,0:T(8,128)S(1)}, f32[80,512]{1,0:T(8,128)S(1)}, u32[]{:S(2)}, u32[]{:S(2)}) collective-permute-start(f32[80,512]{1,0:T(8,128)S(1)} %collective-permute-done.30), channel_id=1, source_target_pairs={{0,48},{16,64},{32,80},{48,96},{64,112},{80,0},{96,16},{112,32},{1... | collective-permute-start | bytes 491528 | tf_op jit(solution)/shard_map/ppermute | solution.py:125
  234.4 13.9 %collective-permute-start.34 = (f32[80,512]{1,0:T(8,128)S(1)}, f32[80,512]{1,0:T(8,128)S(1)}, u32[]{:S(2)}, u32[]{:S(2)}) collective-permute-start(f32[80,512]{1,0:T(8,128)S(1)} %collective-permute-done.30), channel_id=1, source_target_pairs={{0,64},{16,80},{32,96},{48,112},{64,0},{80,16},{96,32},{112,48},{1... | collective-permute-start | bytes 491528 | tf_op jit(solution)/shard_map/ppermute | solution.py:125
  237.4 11.6 %collective-permute-start.35 = (f32[80,512]{1,0:T(8,128)S(1)}, f32[80,512]{1,0:T(8,128)S(1)}, u32[]{:S(2)}, u32[]{:S(2)}) collective-permute-start(f32[80,512]{1,0:T(8,128)S(1)} %collective-permute-done.30), channel_id=1, source_target_pairs={{0,80},{16,96},{32,112},{48,0},{64,16},{80,32},{96,48},{112,64},{1... | collective-permute-start | bytes 491528 | tf_op jit(solution)/shard_map/ppermute | solution.py:125
  237.4 12.1 %collective-permute-start.36 = (f32[80,512]{1,0:T(8,128)S(1)}, f32[80,512]{1,0:T(8,128)S(1)}, u32[]{:S(2)}, u32[]{:S(2)}) collective-permute-start(f32[80,512]{1,0:T(8,128)S(1)} %collective-permute-done.30), channel_id=1, source_target_pairs={{0,96},{16,112},{32,0},{48,16},{64,32},{80,48},{96,64},{112,80},{1... | collective-permute-start | bytes 491528 | tf_op jit(solution)/shard_map/ppermute | solution.py:125
  238.7 12.4 %collective-permute-start.37 = (f32[80,512]{1,0:T(8,128)S(1)}, f32[80,512]{1,0:T(8,128)S(1)}, u32[]{:S(2)}, u32[]{:S(2)}) collective-permute-start(f32[80,512]{1,0:T(8,128)S(1)} %collective-permute-done.30), channel_id=1, source_target_pairs={{0,112},{16,0},{32,16},{48,32},{64,48},{80,64},{96,80},{112,96},{1... | collective-permute-start | bytes 491528 | tf_op jit(solution)/shard_map/ppermute | solution.py:125
  (27 other events, 364.4 us)
Sparse Core Ops, SparseCore 0:
  180.5 52.4 all-gather.4
  235.1 39.7 all-gather.6

commit v9 on v7

--- a/solution.py
+++ b/solution.py
@@ -90,7 +90,6 @@
     raw_panel = assemble(PANEL // BLK) + diag[:, :PANEL]
     front_local = assemble(front_cols) + diag
     piece_rows = height // col_count
-    piece_rows = height // col_count
     piece = jnp.where(col_index == 0, raw_panel[:piece_rows], 0.0)
     for k in range(1, col_count):
         pairs = [(r * col_count, r * col_count + k) for r in range(row_count)]
@@ -103,7 +102,12 @@
         precision=lax.Precision.HIGHEST,
         preferred_element_type=jnp.float32,
     )
-    factor_panel = lax.all_gather(factor_piece, "col", axis=0, tiled=True)
+    col_stack = [factor_piece]
+    for q in range(1, col_count):
+        shift = [(t, (t + q) % col_count) for t in range(col_count)]
+        col_stack.append(lax.ppermute(factor_piece, "col", shift))
+    col_order = (col_index - jnp.arange(col_count, dtype=jnp.int32)) % col_count
+    factor_panel = jnp.take(jnp.stack(col_stack), col_order, axis=0).reshape(height, PANEL)
     ratio = col_count // row_count
     pairs = [
         (r * col_count + k, (k % row_count) * col_count + r * ratio + k // row_count)

time: 268 us -> 368 us (1.37)
  starting transfers between devices: 55.7 us -> 103 us
  waiting for transfers between devices: 116 us -> 158 us
  local copies, waits for them, and re-layouts: 53.2 us -> 73.5 us
  between operations: 14.6 us -> 1.28 us
  other arithmetic: 11.6 us -> 17.3 us
    ppermute x0 -> x15, waiting for transfers between devices: none -> 49 us  [on_device(): col_stack.append(lax.ppermute(factor_piece, 'col', shift))]
    ppermute x0 -> x15, starting transfers between devices: none -> 20.8 us  [on_device(): col_stack.append(lax.ppermute(factor_piece, 'col', shift))]
    ppermute x1, starting transfers between devices: 2.09 us -> 19.9 us  [on_device(): moved = lax.ppermute(factor_piece, ('row', 'col'), pairs)]
    unnamed x23 -> x44, local copies, waits for them, and re-layouts: 6.51 us -> 20.7 us
    ppermute x7, starting transfers between devices: 15.6 us -> 25.8 us  [on_device(): stack.append(lax.ppermute(moved, 'row', shift))]
    ppermute x15, waiting for transfers between devices: 12.8 us -> 3.62 us  [on_device(): lax.ppermute(raw_panel[k * piece_rows:(k + 1) * piece_rows], ('row', 'col...]
    select_n x0 -> x3, other arithmetic: none -> 5.52 us  [on_device(): jnp.take(jnp.stack(col_stack), col_order, axis=0).reshape(height, PANEL)]
    gather x0 -> x1, local copies, waits for them, and re-layouts: none -> 3.94 us  [on_device(): jnp.take(jnp.stack(col_stack), col_order, axis=0).reshape(height, PANEL)]
  transfers between devices with their start and end apart: 25 -> 39, of which waited for: 12 -> 16; matrix products, arithmetic and copies ran while one was open for 11% -> 14% of each run, Pallas kernels for 0% -> 0%
where the time goes in v9:
time: 368 us; the launch traced here: 367 us
  waiting for transfers between devices  158 us (43%)
  starting transfers between devices  103 us (28%)
  local copies, waits for them, and re-layouts  73.5 us (20%)
  other arithmetic  17.3 us (5%)
  matrix products  13.7 us (4%)
    all_to_all x1, waiting for transfers between devices, on_device(): lax.all_to_all(outgoing, ('row', 'col'), split_axis=0, concat_axis=0, til...  92.8 us
    ppermute x15, waiting for transfers between devices, on_device(): col_stack.append(lax.ppermute(factor_piece, 'col', shift))  49 us
    ppermute x7, starting transfers between devices, on_device(): stack.append(lax.ppermute(moved, 'row', shift))  25.8 us
    ppermute x15, starting transfers between devices, on_device(): lax.ppermute(raw_panel[k * piece_rows:(k + 1) * piece_rows], ('row', 'col...  24.9 us
    gather x4, local copies, waits for them, and re-layouts, assemble(): jnp.take(incoming, source[:, :width].reshape(-1), axis=0, mode='fill', fi...  22.8 us
    ppermute x15, starting transfers between devices, on_device(): col_stack.append(lax.ppermute(factor_piece, 'col', shift))  20.8 us
    unnamed x44, local copies, waits for them, and re-layouts  20.7 us
    ppermute x1, starting transfers between devices, on_device(): moved = lax.ppermute(factor_piece, ('row', 'col'), pairs)  19.9 us
  transfers between devices with their start and end apart: 39, of which 16 were waited for; matrix products, arithmetic and copies ran while one was open for 14% of the time, Pallas kernels for 0%

profile of v9, /device:TPU:1, one launch (start us, length us, event | category | flops | bytes accessed | tf_op | source)
XLA Modules:
  0.0 366.7 jit_solution(10194545028255614527)
XLA Ops:
  9.5 6.5 %gather_fusion = f32[128,128,128]{2,1,0:T(8,128)} fusion(f32[65,128,128]{2,1,0:T(8,128)} %concatenate.3, s32[1024]{0:T(1024)S(1)} %pad_clamp_fusion.6), kind=kCustom, calls=%fused_computation.8 | custom fusion | bytes 16777728 | tf_op jit(solution)/shard_map/jit(_take)/gather | solution.py:51
  16.1 11.9 %all-to-all-start = ((f32[128,1,128,128]{3,2,1,0:T(8,128)}), f32[128,1,128,128]{3,2,1,0:T(8,128)}, u32[]{:S(2)}, u32[]{:S(2)}) async-start(f32[128,1,128,128]{3,2,1,0:T(8,128)} %bitcast.117), calls=%async_computation | async-start | bytes 16777216 | tf_op jit(solution)/shard_map/all_to_all | solution.py:54
  35.8 92.8 %all-to-all-done = f32[128,1,128,128]{3,2,1,0:T(8,128)} async-done(((f32[128,1,128,128]{3,2,1,0:T(8,128)}), f32[128,1,128,128]{3,2,1,0:T(8,128)}, u32[]{:S(2)}, u32[]{:S(2)}) %all-to-all-start) | async-done | bytes 8388640 | tf_op jit(solution)/shard_map/all_to_all | solution.py:54
  128.6 5.6 %gather_fusion.8 = f32[40,128,128]{2,1,0:T(8,128)} fusion(f32[128,128,128]{2,1,0:T(8,128)} %bitcast.10, s32[1024]{0:T(1024)S(1)} %pad_clamp_fusion.4), kind=kCustom, calls=%fused_computation.6.clone | custom fusion | bytes 5243040 | tf_op jit(solution)/shard_map/jit(_take)/gather | solution.py:77
  134.2 5.6 %gather_fusion.5 = f32[40,128,128]{2,1,0:T(8,128)} fusion(f32[128,128,128]{2,1,0:T(8,128)} %bitcast.10, s32[1024]{0:T(1024)S(1)} %pad_clamp_fusion.5), kind=kCustom, calls=%fused_computation.2.clone | custom fusion | bytes 5243040 | tf_op jit(solution)/shard_map/jit(_take)/gather | solution.py:77
  178.2 5.8 %gather_fusion.10 = f32[50,128,128]{2,1,0:T(8,128)} fusion(f32[128,128,128]{2,1,0:T(8,128)} %bitcast.10, s32[1024]{0:T(1024)S(1)} %pad_clamp_fusion.1), kind=kCustom, calls=%fused_computation.7.clone | custom fusion | bytes 6553800 | tf_op jit(solution)/shard_map/jit(_take)/gather | solution.py:77
  184.1 5.8 %gather_fusion.9 = f32[50,128,128]{2,1,0:T(8,128)} fusion(f32[128,128,128]{2,1,0:T(8,128)} %bitcast.10, s32[1024]{0:T(1024)S(1)} %pad_clamp_fusion.2), kind=kCustom, calls=%fused_computation.3.clone | custom fusion | bytes 6553800 | tf_op jit(solution)/shard_map/jit(_take)/gather | solution.py:77
  195.6 4.3 %copy.14 = f32[10,128,5,128]{3,2,1,0:T(8,128)} copy(f32[10,128,5,128]{3,1,2,0:T(8,128)S(1)} %bitcast.121) | data formatting | bytes 6553600 | tf_op jit(solution)/shard_map/transpose | solution.py:83
  199.9 4.8 %collective-permute-start.29 = (f32[80,512]{1,0:T(8,128)S(1)}, f32[80,512]{1,0:T(8,128)S(1)}, u32[]{:S(2)}, u32[]{:S(2)}) collective-permute-start(f32[80,512]{1,0:T(8,128)S(1)} %get-tuple-element.37), channel_id=1, source_target_pairs={{0,15},{1,0},{2,1},{3,2},{4,3},{5,4},{6,5},{7,6},{8,7},{9,8},{10,9... | collective-permute-start | bytes 491528 | tf_op jit(solution)/shard_map/ppermute | solution.py:108
  208.4 6.7 %collective-permute-done.16 = f32[80,512]{1,0:T(8,128)S(1)} collective-permute-done((f32[80,512]{1,0:T(8,128)S(1)}, f32[80,512]{1,0:T(8,128)S(1)}, u32[]{:S(2)}, u32[]{:S(2)}) %collective-permute-start.16) | collective-permute-done | bytes 163872 | tf_op jit(solution)/shard_map/ppermute | solution.py:108
  215.8 5.6 %collective-permute-done.17 = f32[80,512]{1,0:T(8,128)S(1)} collective-permute-done((f32[80,512]{1,0:T(8,128)S(1)}, f32[80,512]{1,0:T(8,128)S(1)}, u32[]{:S(2)}, u32[]{:S(2)}) %collective-permute-start.17) | collective-permute-done | bytes 163872 | tf_op jit(solution)/shard_map/ppermute | solution.py:108
  222.1 5.0 %collective-permute-done.18 = f32[80,512]{1,0:T(8,128)S(1)} collective-permute-done((f32[80,512]{1,0:T(8,128)S(1)}, f32[80,512]{1,0:T(8,128)S(1)}, u32[]{:S(2)}, u32[]{:S(2)}) %collective-permute-start.18) | collective-permute-done | bytes 163872 | tf_op jit(solution)/shard_map/ppermute | solution.py:108
  230.6 5.3 %collective-permute-done.19 = f32[80,512]{1,0:T(8,128)S(1)} collective-permute-done((f32[80,512]{1,0:T(8,128)S(1)}, f32[80,512]{1,0:T(8,128)S(1)}, u32[]{:S(2)}, u32[]{:S(2)}) %collective-permute-start.19) | collective-permute-done | bytes 163872 | tf_op jit(solution)/shard_map/ppermute | solution.py:108
  238.2 6.3 %collective-permute-done.20 = f32[80,512]{1,0:T(8,128)S(1)} collective-permute-done((f32[80,512]{1,0:T(8,128)S(1)}, f32[80,512]{1,0:T(8,128)S(1)}, u32[]{:S(2)}, u32[]{:S(2)}) %collective-permute-start.20) | collective-permute-done | bytes 163872 | tf_op jit(solution)/shard_map/ppermute | solution.py:108
  245.4 6.0 %collective-permute-done.21 = f32[80,512]{1,0:T(8,128)S(1)} collective-permute-done((f32[80,512]{1,0:T(8,128)S(1)}, f32[80,512]{1,0:T(8,128)S(1)}, u32[]{:S(2)}, u32[]{:S(2)}) %collective-permute-start.21) | collective-permute-done | bytes 163872 | tf_op jit(solution)/shard_map/ppermute | solution.py:108
  253.7 4.2 %collective-permute-done.22 = f32[80,512]{1,0:T(8,128)S(1)} collective-permute-done((f32[80,512]{1,0:T(8,128)S(1)}, f32[80,512]{1,0:T(8,128)S(1)}, u32[]{:S(2)}, u32[]{:S(2)}) %collective-permute-start.22) | collective-permute-done | bytes 163872 | tf_op jit(solution)/shard_map/ppermute | solution.py:108
  260.0 4.5 %collective-permute-done.23 = f32[80,512]{1,0:T(8,128)S(1)} collective-permute-done((f32[80,512]{1,0:T(8,128)S(1)}, f32[80,512]{1,0:T(8,128)S(1)}, u32[]{:S(2)}, u32[]{:S(2)}) %collective-permute-start.23) | collective-permute-done | bytes 163872 | tf_op jit(solution)/shard_map/ppermute | solution.py:108
  276.5 19.9 %collective-permute-start.30 = (f32[80,512]{1,0:T(8,128)S(1)}, f32[80,512]{1,0:T(8,128)S(1)}, u32[]{:S(2)}, u32[]{:S(2)}) collective-permute-start(f32[80,512]{1,0:T(8,128)S(1)} %get-tuple-element.37), channel_id=1, source_target_pairs={{0,0},{1,16},{2,32},{3,48},{4,64},{5,80},{6,96},{7,112},{8,1},{9,1... | collective-permute-start | bytes 491528 | tf_op jit(solution)/shard_map/ppermute | solution.py:117
  299.8 3.9 %gather_fusion.1 = f32[16,80,512]{2,1,0:T(8,128)} fusion(f32[16,80,512]{2,1,0:T(8,128)} %bitcast_dynamic-update-slice_fusion.8, s32[1024]{0:T(1024)S(1)} %pad_clamp_fusion.3), kind=kCustom, calls=%fused_computation.9 | custom fusion | bytes 5242944 | tf_op jit(solution)/shard_map/jit(_take)/gather | solution.py:110
  309.2 7.0 %collective-permute-start.37 = (f32[80,512]{1,0:T(8,128)S(1)}, f32[80,512]{1,0:T(8,128)S(1)}, u32[]{:S(2)}, u32[]{:S(2)}) collective-permute-start(f32[80,512]{1,0:T(8,128)S(1)} %collective-permute-done.30), channel_id=1, source_target_pairs={{0,112},{16,0},{32,16},{48,32},{64,48},{80,64},{96,80},{112,96},{1... | collective-permute-start | bytes 491528 | tf_op jit(solution)/shard_map/ppermute | solution.py:121
  316.2 8.9 %collective-permute-start.36 = (f32[80,512]{1,0:T(8,128)S(1)}, f32[80,512]{1,0:T(8,128)S(1)}, u32[]{:S(2)}, u32[]{:S(2)}) collective-permute-start(f32[80,512]{1,0:T(8,128)S(1)} %collective-permute-done.30), channel_id=1, source_target_pairs={{0,96},{16,112},{32,0},{48,16},{64,32},{80,48},{96,64},{112,80},{1... | collective-permute-start | bytes 491528 | tf_op jit(solution)/shard_map/ppermute | solution.py:121
  330.8 5.1 %collective-permute-done.31 = f32[80,512]{1,0:T(8,128)S(1)} collective-permute-done((f32[80,512]{1,0:T(8,128)S(1)}, f32[80,512]{1,0:T(8,128)S(1)}, u32[]{:S(2)}, u32[]{:S(2)}) %collective-permute-start.31) | collective-permute-done | bytes 163872 | tf_op jit(solution)/shard_map/ppermute | solution.py:121
  341.3 3.9 %collective-permute-start.33 = (f32[80,512]{1,0:T(8,128)S(1)}, f32[80,512]{1,0:T(8,128)S(1)}, u32[]{:S(2)}, u32[]{:S(2)}) collective-permute-start(f32[80,512]{1,0:T(8,128)S(1)} %collective-permute-done.30), channel_id=1, source_target_pairs={{0,48},{16,64},{32,80},{48,96},{64,112},{80,0},{96,16},{112,32},{1... | collective-permute-start | bytes 491528 | tf_op jit(solution)/shard_map/ppermute | solution.py:121
  356.3 10.4 %convolution_subtract_fusion = f32[1280,640]{1,0:T(8,128)} fusion(f32[1280,512]{1,0:T(8,128)S(1)} %bitcast.124, f32[640,512]{1,0:T(8,128)S(1)} %bitcast.125, f32[160,8,5,128]{3,2,1,0:T(8,128)} %bitcast.120, f32[1280]{0:T(1024)S(1)} %copy-done.6, s32[640]{0:T(1024)S(1)} %iota_add_fusion.1, s32[1280]{0:T(1024)S(1)} %iota_add_fusion), kind=kOutput, calls=%fused_computation.16 | convolution fusion | flops 5036441600 | bytes 10498560 | tf_op jit(solution)/shard_map/dot_general | solution.py:124
  (178 shorter events, 119.5 us)
Async XLA Ops:
  16.1 112.5 %all-to-all-start = ((f32[128,1,128,128]{3,2,1,0:T(8,128)}), f32[128,1,128,128]{3,2,1,0:T(8,128)}, u32[]{:S(2)}, u32[]{:S(2)}) async-start(f32[128,1,128,128]{3,2,1,0:T(8,128)} %bitcast.117), calls=%async_computation | async-start | bytes 16777216 | tf_op jit(solution)/shard_map/all_to_all | solution.py:54
  148.1 8.8 %collective-permute-start.14 = (f32[80,512]{1,0:T(8,128)S(1)}, f32[80,512]{1,0:T(8,128)S(1)}, u32[]{:S(2)}, u32[]{:S(2)}) collective-permute-start(f32[80,512]{1,0:T(8,128)S(1)} %get-tuple-element.18), channel_id=1, source_target_pairs={{0,15},{16,31},{32,47},{48,63},{64,79},{80,95},{96,111},{112,127}} | collective-permute-start | bytes 491528 | tf_op jit(solution)/shard_map/ppermute | solution.py:96
  154.2 10.2 %collective-permute-start.11 = (f32[80,512]{1,0:T(8,128)S(1)}, f32[80,512]{1,0:T(8,128)S(1)}, u32[]{:S(2)}, u32[]{:S(2)}) collective-permute-start(f32[80,512]{1,0:T(8,128)S(1)} %get-tuple-element.21), channel_id=1, source_target_pairs={{0,12},{16,28},{32,44},{48,60},{64,76},{80,92},{96,108},{112,124}} | collective-permute-start | bytes 491528 | tf_op jit(solution)/shard_map/ppermute | solution.py:96
  155.6 10.7 %collective-permute-start.10 = (f32[80,512]{1,0:T(8,128)S(1)}, f32[80,512]{1,0:T(8,128)S(1)}, u32[]{:S(2)}, u32[]{:S(2)}) collective-permute-start(f32[80,512]{1,0:T(8,128)S(1)} %get-tuple-element.22), channel_id=1, source_target_pairs={{0,11},{16,27},{32,43},{48,59},{64,75},{80,91},{96,107},{112,123}} | collective-permute-start | bytes 491528 | tf_op jit(solution)/shard_map/ppermute | solution.py:96
  156.9 11.4 %collective-permute-start.9 = (f32[80,512]{1,0:T(8,128)S(1)}, f32[80,512]{1,0:T(8,128)S(1)}, u32[]{:S(2)}, u32[]{:S(2)}) collective-permute-start(f32[80,512]{1,0:T(8,128)S(1)} %get-tuple-element.23), channel_id=1, source_target_pairs={{0,10},{16,26},{32,42},{48,58},{64,74},{80,90},{96,106},{112,122}} | collective-permute-start | bytes 491528 | tf_op jit(solution)/shard_map/ppermute | solution.py:96
  158.2 12.0 %collective-permute-start.8 = (f32[80,512]{1,0:T(8,128)S(1)}, f32[80,512]{1,0:T(8,128)S(1)}, u32[]{:S(2)}, u32[]{:S(2)}) collective-permute-start(f32[80,512]{1,0:T(8,128)S(1)} %get-tuple-element.24), channel_id=1, source_target_pairs={{0,9},{16,25},{32,41},{48,57},{64,73},{80,89},{96,105},{112,121}} | collective-permute-start | bytes 491528 | tf_op jit(solution)/shard_map/ppermute | solution.py:96
  160.9 11.3 %collective-permute-start.7 = (f32[80,512]{1,0:T(8,128)S(1)}, f32[80,512]{1,0:T(8,128)S(1)}, u32[]{:S(2)}, u32[]{:S(2)}) collective-permute-start(f32[80,512]{1,0:T(8,128)S(1)} %get-tuple-element.25), channel_id=1, source_target_pairs={{0,8},{16,24},{32,40},{48,56},{64,72},{80,88},{96,104},{112,120}} | collective-permute-start | bytes 491528 | tf_op jit(solution)/shard_map/ppermute | solution.py:96
  164.4 9.7 %collective-permute-start.6 = (f32[80,512]{1,0:T(8,128)S(1)}, f32[80,512]{1,0:T(8,128)S(1)}, u32[]{:S(2)}, u32[]{:S(2)}) collective-permute-start(f32[80,512]{1,0:T(8,128)S(1)} %get-tuple-element.26), channel_id=1, source_target_pairs={{0,7},{16,23},{32,39},{48,55},{64,71},{80,87},{96,103},{112,119}} | collective-permute-start | bytes 491528 | tf_op jit(solution)/shard_map/ppermute | solution.py:96
  166.3 23.5 %collective-permute-start.5 = (f32[80,512]{1,0:T(8,128)S(1)}, f32[80,512]{1,0:T(8,128)}, u32[]{:S(2)}, u32[]{:S(2)}) collective-permute-start(f32[80,512]{1,0:T(8,128)S(1)} %get-tuple-element.27), channel_id=1, source_target_pairs={{0,6},{16,22},{32,38},{48,54},{64,70},{80,86},{96,102},{112,118}} | collective-permute-start | bytes 491528 | tf_op jit(solution)/shard_map/ppermute | solution.py:96
  168.3 21.6 %collective-permute-start.4 = (f32[80,512]{1,0:T(8,128)S(1)}, f32[80,512]{1,0:T(8,128)}, u32[]{:S(2)}, u32[]{:S(2)}) collective-permute-start(f32[80,512]{1,0:T(8,128)S(1)} %get-tuple-element.28), channel_id=1, source_target_pairs={{0,5},{16,21},{32,37},{48,53},{64,69},{80,85},{96,101},{112,117}} | collective-permute-start | bytes 491528 | tf_op jit(solution)/shard_map/ppermute | solution.py:96
  170.2 19.6 %collective-permute-start.3 = (f32[80,512]{1,0:T(8,128)S(1)}, f32[80,512]{1,0:T(8,128)}, u32[]{:S(2)}, u32[]{:S(2)}) collective-permute-start(f32[80,512]{1,0:T(8,128)S(1)} %get-tuple-element.29), channel_id=1, source_target_pairs={{0,4},{16,20},{32,36},{48,52},{64,68},{80,84},{96,100},{112,116}} | collective-permute-start | bytes 491528 | tf_op jit(solution)/shard_map/ppermute | solution.py:96
  172.2 17.7 %collective-permute-start.2 = (f32[80,512]{1,0:T(8,128)S(1)}, f32[80,512]{1,0:T(8,128)}, u32[]{:S(2)}, u32[]{:S(2)}) collective-permute-start(f32[80,512]{1,0:T(8,128)S(1)} %get-tuple-element.30), channel_id=1, source_target_pairs={{0,3},{16,19},{32,35},{48,51},{64,67},{80,83},{96,99},{112,115}} | collective-permute-start | bytes 491528 | tf_op jit(solution)/shard_map/ppermute | solution.py:96
  174.2 15.7 %collective-permute-start.1 = (f32[80,512]{1,0:T(8,128)S(1)}, f32[80,512]{1,0:T(8,128)}, u32[]{:S(2)}, u32[]{:S(2)}) collective-permute-start(f32[80,512]{1,0:T(8,128)S(1)} %get-tuple-element.31), channel_id=1, source_target_pairs={{0,2},{16,18},{32,34},{48,50},{64,66},{80,82},{96,98},{112,114}} | collective-permute-start | bytes 491528 | tf_op jit(solution)/shard_map/ppermute | solution.py:96
  193.2 13.2 %collective-permute-start.15 = (f32[80,512]{1,0:T(8,128)S(1)}, f32[80,512]{1,0:T(8,128)S(1)}, u32[]{:S(2)}, u32[]{:S(2)}) collective-permute-start(f32[80,512]{1,0:T(8,128)S(1)} %get-tuple-element.37), channel_id=1, source_target_pairs={{0,1},{1,2},{2,3},{3,4},{4,5},{5,6},{6,7},{7,8},{8,9},{9,10},{10,1... | collective-permute-start | bytes 491528 | tf_op jit(solution)/shard_map/ppermute | solution.py:108
  199.9 99.2 %collective-permute-start.29 = (f32[80,512]{1,0:T(8,128)S(1)}, f32[80,512]{1,0:T(8,128)S(1)}, u32[]{:S(2)}, u32[]{:S(2)}) collective-permute-start(f32[80,512]{1,0:T(8,128)S(1)} %get-tuple-element.37), channel_id=1, source_target_pairs={{0,15},{1,0},{2,1},{3,2},{4,3},{5,4},{6,5},{7,6},{8,7},{9,8},{10,9... | collective-permute-start | bytes 491528 | tf_op jit(solution)/shard_map/ppermute | solution.py:108
  204.7 93.7 %collective-permute-start.28 = (f32[80,512]{1,0:T(8,128)S(1)}, f32[80,512]{1,0:T(8,128)S(1)}, u32[]{:S(2)}, u32[]{:S(2)}) collective-permute-start(f32[80,512]{1,0:T(8,128)S(1)} %get-tuple-element.37), channel_id=1, source_target_pairs={{0,14},{1,15},{2,0},{3,1},{4,2},{5,3},{6,4},{7,5},{8,6},{9,7},{10,... | collective-permute-start | bytes 491528 | tf_op jit(solution)/shard_map/ppermute | solution.py:108
  204.7 93.0 %collective-permute-start.27 = (f32[80,512]{1,0:T(8,128)S(1)}, f32[80,512]{1,0:T(8,128)S(1)}, u32[]{:S(2)}, u32[]{:S(2)}) collective-permute-start(f32[80,512]{1,0:T(8,128)S(1)} %get-tuple-element.37), channel_id=1, source_target_pairs={{0,13},{1,14},{2,15},{3,0},{4,1},{5,2},{6,3},{7,4},{8,5},{9,6},{10... | collective-permute-start | bytes 491528 | tf_op jit(solution)/shard_map/ppermute | solution.py:108
  204.7 92.4 %collective-permute-start.26 = (f32[80,512]{1,0:T(8,128)S(1)}, f32[80,512]{1,0:T(8,128)S(1)}, u32[]{:S(2)}, u32[]{:S(2)}) collective-permute-start(f32[80,512]{1,0:T(8,128)S(1)} %get-tuple-element.37), channel_id=1, source_target_pairs={{0,12},{1,13},{2,14},{3,15},{4,0},{5,1},{6,2},{7,3},{8,4},{9,5},{1... | collective-permute-start | bytes 491528 | tf_op jit(solution)/shard_map/ppermute | solution.py:108
  235.8 8.8 %collective-permute-start.20 = (f32[80,512]{1,0:T(8,128)S(1)}, f32[80,512]{1,0:T(8,128)S(1)}, u32[]{:S(2)}, u32[]{:S(2)}) collective-permute-start(f32[80,512]{1,0:T(8,128)S(1)} %get-tuple-element.37), channel_id=1, source_target_pairs={{0,6},{1,7},{2,8},{3,9},{4,10},{5,11},{6,12},{7,13},{8,14},{9,15},... | collective-permute-start | bytes 491528 | tf_op jit(solution)/shard_map/ppermute | solution.py:108
  276.5 32.8 %collective-permute-start.30 = (f32[80,512]{1,0:T(8,128)S(1)}, f32[80,512]{1,0:T(8,128)S(1)}, u32[]{:S(2)}, u32[]{:S(2)}) collective-permute-start(f32[80,512]{1,0:T(8,128)S(1)} %get-tuple-element.37), channel_id=1, source_target_pairs={{0,0},{1,16},{2,32},{3,48},{4,64},{5,80},{6,96},{7,112},{8,1},{9,1... | collective-permute-start | bytes 491528 | tf_op jit(solution)/shard_map/ppermute | solution.py:117
  309.2 42.7 %collective-permute-start.37 = (f32[80,512]{1,0:T(8,128)S(1)}, f32[80,512]{1,0:T(8,128)S(1)}, u32[]{:S(2)}, u32[]{:S(2)}) collective-permute-start(f32[80,512]{1,0:T(8,128)S(1)} %collective-permute-done.30), channel_id=1, source_target_pairs={{0,112},{16,0},{32,16},{48,32},{64,48},{80,64},{96,80},{112,96},{1... | collective-permute-start | bytes 491528 | tf_op jit(solution)/shard_map/ppermute | solution.py:121
  316.2 35.0 %collective-permute-start.36 = (f32[80,512]{1,0:T(8,128)S(1)}, f32[80,512]{1,0:T(8,128)S(1)}, u32[]{:S(2)}, u32[]{:S(2)}) collective-permute-start(f32[80,512]{1,0:T(8,128)S(1)} %collective-permute-done.30), channel_id=1, source_target_pairs={{0,96},{16,112},{32,0},{48,16},{64,32},{80,48},{96,64},{112,80},{1... | collective-permute-start | bytes 491528 | tf_op jit(solution)/shard_map/ppermute | solution.py:121
  325.1 25.4 %collective-permute-start.35 = (f32[80,512]{1,0:T(8,128)S(1)}, f32[80,512]{1,0:T(8,128)S(1)}, u32[]{:S(2)}, u32[]{:S(2)}) collective-permute-start(f32[80,512]{1,0:T(8,128)S(1)} %collective-permute-done.30), channel_id=1, source_target_pairs={{0,80},{16,96},{32,112},{48,0},{64,16},{80,32},{96,48},{112,64},{1... | collective-permute-start | bytes 491528 | tf_op jit(solution)/shard_map/ppermute | solution.py:121
  328.6 21.3 %collective-permute-start.34 = (f32[80,512]{1,0:T(8,128)S(1)}, f32[80,512]{1,0:T(8,128)S(1)}, u32[]{:S(2)}, u32[]{:S(2)}) collective-permute-start(f32[80,512]{1,0:T(8,128)S(1)} %collective-permute-done.30), channel_id=1, source_target_pairs={{0,64},{16,80},{32,96},{48,112},{64,0},{80,16},{96,32},{112,48},{1... | collective-permute-start | bytes 491528 | tf_op jit(solution)/shard_map/ppermute | solution.py:121
  (26 other events, 404.8 us)

commit v10 on v7

--- a/solution.py
+++ b/solution.py
@@ -51,18 +51,28 @@
     outgoing = jnp.take(local_tiles, slot_tile.reshape(-1), axis=0, mode="clip").reshape(
         devices_all, 1, BLK, BLK
     )
+    panel_blocks = PANEL // BLK
+    is_panel = col_parent < panel_blocks
+    panel_l = jnp.argmax(is_panel).astype(jnp.int32)
+    panel_tile = jnp.where(
+        jnp.any(is_panel), inv_k * col_items + panel_l, row_items * col_items
+    )
+    panel_out = jnp.take(local_tiles, panel_tile, axis=0, mode="clip")
+    panel_in = lax.all_to_all(panel_out, "row", split_axis=0, concat_axis=0, tiled=True)
     incoming = lax.all_to_all(
         outgoing, ("row", "col"), split_axis=0, concat_axis=0, tiled=True
     ).reshape(devices_all, BLK, BLK)
     my_rows = row_index * front_rows + jnp.arange(front_rows, dtype=jnp.int32)
     my_cols = col_index * front_cols + jnp.arange(front_cols, dtype=jnp.int32)
     sources = []
+    inverses = []
     for child_id in range(2):
         inverse = (
             jnp.full((front_blocks,), -1, jnp.int32)
             .at[block_map[child_id]]
             .set(jnp.arange(block_map.shape[1], dtype=jnp.int32))
         )
+        inverses.append(inverse)
         a = jnp.take(inverse, my_rows)
         b = jnp.take(inverse, my_cols)
         source = (jnp.maximum(b, 0) // col_items)[None, :] * col_count + (
@@ -87,23 +97,33 @@
     row_global = row_index * height + jnp.arange(height, dtype=jnp.int32)
     col_global = col_index * col_width + jnp.arange(col_width, dtype=jnp.int32)
     diag = jnp.where(row_global[:, None] == col_global[None, :], own_diag[:, None], 0.0)
-    raw_panel = assemble(PANEL // BLK) + diag[:, :PANEL]
-    front_local = assemble(front_cols) + diag
-    piece_rows = height // col_count
-    piece_rows = height // col_count
-    piece = jnp.where(col_index == 0, raw_panel[:piece_rows], 0.0)
-    for k in range(1, col_count):
-        pairs = [(r * col_count, r * col_count + k) for r in range(row_count)]
-        piece = piece + lax.ppermute(
-            raw_panel[k * piece_rows:(k + 1) * piece_rows], ("row", "col"), pairs
-        )
-    factor_piece = jnp.dot(
-        piece,
+    my_inverse = jnp.where(child == 0, inverses[0], inverses[1])
+    panel_b = my_inverse[:panel_blocks]
+    panel_src = jnp.where(panel_b >= 0, panel_b // col_items, row_count)
+    panel_part = (
+        jnp.take(panel_in, panel_src, axis=0, mode="fill", fill_value=0.0)
+        .transpose(1, 0, 2)
+        .reshape(BLK, PANEL)
+    )
+    panel_parts = lax.all_gather(panel_part, "col", axis=0, tiled=False)
+    raw_panel = None
+    for c in range(2):
+        a = jnp.take(inverses[c], my_rows)
+        holder = jnp.where(a >= 0, c * half_cols + a // row_items, col_count)
+        part = jnp.take(panel_parts, holder, axis=0, mode="fill", fill_value=0.0)
+        raw_panel = part if raw_panel is None else raw_panel + part
+    raw_panel = raw_panel.reshape(height, PANEL) + jnp.where(
+        row_global[:, None] == jnp.arange(PANEL, dtype=jnp.int32)[None, :], own_diag[:, None], 0.0
+    )
+    factor_panel = jnp.dot(
+        raw_panel,
         panel_inverse.T,
         precision=lax.Precision.HIGHEST,
         preferred_element_type=jnp.float32,
     )
-    factor_panel = lax.all_gather(factor_piece, "col", axis=0, tiled=True)
+    front_local = assemble(front_cols) + diag
+    piece_rows = height // col_count
+    factor_piece = lax.dynamic_slice_in_dim(factor_panel, col_index * piece_rows, piece_rows, 0)
     ratio = col_count // row_count
     pairs = [
         (r * col_count + k, (k % row_count) * col_count + r * ratio + k // row_count)

time: 268 us -> 255 us (0.951)
  starting transfers between devices: 55.7 us -> 26 us
  waiting for transfers between devices: 116 us -> 127 us
  local copies, waits for them, and re-layouts: 53.2 us -> 62.2 us
  other arithmetic: 11.6 us -> 8.89 us
    ppermute x15 -> x0, starting transfers between devices: 26 us -> none  [on_device(): lax.ppermute(raw_panel[k * piece_rows:(k + 1) * piece_rows], ('row', 'col...]
    all_to_all x1, waiting for transfers between devices: 93.6 us -> 114 us  [on_device(): lax.all_to_all(outgoing, ('row', 'col'), split_axis=0, concat_axis=0, til...]
    gather x2 -> x6, local copies, waits for them, and re-layouts: 1.32 us -> 14.4 us  [the longest x2 8.89 us: on_device(): part = jnp.take(panel_parts, holder, axis=0, mode='fill', fill_value=0.0)]
    ppermute x15 -> x0, waiting for transfers between devices: 12.8 us -> none  [on_device(): lax.ppermute(raw_panel[k * piece_rows:(k + 1) * piece_rows], ('row', 'col...]
    gather x4 -> x2, local copies, waits for them, and re-layouts: 22.9 us -> 11.7 us  [assemble(): jnp.take(incoming, source[:, :width].reshape(-1), axis=0, mode='fill', fi...]
    ppermute x7, starting transfers between devices: 15.6 us -> 8.28 us  [on_device(): stack.append(lax.ppermute(moved, 'row', shift))]
    all_to_all x0 -> x1, starting transfers between devices: none -> 6.8 us  [on_device(): lax.all_to_all(panel_out, 'row', split_axis=0, concat_axis=0, tiled=True)]
    add x2 -> x1, other arithmetic: 6.3 us -> 0.46 us  [assemble(): total = part if total is None else total + part]
  transfers between devices with their start and end apart: 25 -> 11, of which waited for: 12 -> 6; matrix products, arithmetic and copies ran while one was open for 11% -> 14% of each run, Pallas kernels for 0% -> 0%
where the time goes in v10:
time: 255 us; the launch traced here: 253 us
  waiting for transfers between devices  127 us (50%)
  local copies, waits for them, and re-layouts  62.2 us (24%)
  starting transfers between devices  26 us (10%)
  matrix products  14.9 us (6%)
  between operations  14.5 us (6%)
  other arithmetic  8.89 us (3%)
    all_to_all x1, waiting for transfers between devices, on_device(): lax.all_to_all(outgoing, ('row', 'col'), split_axis=0, concat_axis=0, til...  114 us
    gather x2, local copies, waits for them, and re-layouts, assemble(): jnp.take(incoming, source[:, :width].reshape(-1), axis=0, mode='fill', fi...  11.7 us
    dot_general x1, matrix products, on_device(): lax.dot_general(factor_panel, across, (((1,), (1,)), ((), ())), precision...  10.4 us
    unnamed x22, local copies, waits for them, and re-layouts  9.54 us
    gather x2, local copies, waits for them, and re-layouts, on_device(): part = jnp.take(panel_parts, holder, axis=0, mode='fill', fill_value=0.0)  8.89 us
    all_to_all x1, starting transfers between devices, on_device(): lax.all_to_all(outgoing, ('row', 'col'), split_axis=0, concat_axis=0, til...  8.76 us
    ppermute x7, starting transfers between devices, on_device(): stack.append(lax.ppermute(moved, 'row', shift))  8.28 us
    ppermute x7, waiting for transfers between devices, on_device(): stack.append(lax.ppermute(moved, 'row', shift))  7.47 us
  transfers between devices with their start and end apart: 11, of which 6 were waited for; matrix products, arithmetic and copies ran while one was open for 14% of the time, Pallas kernels for 0%

profile of v10, /device:TPU:1, one launch (start us, length us, event | category | flops | bytes accessed | tf_op | source)
XLA Modules:
  0.0 253.5 jit_solution(4501481509756228365)
XLA Ops:
  9.4 3.2 %copy.17 = f32[128,8,8,128]{3,2,1,0:T(8,128)S(1)} copy(f32[128,8,8,128]{3,1,2,0:T(8,128)} %bitcast.81) | data formatting | bytes 8388608
  12.9 2.7 %copy.12 = f32[8,8,128,128]{3,2,1,0:T(8,128)} copy(f32[8,8,128,128]{3,1,2,0:T(8,128)S(1)} %bitcast_bitcast_fusion) | data formatting | bytes 8388608 | tf_op jit(solution)/shard_map/transpose | solution.py:44
  18.4 4.7 %concatenate.3 = f32[65,128,128]{2,1,0:T(8,128)} pad(f32[64,128,128]{2,1,0:T(8,128)} %bitcast.77, f32[]{:T(128)} %constant.224.clone.1), padding=0_1x0_0x0_0 | pad | bytes 8454148 | tf_op jit(solution)/shard_map/concatenate | solution.py:50
  23.1 3.6 %gather_fusion = f32[8,128,128]{2,1,0:T(8,128)} fusion(f32[65,128,128]{2,1,0:T(8,128)} %concatenate.3, s32[1024]{0:T(1024)S(1)} %get-tuple-element.38), kind=kCustom, calls=%fused_computation.8 | custom fusion | bytes 1048608 | tf_op jit(solution)/shard_map/jit(_take)/gather | solution.py:60
  26.7 6.8 %all-to-all-start = ((f32[8,128,128]{2,1,0:T(8,128)}), f32[8,128,128]{2,1,0:T(8,128)S(1)}, u32[]{:S(2)}, u32[]{:S(2)}) async-start(f32[8,128,128]{2,1,0:T(8,128)} %gather_fusion), calls=%async_computation | async-start | bytes 1048576 | tf_op jit(solution)/shard_map/all_to_all | solution.py:61
  33.5 6.5 %gather_fusion.2 = f32[128,128,128]{2,1,0:T(8,128)} fusion(f32[65,128,128]{2,1,0:T(8,128)} %concatenate.3, s32[1024]{0:T(1024)S(1)} %get-tuple-element.37), kind=kCustom, calls=%fused_computation.10 | custom fusion | bytes 16777728 | tf_op jit(solution)/shard_map/jit(_take)/gather | solution.py:51
  42.8 8.8 %all-to-all-start.1 = ((f32[128,1,128,128]{3,2,1,0:T(8,128)}), f32[128,1,128,128]{3,2,1,0:T(8,128)}, u32[]{:S(2)}, u32[]{:S(2)}) async-start(f32[128,1,128,128]{3,2,1,0:T(8,128)} %bitcast.76), calls=%async_computation.1 | async-start | bytes 16777216 | tf_op jit(solution)/shard_map/all_to_all | solution.py:62
  57.0 113.9 %all-to-all-done.1 = f32[128,1,128,128]{3,2,1,0:T(8,128)} async-done(((f32[128,1,128,128]{3,2,1,0:T(8,128)}), f32[128,1,128,128]{3,2,1,0:T(8,128)}, u32[]{:S(2)}, u32[]{:S(2)}) %all-to-all-start.1) | async-done | bytes 8388640 | tf_op jit(solution)/shard_map/all_to_all | solution.py:62
  170.9 5.8 %gather_fusion.11 = f32[50,128,128]{2,1,0:T(8,128)} fusion(f32[128,128,128]{2,1,0:T(8,128)} %bitcast.16, s32[1024]{0:T(1024)S(1)} %pad_clamp_fusion.1), kind=kCustom, calls=%fused_computation.7.clone | custom fusion | bytes 6553800 | tf_op jit(solution)/shard_map/jit(_take)/gather | solution.py:87
  176.8 5.9 %gather_fusion.9 = f32[50,128,128]{2,1,0:T(8,128)} fusion(f32[128,128,128]{2,1,0:T(8,128)} %bitcast.16, s32[1024]{0:T(1024)S(1)} %pad_clamp_fusion.2), kind=kCustom, calls=%fused_computation.3.clone | custom fusion | bytes 6553800 | tf_op jit(solution)/shard_map/jit(_take)/gather | solution.py:87
  182.7 4.4 %gather_fusion.7 = f32[10,128,512]{2,1,0:T(8,128)} fusion(f32[16,128,512]{2,1,0:T(8,128)} %all-gather.2.cloned.1.call-done, s32[1024]{0:T(1024)S(1)} %get-tuple-element.39), kind=kCustom, calls=%fused_computation.5.clone | custom fusion | bytes 5242920 | tf_op jit(solution)/shard_map/jit(_take)/gather | solution.py:113
  187.1 4.5 %gather_fusion.5 = f32[10,128,512]{2,1,0:T(8,128)} fusion(f32[16,128,512]{2,1,0:T(8,128)} %all-gather.2.cloned.1.call-done, s32[1024]{0:T(1024)S(1)} %get-tuple-element.40), kind=kCustom, calls=%fused_computation.1.clone | custom fusion | bytes 5242920 | tf_op jit(solution)/shard_map/jit(_take)/gather | solution.py:113
  191.6 3.2 %select_add_fusion.1 = f32[10,128,512]{2,1,0:T(8,128)S(1)} fusion(f32[10,128,512]{2,1,0:T(8,128)} %gather_fusion.7, f32[10,128,512]{2,1,0:T(8,128)} %gather_fusion.5, pred[10]{0:T(512)(128)(4,1)S(1)} %get-tuple-element.21, pred[10]{0:T(512)(128)(4,1)S(1)} %get-tuple-element.19), kind=kLoop, calls=%fused_computation.21 | loop fusion | flops 1966080 | bytes 7864340 | tf_op jit(solution)/shard_map/add | solution.py:114
  195.8 4.5 %fusion.16 = f32[1280,512]{1,0:T(8,128)S(1)} fusion(f32[1280,512]{1,0:T(8,128)S(1)} %bitcast_add_fusion.1, f32[512,512]{1,0:T(8,128)S(1)} %copy-done), kind=kOutput, calls=%fused_computation.129 | convolution fusion | flops 4026531840 | bytes 6291456 | tf_op jit(solution)/shard_map/dot_general | solution.py:118
  200.3 1.9 collective-permute-start
  202.7 4.2 %copy.16 = f32[10,128,5,128]{3,2,1,0:T(8,128)} copy(f32[10,128,5,128]{3,1,2,0:T(8,128)S(1)} %bitcast.80) | data formatting | bytes 6553600 | tf_op jit(solution)/shard_map/transpose | solution.py:93
  206.9 4.4 %collective-permute-done = f32[80,512]{1,0:T(8,128)S(1)} collective-permute-done((f32[80,512]{1,0:T(8,128)S(1)}, f32[80,512]{1,0:T(8,128)S(1)}, u32[]{:S(2)}, u32[]{:S(2)}) %collective-permute-start) | collective-permute-done | bytes 163872 | tf_op jit(solution)/shard_map/ppermute | solution.py:133
  211.3 2.9 %collective-permute-start.1 = (f32[80,512]{1,0:T(8,128)S(1)}, f32[80,512]{1,0:T(8,128)S(1)}, u32[]{:S(2)}, u32[]{:S(2)}) collective-permute-start(f32[80,512]{1,0:T(8,128)S(1)} %collective-permute-done), channel_id=1, source_target_pairs={{0,16},{16,32},{32,48},{48,64},{64,80},{80,96},{96,112},{112,0},{1... | collective-permute-start | bytes 491528 | tf_op jit(solution)/shard_map/ppermute | solution.py:137
  215.7 1.8 collective-permute-start.4
  222.6 2.1 collective-permute-done.3
  225.4 4.4 %collective-permute-done.4 = f32[80,512]{1,0:T(8,128)S(1)} collective-permute-done((f32[80,512]{1,0:T(8,128)S(1)}, f32[80,512]{1,0:T(8,128)S(1)}, u32[]{:S(2)}, u32[]{:S(2)}) %collective-permute-start.4) | collective-permute-done | bytes 163872 | tf_op jit(solution)/shard_map/ppermute | solution.py:137
  232.5 1.9 gather_fusion.3
  234.7 1.6 copy-done.4
  236.2 10.4 %convolution_subtract_fusion = f32[1280,640]{1,0:T(8,128)} fusion(f32[1280,512]{1,0:T(8,128)S(1)} %copy-done.4, f32[640,512]{1,0:T(8,128)S(1)} %bitcast_select_fusion, f32[160,8,5,128]{3,2,1,0:T(8,128)} %bitcast.79, f32[1280]{0:T(1024)S(1)} %copy-done.5, s32[640]{0:T(1024)S(1)} %iota_add_fusion.1, s32[1280]{0:T(1024)S(1)} %iota_add_fusion), kind=kOutput, calls=%fused_computation.17 | convolution fusion | flops 5036441600 | bytes 10498560 | tf_op jit(solution)/shard_map/dot_general | solution.py:140
  (97 shorter events, 24.6 us)
Async XLA Ops:
  7.2 188.6 %copy-start = (f32[512,512]{1,0:T(8,128)S(1)}, f32[512,512]{1,0:T(8,128)}, u32[]{:S(2)}) copy-start(f32[512,512]{1,0:T(8,128)} %param.15) | copy-start | bytes 3145732
  26.7 16.2 %all-to-all-start = ((f32[8,128,128]{2,1,0:T(8,128)}), f32[8,128,128]{2,1,0:T(8,128)S(1)}, u32[]{:S(2)}, u32[]{:S(2)}) async-start(f32[8,128,128]{2,1,0:T(8,128)} %gather_fusion), calls=%async_computation | async-start | bytes 1048576 | tf_op jit(solution)/shard_map/all_to_all | solution.py:61
  33.5 6.5 %copy-start.6 = (s32[2,64]{1,0:T(2,128)S(1)}, s32[2,64]{1,0:T(2,128)}, u32[]{:S(2)}) copy-start(s32[2,64]{1,0:T(2,128)} %param.13) | copy-start | bytes 1540
  42.8 128.1 %all-to-all-start.1 = ((f32[128,1,128,128]{3,2,1,0:T(8,128)}), f32[128,1,128,128]{3,2,1,0:T(8,128)}, u32[]{:S(2)}, u32[]{:S(2)}) async-start(f32[128,1,128,128]{3,2,1,0:T(8,128)} %bitcast.76), calls=%async_computation.1 | async-start | bytes 16777216 | tf_op jit(solution)/shard_map/all_to_all | solution.py:62
  51.6 131.1 %all-gather.2.cloned.1.call-start = ((), (), s32[]{:S(2)}) async-start(), calls=%async_computation.2 | async-start | bytes 4456448 | tf_op jit(solution)/shard_map/all_gather | solution.py:108
  191.6 3.3 %copy-start.5 = (f32[1280]{0:T(1024)S(1)}, f32[1280]{0:T(1024)}, u32[]{:S(2)}) copy-start(f32[1280]{0:T(1024)} %param.14) | copy-start | bytes 15364
  195.7 6.5 %copy-start.1 = (f32[50,128,128]{2,1,0:T(8,128)S(1)}, f32[50,128,128]{2,1,0:T(8,128)}, u32[]{:S(2)}) copy-start(f32[50,128,128]{2,1,0:T(8,128)} %gather_fusion.11) | copy-start | bytes 9830404
  195.7 6.5 %copy-start.2 = (f32[50,128,128]{2,1,0:T(8,128)S(1)}, f32[50,128,128]{2,1,0:T(8,128)}, u32[]{:S(2)}) copy-start(f32[50,128,128]{2,1,0:T(8,128)} %gather_fusion.9) | copy-start | bytes 9830404
  200.2 2.0 copy-start.3
  200.3 11.1 %collective-permute-start = (f32[80,512]{1,0:T(8,128)S(1)}, f32[80,512]{1,0:T(8,128)S(1)}, u32[]{:S(2)}, u32[]{:S(2)}) collective-permute-start(f32[80,512]{1,0:T(8,128)S(1)} %constant_dynamic-slice_fusion.3), channel_id=1, source_target_pairs={{0,0},{1,16},{2,32},{3,48},{4,64},{5,80},{6,96},{7,112},{8,1},{9,1... | collective-permute-start | bytes 491528 | tf_op jit(solution)/shard_map/ppermute | solution.py:133
  211.3 7.4 %collective-permute-start.1 = (f32[80,512]{1,0:T(8,128)S(1)}, f32[80,512]{1,0:T(8,128)S(1)}, u32[]{:S(2)}, u32[]{:S(2)}) collective-permute-start(f32[80,512]{1,0:T(8,128)S(1)} %collective-permute-done), channel_id=1, source_target_pairs={{0,16},{16,32},{32,48},{48,64},{64,80},{80,96},{96,112},{112,0},{1... | collective-permute-start | bytes 491528 | tf_op jit(solution)/shard_map/ppermute | solution.py:137
  214.3 6.9 %collective-permute-start.2 = (f32[80,512]{1,0:T(8,128)S(1)}, f32[80,512]{1,0:T(8,128)S(1)}, u32[]{:S(2)}, u32[]{:S(2)}) collective-permute-start(f32[80,512]{1,0:T(8,128)S(1)} %collective-permute-done), channel_id=1, source_target_pairs={{0,32},{16,48},{32,64},{48,80},{64,96},{80,112},{96,0},{112,16},{1... | collective-permute-start | bytes 491528 | tf_op jit(solution)/shard_map/ppermute | solution.py:137
  214.3 10.5 %collective-permute-start.3 = (f32[80,512]{1,0:T(8,128)S(1)}, f32[80,512]{1,0:T(8,128)S(1)}, u32[]{:S(2)}, u32[]{:S(2)}) collective-permute-start(f32[80,512]{1,0:T(8,128)S(1)} %collective-permute-done), channel_id=1, source_target_pairs={{0,48},{16,64},{32,80},{48,96},{64,112},{80,0},{96,16},{112,32},{1... | collective-permute-start | bytes 491528 | tf_op jit(solution)/shard_map/ppermute | solution.py:137
  215.7 14.1 %collective-permute-start.4 = (f32[80,512]{1,0:T(8,128)S(1)}, f32[80,512]{1,0:T(8,128)S(1)}, u32[]{:S(2)}, u32[]{:S(2)}) collective-permute-start(f32[80,512]{1,0:T(8,128)S(1)} %collective-permute-done), channel_id=1, source_target_pairs={{0,64},{16,80},{32,96},{48,112},{64,0},{80,16},{96,32},{112,48},{1... | collective-permute-start | bytes 491528 | tf_op jit(solution)/shard_map/ppermute | solution.py:137
  217.5 13.0 %collective-permute-start.5 = (f32[80,512]{1,0:T(8,128)S(1)}, f32[80,512]{1,0:T(8,128)S(1)}, u32[]{:S(2)}, u32[]{:S(2)}) collective-permute-start(f32[80,512]{1,0:T(8,128)S(1)} %collective-permute-done), channel_id=1, source_target_pairs={{0,80},{16,96},{32,112},{48,0},{64,16},{80,32},{96,48},{112,64},{1... | collective-permute-start | bytes 491528 | tf_op jit(solution)/shard_map/ppermute | solution.py:137
  218.7 12.5 %collective-permute-start.6 = (f32[80,512]{1,0:T(8,128)S(1)}, f32[80,512]{1,0:T(8,128)S(1)}, u32[]{:S(2)}, u32[]{:S(2)}) collective-permute-start(f32[80,512]{1,0:T(8,128)S(1)} %collective-permute-done), channel_id=1, source_target_pairs={{0,96},{16,112},{32,0},{48,16},{64,32},{80,48},{96,64},{112,80},{1... | collective-permute-start | bytes 491528 | tf_op jit(solution)/shard_map/ppermute | solution.py:137
  221.2 10.6 %collective-permute-start.7 = (f32[80,512]{1,0:T(8,128)S(1)}, f32[80,512]{1,0:T(8,128)S(1)}, u32[]{:S(2)}, u32[]{:S(2)}) collective-permute-start(f32[80,512]{1,0:T(8,128)S(1)} %collective-permute-done), channel_id=1, source_target_pairs={{0,112},{16,0},{32,16},{48,32},{64,48},{80,64},{96,80},{112,96},{1... | collective-permute-start | bytes 491528 | tf_op jit(solution)/shard_map/ppermute | solution.py:137
  234.5 1.7 copy-start.4
Sparse Core Ops, SparseCore 0:
  55.1 112.5 all-gather.1

commit v11 on v10

--- a/solution.py
+++ b/solution.py
@@ -106,12 +106,35 @@
         .reshape(BLK, PANEL)
     )
     panel_parts = lax.all_gather(panel_part, "col", axis=0, tiled=False)
+    piece_rows = height // col_count
+    first_row = col_index * piece_rows
+    first_block = first_row // BLK
     raw_panel = None
+    piece_pair = None
     for c in range(2):
         a = jnp.take(inverses[c], my_rows)
         holder = jnp.where(a >= 0, c * half_cols + a // row_items, col_count)
+        pair_holder = jnp.take(
+            holder, first_block + jnp.arange(2, dtype=jnp.int32), mode="fill", fill_value=col_count
+        )
+        pair = jnp.take(panel_parts, pair_holder, axis=0, mode="fill", fill_value=0.0)
+        piece_pair = pair if piece_pair is None else piece_pair + pair
         part = jnp.take(panel_parts, holder, axis=0, mode="fill", fill_value=0.0)
         raw_panel = part if raw_panel is None else raw_panel + part
+    piece_rows_global = row_index * height + first_row + jnp.arange(piece_rows, dtype=jnp.int32)
+    raw_piece = lax.dynamic_slice_in_dim(
+        piece_pair.reshape(2 * BLK, PANEL), first_row % BLK, piece_rows, 0
+    ) + jnp.where(
+        piece_rows_global[:, None] == jnp.arange(PANEL, dtype=jnp.int32)[None, :],
+        lax.dynamic_slice_in_dim(own_diag, first_row, piece_rows)[:, None],
+        0.0,
+    )
+    factor_piece = jnp.dot(
+        raw_piece,
+        panel_inverse.T,
+        precision=lax.Precision.HIGHEST,
+        preferred_element_type=jnp.float32,
+    )
     raw_panel = raw_panel.reshape(height, PANEL) + jnp.where(
         row_global[:, None] == jnp.arange(PANEL, dtype=jnp.int32)[None, :], own_diag[:, None], 0.0
     )
@@ -121,9 +144,8 @@
         precision=lax.Precision.HIGHEST,
         preferred_element_type=jnp.float32,
     )
+    incoming, factor_piece = lax.optimization_barrier((incoming, factor_piece))
     front_local = assemble(front_cols) + diag
-    piece_rows = height // col_count
-    factor_piece = lax.dynamic_slice_in_dim(factor_panel, col_index * piece_rows, piece_rows, 0)
     ratio = col_count // row_count
     pairs = [
         (r * col_count + k, (k % row_count) * col_count + r * ratio + k // row_count)

time: 255 us -> 273 us (1.071)
  waiting for transfers between devices: 127 us -> 132 us
  starting transfers between devices: 26 us -> 30.4 us
  local copies, waits for them, and re-layouts: 62.2 us -> 65.7 us
    all_to_all x1, waiting for transfers between devices: 114 us -> 0.01 us  [on_device(): lax.all_to_all(outgoing, ('row', 'col'), split_axis=0, concat_axis=0, til...]
    all_gather x1, waiting for transfers between devices: 0.01 us -> 112 us  [on_device(): panel_parts = lax.all_gather(panel_part, 'col', axis=0, tiled=False)]
    gather x0 -> x4, local copies, waits for them, and re-layouts: none -> 6.81 us  [the longest x2 5.53 us: on_device(): jnp.take(panel_parts, pair_holder, axis=0, mode='fill', fill_value=0.0)]
    all_to_all x1, waiting for transfers between devices: 1.2 us -> 7.7 us  [on_device(): lax.all_to_all(panel_out, 'row', split_axis=0, concat_axis=0, tiled=True)]
    ppermute x7, waiting for transfers between devices: 7.47 us -> 12.5 us  [on_device(): stack.append(lax.ppermute(moved, 'row', shift))]
    ppermute x7, starting transfers between devices: 8.28 us -> 12.9 us  [on_device(): stack.append(lax.ppermute(moved, 'row', shift))]
    ppermute x1, waiting for transfers between devices: 4.4 us -> 0.01 us  [on_device(): moved = lax.ppermute(factor_piece, ('row', 'col'), pairs)]
    unnamed x22 -> x20, local copies, waits for them, and re-layouts: 9.54 us -> 10.6 us
  transfers between devices with their start and end apart: 11 -> 11, of which waited for: 6 -> 5; matrix products, arithmetic and copies ran while one was open for 14% -> 22% of each run, Pallas kernels for 0% -> 0%
where the time goes in v11:
time: 273 us; the launch traced here: 269 us
  waiting for transfers between devices  132 us (48%)
  local copies, waits for them, and re-layouts  65.7 us (24%)
  starting transfers between devices  30.4 us (11%)
  matrix products  17.4 us (6%)
  between operations  14.6 us (5%)
  other arithmetic  9.25 us (3%)
    all_gather x1, waiting for transfers between devices, on_device(): panel_parts = lax.all_gather(panel_part, 'col', axis=0, tiled=False)  112 us
    ppermute x7, starting transfers between devices, on_device(): stack.append(lax.ppermute(moved, 'row', shift))  12.9 us
    ppermute x7, waiting for transfers between devices, on_device(): stack.append(lax.ppermute(moved, 'row', shift))  12.5 us
    gather x2, local copies, waits for them, and re-layouts, assemble(): jnp.take(incoming, source[:, :width].reshape(-1), axis=0, mode='fill', fi...  11.7 us
    unnamed x20, local copies, waits for them, and re-layouts  10.6 us
    dot_general x1, matrix products, on_device(): lax.dot_general(factor_panel, across, (((1,), (1,)), ((), ())), precision...  10.4 us
    gather x2, local copies, waits for them, and re-layouts, on_device(): part = jnp.take(panel_parts, holder, axis=0, mode='fill', fill_value=0.0)  8.89 us
    all_to_all x1, starting transfers between devices, on_device(): lax.all_to_all(outgoing, ('row', 'col'), split_axis=0, concat_axis=0, til...  8.55 us
  transfers between devices with their start and end apart: 11, of which 5 were waited for; matrix products, arithmetic and copies ran while one was open for 22% of the time, Pallas kernels for 0%

profile of v11, /device:TPU:1, one launch (start us, length us, event | category | flops | bytes accessed | tf_op | source)
XLA Modules:
  0.0 269.3 jit_solution(17816381960642489844)
XLA Ops:
  12.2 3.2 %copy.18 = f32[128,8,8,128]{3,2,1,0:T(8,128)S(1)} copy(f32[128,8,8,128]{3,1,2,0:T(8,128)} %bitcast.87) | data formatting | bytes 8388608
  16.5 2.3 concatenate.3
  18.8 3.6 %gather_fusion = f32[8,128,128]{2,1,0:T(8,128)} fusion(f32[65,128,128]{2,1,0:T(8,128)} %concatenate.3, s32[1024]{0:T(1024)S(1)} %get-tuple-element.52), kind=kCustom, calls=%fused_computation.12 | custom fusion | bytes 1048608 | tf_op jit(solution)/shard_map/jit(_take)/gather | solution.py:60
  22.3 6.8 %all-to-all-start = ((f32[8,128,128]{2,1,0:T(8,128)}), f32[8,128,128]{2,1,0:T(8,128)S(1)}, u32[]{:S(2)}, u32[]{:S(2)}) async-start(f32[8,128,128]{2,1,0:T(8,128)} %gather_fusion), calls=%async_computation | async-start | bytes 1048576 | tf_op jit(solution)/shard_map/all_to_all | solution.py:61
  30.8 7.7 %all-to-all-done = f32[8,128,128]{2,1,0:T(8,128)S(1)} async-done(((f32[8,128,128]{2,1,0:T(8,128)}), f32[8,128,128]{2,1,0:T(8,128)S(1)}, u32[]{:S(2)}, u32[]{:S(2)}) %all-to-all-start) | async-done | bytes 524320 | tf_op jit(solution)/shard_map/all_to_all | solution.py:61
  40.2 6.5 %gather_fusion.2 = f32[128,128,128]{2,1,0:T(8,128)} fusion(f32[65,128,128]{2,1,0:T(8,128)} %concatenate.3, s32[1024]{0:T(1024)S(1)} %get-tuple-element.51), kind=kCustom, calls=%fused_computation.14 | custom fusion | bytes 16777728 | tf_op jit(solution)/shard_map/jit(_take)/gather | solution.py:51
  46.7 8.6 %all-to-all-start.1 = ((f32[128,1,128,128]{3,2,1,0:T(8,128)}), f32[128,1,128,128]{3,2,1,0:T(8,128)}, u32[]{:S(2)}, u32[]{:S(2)}) async-start(f32[128,1,128,128]{3,2,1,0:T(8,128)} %bitcast.82), calls=%async_computation.1 | async-start | bytes 16777216 | tf_op jit(solution)/shard_map/all_to_all | solution.py:62
  60.2 111.8 %all-gather.2.cloned.1.call-done = f32[16,128,512]{2,1,0:T(8,128)} async-done(((f32[1,128,512]{2,1,0:T(8,128)}), f32[16,128,512]{2,1,0:T(8,128)}) %all-gather.2.cloned.1.call-update) | async-done | bytes 4194320 | tf_op jit(solution)/shard_map/all_gather | solution.py:108
  172.0 2.8 %gather_fusion.11 = f32[2,128,512]{2,1,0:T(8,128)S(1)} fusion(f32[16,128,512]{2,1,0:T(8,128)} %all-gather.2.cloned.1.call-done, s32[1024]{0:T(1024)S(1)} %pad_clamp_fusion.3), kind=kCustom, calls=%fused_computation.9.clone | custom fusion | bytes 1048584 | tf_op jit(solution)/shard_map/jit(_take)/gather | solution.py:120
  174.8 2.8 %gather_fusion.9 = f32[2,128,512]{2,1,0:T(8,128)S(1)} fusion(f32[16,128,512]{2,1,0:T(8,128)} %all-gather.2.cloned.1.call-done, s32[1024]{0:T(1024)S(1)} %pad_clamp_fusion.4), kind=kCustom, calls=%fused_computation.3.clone | custom fusion | bytes 1048584 | tf_op jit(solution)/shard_map/jit(_take)/gather | solution.py:120
  178.9 2.1 collective-permute-start
  181.0 5.8 %gather_fusion.15 = f32[50,128,128]{2,1,0:T(8,128)} fusion(f32[128,128,128]{2,1,0:T(8,128)} %bitcast.16, s32[1024]{0:T(1024)S(1)} %pad_clamp_fusion.1), kind=kCustom, calls=%fused_computation.11.clone | custom fusion | bytes 6553800 | tf_op jit(solution)/shard_map/jit(_take)/gather | solution.py:87
  186.8 5.9 %gather_fusion.13 = f32[50,128,128]{2,1,0:T(8,128)} fusion(f32[128,128,128]{2,1,0:T(8,128)} %bitcast.16, s32[1024]{0:T(1024)S(1)} %pad_clamp_fusion.2), kind=kCustom, calls=%fused_computation.5.clone | custom fusion | bytes 6553800 | tf_op jit(solution)/shard_map/jit(_take)/gather | solution.py:87
  192.7 4.4 %gather_fusion.7 = f32[10,128,512]{2,1,0:T(8,128)} fusion(f32[16,128,512]{2,1,0:T(8,128)} %all-gather.2.cloned.1.call-done, s32[1024]{0:T(1024)S(1)} %pad_clamp_fusion.8), kind=kCustom, calls=%fused_computation.7.clone | custom fusion | bytes 5242920 | tf_op jit(solution)/shard_map/jit(_take)/gather | solution.py:122
  197.1 4.5 %gather_fusion.5 = f32[10,128,512]{2,1,0:T(8,128)} fusion(f32[16,128,512]{2,1,0:T(8,128)} %all-gather.2.cloned.1.call-done, s32[1024]{0:T(1024)S(1)} %pad_clamp_fusion.9), kind=kCustom, calls=%fused_computation.1.clone | custom fusion | bytes 5242920 | tf_op jit(solution)/shard_map/jit(_take)/gather | solution.py:122
  201.6 3.4 %select_add_fusion.1 = f32[10,128,512]{2,1,0:T(8,128)S(1)} fusion(f32[10,128,512]{2,1,0:T(8,128)} %gather_fusion.7, f32[10,128,512]{2,1,0:T(8,128)} %gather_fusion.5, pred[10]{0:T(512)(128)(4,1)S(1)} %get-tuple-element.31, pred[10]{0:T(512)(128)(4,1)S(1)} %get-tuple-element.29), kind=kLoop, calls=%fused_computation.25 | loop fusion | flops 1966080 | bytes 7864340 | tf_op jit(solution)/shard_map/add | solution.py:123
  207.4 5.8 %fusion.27 = f32[1280,512]{1,0:T(8,128)} fusion(f32[1280,512]{1,0:T(8,128)S(1)} %bitcast_add_fusion.1, f32[512,512]{1,0:T(8,128)S(1)} %copy-done), kind=kOutput, calls=%fused_computation.155 | convolution fusion | flops 4026531840 | bytes 6291456 | tf_op jit(solution)/shard_map/dot_general | solution.py:141
  213.3 4.2 %copy.17 = f32[10,128,5,128]{3,2,1,0:T(8,128)} copy(f32[10,128,5,128]{3,1,2,0:T(8,128)S(1)} %bitcast.86) | data formatting | bytes 6553600 | tf_op jit(solution)/shard_map/transpose | solution.py:93
  217.5 4.6 %collective-permute-start.6 = (f32[80,512]{1,0:T(8,128)S(1)}, f32[80,512]{1,0:T(8,128)S(1)}, u32[]{:S(2)}, u32[]{:S(2)}) collective-permute-start(f32[80,512]{1,0:T(8,128)S(1)} %collective-permute-done), channel_id=1, source_target_pairs={{0,96},{16,112},{32,0},{48,16},{64,32},{80,48},{96,64},{112,80},{1... | collective-permute-start | bytes 491528 | tf_op jit(solution)/shard_map/ppermute | solution.py:159
  226.1 5.6 %collective-permute-done.1 = f32[80,512]{1,0:T(8,128)S(1)} collective-permute-done((f32[80,512]{1,0:T(8,128)S(1)}, f32[80,512]{1,0:T(8,128)S(1)}, u32[]{:S(2)}, u32[]{:S(2)}) %collective-permute-start.1) | collective-permute-done | bytes 163872 | tf_op jit(solution)/shard_map/ppermute | solution.py:159
  233.5 3.6 %collective-permute-done.2 = f32[80,512]{1,0:T(8,128)S(1)} collective-permute-done((f32[80,512]{1,0:T(8,128)S(1)}, f32[80,512]{1,0:T(8,128)S(1)}, u32[]{:S(2)}, u32[]{:S(2)}) %collective-permute-start.2) | collective-permute-done | bytes 163872 | tf_op jit(solution)/shard_map/ppermute | solution.py:159
  237.1 3.9 %collective-permute-start.3 = (f32[80,512]{1,0:T(8,128)S(1)}, f32[80,512]{1,0:T(8,128)S(1)}, u32[]{:S(2)}, u32[]{:S(2)}) collective-permute-start(f32[80,512]{1,0:T(8,128)S(1)} %collective-permute-done), channel_id=1, source_target_pairs={{0,48},{16,64},{32,80},{48,96},{64,112},{80,0},{96,16},{112,32},{1... | collective-permute-start | bytes 491528 | tf_op jit(solution)/shard_map/ppermute | solution.py:159
  241.7 3.3 %collective-permute-done.3 = f32[80,512]{1,0:T(8,128)S(1)} collective-permute-done((f32[80,512]{1,0:T(8,128)S(1)}, f32[80,512]{1,0:T(8,128)S(1)}, u32[]{:S(2)}, u32[]{:S(2)}) %collective-permute-start.3) | collective-permute-done | bytes 163872 | tf_op jit(solution)/shard_map/ppermute | solution.py:159
  252.1 10.4 %convolution_subtract_fusion = f32[1280,640]{1,0:T(8,128)} fusion(f32[1280,512]{1,0:T(8,128)S(1)} %copy-done.3, f32[640,512]{1,0:T(8,128)S(1)} %bitcast_select_fusion, f32[160,8,5,128]{3,2,1,0:T(8,128)} %bitcast.85, f32[1280]{0:T(1024)S(1)} %copy-done.4, s32[640]{0:T(1024)S(1)} %iota_add_fusion.1, s32[1280]{0:T(1024)S(1)} %iota_add_fusion), kind=kOutput, calls=%fused_computation.21 | convolution fusion | flops 5036441600 | bytes 10498560 | tf_op jit(solution)/shard_map/dot_general | solution.py:162
  (109 shorter events, 31.2 us)
Async XLA Ops:
  7.2 170.6 %copy-start = (f32[512,512]{1,0:T(8,128)S(1)}, f32[512,512]{1,0:T(8,128)}, u32[]{:S(2)}) copy-start(f32[512,512]{1,0:T(8,128)} %param.19) | copy-start | bytes 3145732
  16.5 12.7 %copy-start.5 = (s32[2,64]{1,0:T(2,128)S(1)}, s32[2,64]{1,0:T(2,128)}, u32[]{:S(2)}) copy-start(s32[2,64]{1,0:T(2,128)} %param.17) | copy-start | bytes 1540
  22.3 16.2 %all-to-all-start = ((f32[8,128,128]{2,1,0:T(8,128)}), f32[8,128,128]{2,1,0:T(8,128)S(1)}, u32[]{:S(2)}, u32[]{:S(2)}) async-start(f32[8,128,128]{2,1,0:T(8,128)} %gather_fusion), calls=%async_computation | async-start | bytes 1048576 | tf_op jit(solution)/shard_map/all_to_all | solution.py:61
  29.1 142.9 %all-gather.2.cloned.1.call-start = ((), (), s32[]{:S(2)}) async-start(), calls=%async_computation.2 | async-start | bytes 4456448 | tf_op jit(solution)/shard_map/all_gather | solution.py:108
  46.7 132.2 %all-to-all-start.1 = ((f32[128,1,128,128]{3,2,1,0:T(8,128)}), f32[128,1,128,128]{3,2,1,0:T(8,128)}, u32[]{:S(2)}, u32[]{:S(2)}) async-start(f32[128,1,128,128]{3,2,1,0:T(8,128)} %bitcast.82), calls=%async_computation.1 | async-start | bytes 16777216 | tf_op jit(solution)/shard_map/all_to_all | solution.py:62
  55.2 4.7 %copy-start.4 = (f32[1280]{0:T(1024)S(1)}, f32[1280]{0:T(1024)}, u32[]{:S(2)}) copy-start(f32[1280]{0:T(1024)} %param.18) | copy-start | bytes 15364
  178.9 38.6 %collective-permute-start = (f32[80,512]{1,0:T(8,128)S(1)}, f32[80,512]{1,0:T(8,128)S(1)}, u32[]{:S(2)}, u32[]{:S(2)}) collective-permute-start(f32[80,512]{1,0:T(8,128)S(1)} %fusion), channel_id=1, source_target_pairs={{0,0},{1,16},{2,32},{3,48},{4,64},{5,80},{6,96},{7,112},{8,1},{9,1... | collective-permute-start | bytes 491528 | tf_op jit(solution)/shard_map/ppermute | solution.py:155
  201.6 4.3 %copy-start.2 = (f32[50,128,128]{2,1,0:T(8,128)S(1)}, f32[50,128,128]{2,1,0:T(8,128)}, u32[]{:S(2)}) copy-start(f32[50,128,128]{2,1,0:T(8,128)} %gather_fusion.13) | copy-start | bytes 9830404
  205.0 2.0 copy-start.1
  217.5 30.2 %collective-permute-start.7 = (f32[80,512]{1,0:T(8,128)S(1)}, f32[80,512]{1,0:T(8,128)S(1)}, u32[]{:S(2)}, u32[]{:S(2)}) collective-permute-start(f32[80,512]{1,0:T(8,128)S(1)} %collective-permute-done), channel_id=1, source_target_pairs={{0,112},{16,0},{32,16},{48,32},{64,48},{80,64},{96,80},{112,96},{1... | collective-permute-start | bytes 491528 | tf_op jit(solution)/shard_map/ppermute | solution.py:159
  217.5 29.5 %collective-permute-start.6 = (f32[80,512]{1,0:T(8,128)S(1)}, f32[80,512]{1,0:T(8,128)S(1)}, u32[]{:S(2)}, u32[]{:S(2)}) collective-permute-start(f32[80,512]{1,0:T(8,128)S(1)} %collective-permute-done), channel_id=1, source_target_pairs={{0,96},{16,112},{32,0},{48,16},{64,32},{80,48},{96,64},{112,80},{1... | collective-permute-start | bytes 491528 | tf_op jit(solution)/shard_map/ppermute | solution.py:159
  222.1 24.3 %collective-permute-start.5 = (f32[80,512]{1,0:T(8,128)S(1)}, f32[80,512]{1,0:T(8,128)S(1)}, u32[]{:S(2)}, u32[]{:S(2)}) collective-permute-start(f32[80,512]{1,0:T(8,128)S(1)} %collective-permute-done), channel_id=1, source_target_pairs={{0,80},{16,96},{32,112},{48,0},{64,16},{80,32},{96,48},{112,64},{1... | collective-permute-start | bytes 491528 | tf_op jit(solution)/shard_map/ppermute | solution.py:159
  223.6 22.1 %collective-permute-start.4 = (f32[80,512]{1,0:T(8,128)S(1)}, f32[80,512]{1,0:T(8,128)S(1)}, u32[]{:S(2)}, u32[]{:S(2)}) collective-permute-start(f32[80,512]{1,0:T(8,128)S(1)} %collective-permute-done), channel_id=1, source_target_pairs={{0,64},{16,80},{32,96},{48,112},{64,0},{80,16},{96,32},{112,48},{1... | collective-permute-start | bytes 491528 | tf_op jit(solution)/shard_map/ppermute | solution.py:159
  225.4 6.3 %collective-permute-start.1 = (f32[80,512]{1,0:T(8,128)S(1)}, f32[80,512]{1,0:T(8,128)S(1)}, u32[]{:S(2)}, u32[]{:S(2)}) collective-permute-start(f32[80,512]{1,0:T(8,128)S(1)} %collective-permute-done), channel_id=1, source_target_pairs={{0,16},{16,32},{32,48},{48,64},{64,80},{80,96},{96,112},{112,0},{1... | collective-permute-start | bytes 491528 | tf_op jit(solution)/shard_map/ppermute | solution.py:159
  231.7 5.4 %collective-permute-start.2 = (f32[80,512]{1,0:T(8,128)S(1)}, f32[80,512]{1,0:T(8,128)S(1)}, u32[]{:S(2)}, u32[]{:S(2)}) collective-permute-start(f32[80,512]{1,0:T(8,128)S(1)} %collective-permute-done), channel_id=1, source_target_pairs={{0,32},{16,48},{32,64},{48,80},{64,96},{80,112},{96,0},{112,16},{1... | collective-permute-start | bytes 491528 | tf_op jit(solution)/shard_map/ppermute | solution.py:159
  237.1 7.9 %collective-permute-start.3 = (f32[80,512]{1,0:T(8,128)S(1)}, f32[80,512]{1,0:T(8,128)S(1)}, u32[]{:S(2)}, u32[]{:S(2)}) collective-permute-start(f32[80,512]{1,0:T(8,128)S(1)} %collective-permute-done), channel_id=1, source_target_pairs={{0,48},{16,64},{32,80},{48,96},{64,112},{80,0},{96,16},{112,32},{1... | collective-permute-start | bytes 491528 | tf_op jit(solution)/shard_map/ppermute | solution.py:159
  250.4 1.7 copy-start.3
Sparse Core Ops, SparseCore 0:
  40.3 131.6 all-gather.1

commit v12 on v10

--- a/solution.py
+++ b/solution.py
@@ -47,7 +47,7 @@
     slot_tile = jnp.where(
         (inv_l >= 0)[None, :], inv_k[:, None] * col_items + inv_l[None, :], row_items * col_items
     )
-    local_tiles = jnp.concatenate([local_tiles, jnp.zeros((1, BLK, BLK), jnp.float32)], axis=0)
+    local_tiles = jnp.pad(local_tiles, ((0, 1), (0, 0), (0, 0)))
     outgoing = jnp.take(local_tiles, slot_tile.reshape(-1), axis=0, mode="clip").reshape(
         devices_all, 1, BLK, BLK
     )
@@ -58,6 +58,7 @@
         jnp.any(is_panel), inv_k * col_items + panel_l, row_items * col_items
     )
     panel_out = jnp.take(local_tiles, panel_tile, axis=0, mode="clip")
+    outgoing, panel_out = lax.optimization_barrier((outgoing, panel_out))
     panel_in = lax.all_to_all(panel_out, "row", split_axis=0, concat_axis=0, tiled=True)
     incoming = lax.all_to_all(
         outgoing, ("row", "col"), split_axis=0, concat_axis=0, tiled=True

time: 255 us -> 257 us (level)
  waiting for transfers between devices: 127 us -> 134 us
  local copies, waits for them, and re-layouts: 62.2 us -> 57.8 us
    all_to_all x1, waiting for transfers between devices: 1.2 us -> 7.74 us  [on_device(): lax.all_to_all(panel_out, 'row', split_axis=0, concat_axis=0, tiled=True)]
    concatenate x1 -> x0, local copies, waits for them, and re-layouts: 4.7 us -> none  [on_device(): jnp.concatenate([local_tiles, jnp.zeros((1, BLK, BLK), jnp.float32)], axi...]
  transfers between devices with their start and end apart: 11 -> 11, of which waited for: 6 -> 6; matrix products, arithmetic and copies ran while one was open for 14% -> 11% of each run, Pallas kernels for 0% -> 0%
where the time goes in v12:
time: 257 us; the launch traced here: 255 us
  waiting for transfers between devices  134 us (52%)
  local copies, waits for them, and re-layouts  57.8 us (22%)
  starting transfers between devices  25.4 us (10%)
  matrix products  14.9 us (6%)
  between operations  14.5 us (6%)
  other arithmetic  8.89 us (3%)
    all_to_all x1, waiting for transfers between devices, on_device(): lax.all_to_all(outgoing, ('row', 'col'), split_axis=0, concat_axis=0, til...  114 us
    gather x2, local copies, waits for them, and re-layouts, assemble(): jnp.take(incoming, source[:, :width].reshape(-1), axis=0, mode='fill', fi...  11.7 us
    dot_general x1, matrix products, on_device(): lax.dot_general(factor_panel, across, (((1,), (1,)), ((), ())), precision...  10.4 us
    unnamed x22, local copies, waits for them, and re-layouts  9.54 us
    gather x2, local copies, waits for them, and re-layouts, on_device(): part = jnp.take(panel_parts, holder, axis=0, mode='fill', fill_value=0.0)  8.89 us
    all_to_all x1, starting transfers between devices, on_device(): lax.all_to_all(outgoing, ('row', 'col'), split_axis=0, concat_axis=0, til...  8.55 us
    ppermute x7, starting transfers between devices, on_device(): stack.append(lax.ppermute(moved, 'row', shift))  7.88 us
    all_to_all x1, waiting for transfers between devices, on_device(): lax.all_to_all(panel_out, 'row', split_axis=0, concat_axis=0, tiled=True)  7.74 us
  transfers between devices with their start and end apart: 11, of which 6 were waited for; matrix products, arithmetic and copies ran while one was open for 11% of the time, Pallas kernels for 0%

profile of v12, /device:TPU:1, one launch (start us, length us, event | category | flops | bytes accessed | tf_op | source)
XLA Modules:
  0.0 255.2 jit_solution(7975887862348327341)
XLA Ops:
  12.2 3.2 %copy.17 = f32[128,8,8,128]{3,2,1,0:T(8,128)S(1)} copy(f32[128,8,8,128]{3,1,2,0:T(8,128)} %bitcast.80) | data formatting | bytes 8388608
  16.4 2.3 pad.4
  18.7 6.5 %gather_fusion = f32[128,128,128]{2,1,0:T(8,128)} fusion(f32[65,128,128]{2,1,0:T(8,128)} %pad.4, s32[1024]{0:T(1024)S(1)} %get-tuple-element.44), kind=kCustom, calls=%fused_computation.8 | custom fusion | bytes 16777728 | tf_op jit(solution)/shard_map/jit(_take)/gather | solution.py:51
  25.3 3.6 %gather_fusion.1 = f32[8,128,128]{2,1,0:T(8,128)} fusion(f32[65,128,128]{2,1,0:T(8,128)} %pad.4, s32[1024]{0:T(1024)S(1)} %get-tuple-element.43), kind=kCustom, calls=%fused_computation.9 | custom fusion | bytes 1048608 | tf_op jit(solution)/shard_map/jit(_take)/gather | solution.py:60
  28.9 6.8 %all-to-all-start = ((f32[8,128,128]{2,1,0:T(8,128)}), f32[8,128,128]{2,1,0:T(8,128)S(1)}, u32[]{:S(2)}, u32[]{:S(2)}) async-start(f32[8,128,128]{2,1,0:T(8,128)} %gather_fusion.1), calls=%async_computation | async-start | bytes 1048576 | tf_op jit(solution)/shard_map/all_to_all | solution.py:62
  37.3 7.7 %all-to-all-done = f32[8,128,128]{2,1,0:T(8,128)S(1)} async-done(((f32[8,128,128]{2,1,0:T(8,128)}), f32[8,128,128]{2,1,0:T(8,128)S(1)}, u32[]{:S(2)}, u32[]{:S(2)}) %all-to-all-start) | async-done | bytes 524320 | tf_op jit(solution)/shard_map/all_to_all | solution.py:62
  45.0 8.6 %all-to-all-start.1 = ((f32[128,1,128,128]{3,2,1,0:T(8,128)}), f32[128,1,128,128]{3,2,1,0:T(8,128)}, u32[]{:S(2)}, u32[]{:S(2)}) async-start(f32[128,1,128,128]{3,2,1,0:T(8,128)} %bitcast.75), calls=%async_computation.1 | async-start | bytes 16777216 | tf_op jit(solution)/shard_map/all_to_all | solution.py:63
  59.0 114.0 %all-to-all-done.1 = f32[128,1,128,128]{3,2,1,0:T(8,128)} async-done(((f32[128,1,128,128]{3,2,1,0:T(8,128)}), f32[128,1,128,128]{3,2,1,0:T(8,128)}, u32[]{:S(2)}, u32[]{:S(2)}) %all-to-all-start.1) | async-done | bytes 8388640 | tf_op jit(solution)/shard_map/all_to_all | solution.py:63
  172.9 5.9 %gather_fusion.9 = f32[50,128,128]{2,1,0:T(8,128)} fusion(f32[128,128,128]{2,1,0:T(8,128)} %bitcast.16, s32[1024]{0:T(1024)S(1)} %pad_clamp_fusion.2), kind=kCustom, calls=%fused_computation.3.clone | custom fusion | bytes 6553800 | tf_op jit(solution)/shard_map/jit(_take)/gather | solution.py:88
  178.8 5.8 %gather_fusion.11 = f32[50,128,128]{2,1,0:T(8,128)} fusion(f32[128,128,128]{2,1,0:T(8,128)} %bitcast.16, s32[1024]{0:T(1024)S(1)} %pad_clamp_fusion.1), kind=kCustom, calls=%fused_computation.7.clone | custom fusion | bytes 6553800 | tf_op jit(solution)/shard_map/jit(_take)/gather | solution.py:88
  184.7 4.5 %gather_fusion.5 = f32[10,128,512]{2,1,0:T(8,128)} fusion(f32[16,128,512]{2,1,0:T(8,128)} %all-gather.2.cloned.1.call-done, s32[1024]{0:T(1024)S(1)} %get-tuple-element.42), kind=kCustom, calls=%fused_computation.1.clone | custom fusion | bytes 5242920 | tf_op jit(solution)/shard_map/jit(_take)/gather | solution.py:114
  189.2 4.4 %gather_fusion.7 = f32[10,128,512]{2,1,0:T(8,128)} fusion(f32[16,128,512]{2,1,0:T(8,128)} %all-gather.2.cloned.1.call-done, s32[1024]{0:T(1024)S(1)} %get-tuple-element.41), kind=kCustom, calls=%fused_computation.5.clone | custom fusion | bytes 5242920 | tf_op jit(solution)/shard_map/jit(_take)/gather | solution.py:114
  193.6 3.2 %select_add_fusion.1 = f32[10,128,512]{2,1,0:T(8,128)S(1)} fusion(f32[10,128,512]{2,1,0:T(8,128)} %gather_fusion.7, f32[10,128,512]{2,1,0:T(8,128)} %gather_fusion.5, pred[10]{0:T(512)(128)(4,1)S(1)} %get-tuple-element.25, pred[10]{0:T(512)(128)(4,1)S(1)} %get-tuple-element.23), kind=kLoop, calls=%fused_computation.21 | loop fusion | flops 1966080 | bytes 7864340 | tf_op jit(solution)/shard_map/add | solution.py:115
  197.8 4.5 %fusion.16 = f32[1280,512]{1,0:T(8,128)S(1)} fusion(f32[1280,512]{1,0:T(8,128)S(1)} %bitcast_add_fusion.1, f32[512,512]{1,0:T(8,128)S(1)} %copy-done), kind=kOutput, calls=%fused_computation.129 | convolution fusion | flops 4026531840 | bytes 6291456 | tf_op jit(solution)/shard_map/dot_general | solution.py:119
  202.3 1.9 collective-permute-start
  204.7 4.2 %copy.16 = f32[10,128,5,128]{3,2,1,0:T(8,128)} copy(f32[10,128,5,128]{3,1,2,0:T(8,128)S(1)} %bitcast.79) | data formatting | bytes 6553600 | tf_op jit(solution)/shard_map/transpose | solution.py:94
  209.0 4.5 %collective-permute-done = f32[80,512]{1,0:T(8,128)S(1)} collective-permute-done((f32[80,512]{1,0:T(8,128)S(1)}, f32[80,512]{1,0:T(8,128)S(1)}, u32[]{:S(2)}, u32[]{:S(2)}) %collective-permute-start) | collective-permute-done | bytes 163872 | tf_op jit(solution)/shard_map/ppermute | solution.py:134
  213.5 2.7 %collective-permute-start.1 = (f32[80,512]{1,0:T(8,128)S(1)}, f32[80,512]{1,0:T(8,128)S(1)}, u32[]{:S(2)}, u32[]{:S(2)}) collective-permute-start(f32[80,512]{1,0:T(8,128)S(1)} %collective-permute-done), channel_id=1, source_target_pairs={{0,16},{16,32},{32,48},{48,64},{64,80},{80,96},{96,112},{112,0},{1... | collective-permute-start | bytes 491528 | tf_op jit(solution)/shard_map/ppermute | solution.py:138
  217.4 2.0 collective-permute-start.4
  224.6 2.1 collective-permute-done.3
  227.3 4.2 %collective-permute-done.4 = f32[80,512]{1,0:T(8,128)S(1)} collective-permute-done((f32[80,512]{1,0:T(8,128)S(1)}, f32[80,512]{1,0:T(8,128)S(1)}, u32[]{:S(2)}, u32[]{:S(2)}) %collective-permute-start.4) | collective-permute-done | bytes 163872 | tf_op jit(solution)/shard_map/ppermute | solution.py:138
  234.3 1.9 gather_fusion.3
  236.4 1.6 copy-done.4
  237.9 10.4 %convolution_subtract_fusion = f32[1280,640]{1,0:T(8,128)} fusion(f32[1280,512]{1,0:T(8,128)S(1)} %copy-done.4, f32[640,512]{1,0:T(8,128)S(1)} %bitcast_select_fusion, f32[160,8,5,128]{3,2,1,0:T(8,128)} %bitcast.78, f32[1280]{0:T(1024)S(1)} %copy-done.5, s32[640]{0:T(1024)S(1)} %iota_add_fusion.1, s32[1280]{0:T(1024)S(1)} %iota_add_fusion), kind=kOutput, calls=%fused_computation.17 | convolution fusion | flops 5036441600 | bytes 10498560 | tf_op jit(solution)/shard_map/dot_general | solution.py:141
  (97 shorter events, 24.0 us)
Async XLA Ops:
  7.2 190.6 %copy-start = (f32[512,512]{1,0:T(8,128)S(1)}, f32[512,512]{1,0:T(8,128)}, u32[]{:S(2)}) copy-start(f32[512,512]{1,0:T(8,128)} %param.15) | copy-start | bytes 3145732
  18.7 16.9 %copy-start.6 = (s32[2,64]{1,0:T(2,128)S(1)}, s32[2,64]{1,0:T(2,128)}, u32[]{:S(2)}) copy-start(s32[2,64]{1,0:T(2,128)} %param.13) | copy-start | bytes 1540
  28.9 16.2 %all-to-all-start = ((f32[8,128,128]{2,1,0:T(8,128)}), f32[8,128,128]{2,1,0:T(8,128)S(1)}, u32[]{:S(2)}, u32[]{:S(2)}) async-start(f32[8,128,128]{2,1,0:T(8,128)} %gather_fusion.1), calls=%async_computation | async-start | bytes 1048576 | tf_op jit(solution)/shard_map/all_to_all | solution.py:62
  45.0 127.9 %all-to-all-start.1 = ((f32[128,1,128,128]{3,2,1,0:T(8,128)}), f32[128,1,128,128]{3,2,1,0:T(8,128)}, u32[]{:S(2)}, u32[]{:S(2)}) async-start(f32[128,1,128,128]{3,2,1,0:T(8,128)} %bitcast.75), calls=%async_computation.1 | async-start | bytes 16777216 | tf_op jit(solution)/shard_map/all_to_all | solution.py:63
  53.6 131.1 %all-gather.2.cloned.1.call-start = ((), (), s32[]{:S(2)}) async-start(), calls=%async_computation.2 | async-start | bytes 4456448 | tf_op jit(solution)/shard_map/all_gather | solution.py:109
  193.6 3.3 %copy-start.5 = (f32[1280]{0:T(1024)S(1)}, f32[1280]{0:T(1024)}, u32[]{:S(2)}) copy-start(f32[1280]{0:T(1024)} %param.14) | copy-start | bytes 15364
  197.7 6.5 %copy-start.1 = (f32[50,128,128]{2,1,0:T(8,128)S(1)}, f32[50,128,128]{2,1,0:T(8,128)}, u32[]{:S(2)}) copy-start(f32[50,128,128]{2,1,0:T(8,128)} %gather_fusion.9) | copy-start | bytes 9830404
  197.8 6.5 %copy-start.2 = (f32[50,128,128]{2,1,0:T(8,128)S(1)}, f32[50,128,128]{2,1,0:T(8,128)}, u32[]{:S(2)}) copy-start(f32[50,128,128]{2,1,0:T(8,128)} %gather_fusion.11) | copy-start | bytes 9830404
  202.3 2.0 copy-start.3
  202.3 11.2 %collective-permute-start = (f32[80,512]{1,0:T(8,128)S(1)}, f32[80,512]{1,0:T(8,128)S(1)}, u32[]{:S(2)}, u32[]{:S(2)}) collective-permute-start(f32[80,512]{1,0:T(8,128)S(1)} %constant_dynamic-slice_fusion.3), channel_id=1, source_target_pairs={{0,0},{1,16},{2,32},{3,48},{4,64},{5,80},{6,96},{7,112},{8,1},{9,1... | collective-permute-start | bytes 491528 | tf_op jit(solution)/shard_map/ppermute | solution.py:134
  213.5 7.0 %collective-permute-start.1 = (f32[80,512]{1,0:T(8,128)S(1)}, f32[80,512]{1,0:T(8,128)S(1)}, u32[]{:S(2)}, u32[]{:S(2)}) collective-permute-start(f32[80,512]{1,0:T(8,128)S(1)} %collective-permute-done), channel_id=1, source_target_pairs={{0,16},{16,32},{32,48},{48,64},{64,80},{80,96},{96,112},{112,0},{1... | collective-permute-start | bytes 491528 | tf_op jit(solution)/shard_map/ppermute | solution.py:138
  216.2 6.9 %collective-permute-start.2 = (f32[80,512]{1,0:T(8,128)S(1)}, f32[80,512]{1,0:T(8,128)S(1)}, u32[]{:S(2)}, u32[]{:S(2)}) collective-permute-start(f32[80,512]{1,0:T(8,128)S(1)} %collective-permute-done), channel_id=1, source_target_pairs={{0,32},{16,48},{32,64},{48,80},{64,96},{80,112},{96,0},{112,16},{1... | collective-permute-start | bytes 491528 | tf_op jit(solution)/shard_map/ppermute | solution.py:138
  216.2 10.5 %collective-permute-start.3 = (f32[80,512]{1,0:T(8,128)S(1)}, f32[80,512]{1,0:T(8,128)S(1)}, u32[]{:S(2)}, u32[]{:S(2)}) collective-permute-start(f32[80,512]{1,0:T(8,128)S(1)} %collective-permute-done), channel_id=1, source_target_pairs={{0,48},{16,64},{32,80},{48,96},{64,112},{80,0},{96,16},{112,32},{1... | collective-permute-start | bytes 491528 | tf_op jit(solution)/shard_map/ppermute | solution.py:138
  217.4 14.1 %collective-permute-start.4 = (f32[80,512]{1,0:T(8,128)S(1)}, f32[80,512]{1,0:T(8,128)S(1)}, u32[]{:S(2)}, u32[]{:S(2)}) collective-permute-start(f32[80,512]{1,0:T(8,128)S(1)} %collective-permute-done), channel_id=1, source_target_pairs={{0,64},{16,80},{32,96},{48,112},{64,0},{80,16},{96,32},{112,48},{1... | collective-permute-start | bytes 491528 | tf_op jit(solution)/shard_map/ppermute | solution.py:138
  219.4 12.8 %collective-permute-start.5 = (f32[80,512]{1,0:T(8,128)S(1)}, f32[80,512]{1,0:T(8,128)S(1)}, u32[]{:S(2)}, u32[]{:S(2)}) collective-permute-start(f32[80,512]{1,0:T(8,128)S(1)} %collective-permute-done), channel_id=1, source_target_pairs={{0,80},{16,96},{32,112},{48,0},{64,16},{80,32},{96,48},{112,64},{1... | collective-permute-start | bytes 491528 | tf_op jit(solution)/shard_map/ppermute | solution.py:138
  220.4 12.5 %collective-permute-start.6 = (f32[80,512]{1,0:T(8,128)S(1)}, f32[80,512]{1,0:T(8,128)S(1)}, u32[]{:S(2)}, u32[]{:S(2)}) collective-permute-start(f32[80,512]{1,0:T(8,128)S(1)} %collective-permute-done), channel_id=1, source_target_pairs={{0,96},{16,112},{32,0},{48,16},{64,32},{80,48},{96,64},{112,80},{1... | collective-permute-start | bytes 491528 | tf_op jit(solution)/shard_map/ppermute | solution.py:138
  223.1 10.4 %collective-permute-start.7 = (f32[80,512]{1,0:T(8,128)S(1)}, f32[80,512]{1,0:T(8,128)S(1)}, u32[]{:S(2)}, u32[]{:S(2)}) collective-permute-start(f32[80,512]{1,0:T(8,128)S(1)} %collective-permute-done), channel_id=1, source_target_pairs={{0,112},{16,0},{32,16},{48,32},{64,48},{80,64},{96,80},{112,96},{1... | collective-permute-start | bytes 491528 | tf_op jit(solution)/shard_map/ppermute | solution.py:138
  236.2 1.7 copy-start.4
Sparse Core Ops, SparseCore 0:
  57.1 112.5 all-gather.1

commit v13 on v10

--- a/solution.py
+++ b/solution.py
@@ -105,7 +105,13 @@
         .transpose(1, 0, 2)
         .reshape(BLK, PANEL)
     )
-    panel_parts = lax.all_gather(panel_part, "col", axis=0, tiled=False)
+    panel_parts = lax.all_to_all(
+        jnp.broadcast_to(panel_part[None], (col_count, BLK, PANEL)),
+        "col",
+        split_axis=0,
+        concat_axis=0,
+        tiled=True,
+    )
     raw_panel = None
     for c in range(2):
         a = jnp.take(inverses[c], my_rows)

time: 255 us -> 276 us (1.082)
  waiting for transfers between devices: 127 us -> 146 us
  starting transfers between devices: 26 us -> 43.8 us
  between operations: 14.5 us -> 1.16 us
  local copies, waits for them, and re-layouts: 62.2 us -> 55.8 us
  other arithmetic: 8.89 us -> 13.1 us
    all_to_all x1, waiting for transfers between devices: 114 us -> 0.01 us  [on_device(): lax.all_to_all(outgoing, ('row', 'col'), split_axis=0, concat_axis=0, til...]
    ppermute x1, waiting for transfers between devices: 4.4 us -> 74.7 us  [on_device(): moved = lax.ppermute(factor_piece, ('row', 'col'), pairs)]
    all_to_all x0 -> x1, waiting for transfers between devices: none -> 51.5 us  [on_device(): lax.all_to_all(jnp.broadcast_to(panel_part[None], (col_count, BLK, PANEL)...]
    all_to_all x1, starting transfers between devices: 8.76 us -> 16.8 us  [on_device(): lax.all_to_all(outgoing, ('row', 'col'), split_axis=0, concat_axis=0, til...]
    all_to_all x0 -> x1, starting transfers between devices: none -> 6.81 us  [on_device(): lax.all_to_all(jnp.broadcast_to(panel_part[None], (col_count, BLK, PANEL)...]
    all_to_all x1, waiting for transfers between devices: 1.2 us -> 7.7 us  [on_device(): lax.all_to_all(panel_out, 'row', split_axis=0, concat_axis=0, tiled=True)]
    unnamed x22 -> x18, local copies, waits for them, and re-layouts: 9.54 us -> 4.79 us
    ppermute x7, waiting for transfers between devices: 7.47 us -> 11.8 us  [on_device(): stack.append(lax.ppermute(moved, 'row', shift))]
  transfers between devices with their start and end apart: 11 -> 11, of which waited for: 6 -> 8; matrix products, arithmetic and copies ran while one was open for 14% -> 12% of each run, Pallas kernels for 0% -> 0%
where the time goes in v13:
time: 276 us; the launch traced here: 273 us
  waiting for transfers between devices  146 us (53%)
  local copies, waits for them, and re-layouts  55.8 us (20%)
  starting transfers between devices  43.8 us (16%)
  other arithmetic  13.1 us (5%)
  matrix products  13.1 us (5%)
    ppermute x1, waiting for transfers between devices, on_device(): moved = lax.ppermute(factor_piece, ('row', 'col'), pairs)  74.7 us
    all_to_all x1, waiting for transfers between devices, on_device(): lax.all_to_all(jnp.broadcast_to(panel_part[None], (col_count, BLK, PANEL)...  51.5 us
    all_to_all x1, starting transfers between devices, on_device(): lax.all_to_all(outgoing, ('row', 'col'), split_axis=0, concat_axis=0, til...  16.8 us
    ppermute x7, waiting for transfers between devices, on_device(): stack.append(lax.ppermute(moved, 'row', shift))  11.8 us
    gather x2, local copies, waits for them, and re-layouts, assemble(): jnp.take(incoming, source[:, :width].reshape(-1), axis=0, mode='fill', fi...  11.7 us
    gather x2, local copies, waits for them, and re-layouts, on_device(): part = jnp.take(panel_parts, holder, axis=0, mode='fill', fill_value=0.0)  8.79 us
    dot_general x1, matrix products, on_device(): lax.dot_general(factor_panel, across, (((1,), (1,)), ((), ())), precision...  8.6 us
    ppermute x7, starting transfers between devices, on_device(): stack.append(lax.ppermute(moved, 'row', shift))  8.36 us
  transfers between devices with their start and end apart: 11, of which 8 were waited for; matrix products, arithmetic and copies ran while one was open for 12% of the time, Pallas kernels for 0%

profile of v13, /device:TPU:1, one launch (start us, length us, event | category | flops | bytes accessed | tf_op | source)
XLA Modules:
  0.0 272.7 jit_solution(8671028536043995258)
XLA Ops:
  2.9 3.2 %copy.18 = f32[128,8,8,128]{3,2,1,0:T(8,128)S(1)} copy(f32[128,8,8,128]{3,1,2,0:T(8,128)} %bitcast.81) | data formatting | bytes 8388608
  6.3 2.7 copy.13
  11.8 4.7 %concatenate.3 = f32[65,128,128]{2,1,0:T(8,128)} pad(f32[64,128,128]{2,1,0:T(8,128)} %bitcast.77, f32[]{:T(128)} %constant.224.clone.1), padding=0_1x0_0x0_0 | pad | bytes 8454148 | tf_op jit(solution)/shard_map/concatenate | solution.py:50
  16.6 3.6 %gather_fusion = f32[8,128,128]{2,1,0:T(8,128)} fusion(f32[65,128,128]{2,1,0:T(8,128)} %concatenate.3, s32[1024]{0:T(1024)S(1)} %get-tuple-element.38), kind=kCustom, calls=%fused_computation.8 | custom fusion | bytes 1048608 | tf_op jit(solution)/shard_map/jit(_take)/gather | solution.py:60
  20.1 6.8 %all-to-all-start = ((f32[8,128,128]{2,1,0:T(8,128)}), f32[8,128,128]{2,1,0:T(8,128)S(1)}, u32[]{:S(2)}, u32[]{:S(2)}) async-start(f32[8,128,128]{2,1,0:T(8,128)} %gather_fusion), calls=%async_computation | async-start | bytes 1048576 | tf_op jit(solution)/shard_map/all_to_all | solution.py:61
  28.6 7.7 %all-to-all-done = f32[8,128,128]{2,1,0:T(8,128)S(1)} async-done(((f32[8,128,128]{2,1,0:T(8,128)}), f32[8,128,128]{2,1,0:T(8,128)S(1)}, u32[]{:S(2)}, u32[]{:S(2)}) %all-to-all-start) | async-done | bytes 524320 | tf_op jit(solution)/shard_map/all_to_all | solution.py:61
  39.7 6.8 %all-to-all-start.1 = ((f32[16,128,512]{2,1,0:T(8,128)}), f32[16,128,512]{2,1,0:T(8,128)}, u32[]{:S(2)}, u32[]{:S(2)}) async-start(f32[16,128,512]{2,1,0:T(8,128)} %broadcast_in_dim.163), calls=%async_computation.1 | async-start | bytes 8388608 | tf_op jit(solution)/shard_map/all_to_all | solution.py:108
  46.6 6.5 %gather_fusion.2 = f32[128,128,128]{2,1,0:T(8,128)} fusion(f32[65,128,128]{2,1,0:T(8,128)} %concatenate.3, s32[1024]{0:T(1024)S(1)} %get-tuple-element.37), kind=kCustom, calls=%fused_computation.10 | custom fusion | bytes 16777728 | tf_op jit(solution)/shard_map/jit(_take)/gather | solution.py:51
  53.1 51.5 %all-to-all-done.1 = f32[16,128,512]{2,1,0:T(8,128)} async-done(((f32[16,128,512]{2,1,0:T(8,128)}), f32[16,128,512]{2,1,0:T(8,128)}, u32[]{:S(2)}, u32[]{:S(2)}) %all-to-all-start.1) | async-done | bytes 4194336 | tf_op jit(solution)/shard_map/all_to_all | solution.py:108
  104.6 16.8 %all-to-all-start.2 = ((f32[128,1,128,128]{3,2,1,0:T(8,128)}), f32[128,1,128,128]{3,2,1,0:T(8,128)}, u32[]{:S(2)}, u32[]{:S(2)}) async-start(f32[128,1,128,128]{3,2,1,0:T(8,128)} %bitcast.76), calls=%async_computation.2 | async-start | bytes 16777216 | tf_op jit(solution)/shard_map/all_to_all | solution.py:62
  124.7 4.4 %gather_fusion.7 = f32[10,128,512]{2,1,0:T(8,128)} fusion(f32[16,128,512]{2,1,0:T(8,128)} %all-to-all-done.1, s32[1024]{0:T(1024)S(1)} %get-tuple-element.39), kind=kCustom, calls=%fused_computation.5.clone | custom fusion | bytes 5242920 | tf_op jit(solution)/shard_map/jit(_take)/gather | solution.py:119
  129.0 4.4 %gather_fusion.5 = f32[10,128,512]{2,1,0:T(8,128)} fusion(f32[16,128,512]{2,1,0:T(8,128)} %all-to-all-done.1, s32[1024]{0:T(1024)S(1)} %get-tuple-element.40), kind=kCustom, calls=%fused_computation.1.clone | custom fusion | bytes 5242920 | tf_op jit(solution)/shard_map/jit(_take)/gather | solution.py:119
  133.4 3.2 %select_add_fusion.1 = f32[10,128,512]{2,1,0:T(8,128)S(1)} fusion(f32[10,128,512]{2,1,0:T(8,128)} %gather_fusion.7, f32[10,128,512]{2,1,0:T(8,128)} %gather_fusion.5, pred[10]{0:T(512)(128)(4,1)S(1)} %get-tuple-element.21, pred[10]{0:T(512)(128)(4,1)S(1)} %get-tuple-element.19), kind=kLoop, calls=%fused_computation.21 | loop fusion | flops 1966080 | bytes 7864340 | tf_op jit(solution)/shard_map/add | solution.py:120
  137.6 4.5 %fusion.16 = f32[1280,512]{1,0:T(8,128)S(1)} fusion(f32[1280,512]{1,0:T(8,128)S(1)} %bitcast_add_fusion.1, f32[512,512]{1,0:T(8,128)S(1)} %copy-done), kind=kOutput, calls=%fused_computation.129 | convolution fusion | flops 4026531840 | bytes 6291456 | tf_op jit(solution)/shard_map/dot_general | solution.py:124
  143.6 5.1 %collective-permute-start = (f32[80,512]{1,0:T(8,128)S(1)}, f32[80,512]{1,0:T(8,128)S(1)}, u32[]{:S(2)}, u32[]{:S(2)}) collective-permute-start(f32[80,512]{1,0:T(8,128)S(1)} %constant_dynamic-slice_fusion.3), channel_id=1, source_target_pairs={{0,0},{1,16},{2,32},{3,48},{4,64},{5,80},{6,96},{7,112},{8,1},{9,1... | collective-permute-start | bytes 491528 | tf_op jit(solution)/shard_map/ppermute | solution.py:139
  148.9 74.7 %collective-permute-done = f32[80,512]{1,0:T(8,128)S(1)} collective-permute-done((f32[80,512]{1,0:T(8,128)S(1)}, f32[80,512]{1,0:T(8,128)S(1)}, u32[]{:S(2)}, u32[]{:S(2)}) %collective-permute-start) | collective-permute-done | bytes 163872 | tf_op jit(solution)/shard_map/ppermute | solution.py:139
  223.5 3.8 %collective-permute-start.1 = (f32[80,512]{1,0:T(8,128)S(1)}, f32[80,512]{1,0:T(8,128)S(1)}, u32[]{:S(2)}, u32[]{:S(2)}) collective-permute-start(f32[80,512]{1,0:T(8,128)S(1)} %collective-permute-done), channel_id=1, source_target_pairs={{0,16},{16,32},{32,48},{48,64},{64,80},{80,96},{96,112},{112,0},{1... | collective-permute-start | bytes 491528 | tf_op jit(solution)/shard_map/ppermute | solution.py:143
  227.3 3.2 %collective-permute-start.4 = (f32[80,512]{1,0:T(8,128)S(1)}, f32[80,512]{1,0:T(8,128)S(1)}, u32[]{:S(2)}, u32[]{:S(2)}) collective-permute-start(f32[80,512]{1,0:T(8,128)S(1)} %collective-permute-done), channel_id=1, source_target_pairs={{0,64},{16,80},{32,96},{48,112},{64,0},{80,16},{96,32},{112,48},{1... | collective-permute-start | bytes 491528 | tf_op jit(solution)/shard_map/ppermute | solution.py:143
  232.1 3.7 %collective-permute-done.2 = f32[80,512]{1,0:T(8,128)S(1)} collective-permute-done((f32[80,512]{1,0:T(8,128)S(1)}, f32[80,512]{1,0:T(8,128)S(1)}, u32[]{:S(2)}, u32[]{:S(2)}) %collective-permute-start.2) | collective-permute-done | bytes 163872 | tf_op jit(solution)/shard_map/ppermute | solution.py:143
  235.8 5.7 %collective-permute-done.3 = f32[80,512]{1,0:T(8,128)S(1)} collective-permute-done((f32[80,512]{1,0:T(8,128)S(1)}, f32[80,512]{1,0:T(8,128)S(1)}, u32[]{:S(2)}, u32[]{:S(2)}) %collective-permute-start.3) | collective-permute-done | bytes 163872 | tf_op jit(solution)/shard_map/ppermute | solution.py:143
  247.1 5.8 %gather_fusion.11 = f32[50,128,128]{2,1,0:T(8,128)} fusion(f32[128,128,128]{2,1,0:T(8,128)} %bitcast.16, s32[1024]{0:T(1024)S(1)} %pad_clamp_fusion.1), kind=kCustom, calls=%fused_computation.7.clone | custom fusion | bytes 6553800 | tf_op jit(solution)/shard_map/jit(_take)/gather | solution.py:87
  252.9 5.8 %gather_fusion.9 = f32[50,128,128]{2,1,0:T(8,128)} fusion(f32[128,128,128]{2,1,0:T(8,128)} %bitcast.16, s32[1024]{0:T(1024)S(1)} %pad_clamp_fusion.2), kind=kCustom, calls=%fused_computation.3.clone | custom fusion | bytes 6553800 | tf_op jit(solution)/shard_map/jit(_take)/gather | solution.py:87
  258.7 3.4 %select_add_fusion = f32[50,128,128]{2,1,0:T(8,128)S(1)} fusion(f32[50,128,128]{2,1,0:T(8,128)} %gather_fusion.11, f32[50,128,128]{2,1,0:T(8,128)} %gather_fusion.9, pred[50]{0:T(512)(128)(4,1)S(1)} %get-tuple-element.35, pred[50]{0:T(512)(128)(4,1)S(1)} %get-tuple-element.36), kind=kLoop, calls=%fused_computation.19 | loop fusion | flops 2457600 | bytes 9830500 | tf_op jit(solution)/shard_map/add | solution.py:90
  264.1 8.6 %convolution_subtract_fusion = f32[1280,640]{1,0:T(8,128)} fusion(f32[1280,512]{1,0:T(8,128)S(1)} %copy-done.2, f32[640,512]{1,0:T(8,128)S(1)} %bitcast_select_fusion, f32[160,8,5,128]{3,2,1,0:T(8,128)S(1)} %bitcast.79, f32[1280]{0:T(1024)S(1)} %copy-done.3, s32[640]{0:T(1024)S(1)} %iota_add_fusion.1, s32[1280]{0:T(1024)S(1)} %iota_add_fusion), kind=kOutput, calls=%fused_computation.17 | convolution fusion | flops 5036441600 | bytes 10498560 | tf_op jit(solution)/shard_map/dot_general | solution.py:146
  (93 shorter events, 24.9 us)
Async XLA Ops:
  0.6 137.0 %copy-start = (f32[512,512]{1,0:T(8,128)S(1)}, f32[512,512]{1,0:T(8,128)}, u32[]{:S(2)}) copy-start(f32[512,512]{1,0:T(8,128)} %param.15) | copy-start | bytes 3145732
  11.8 15.1 %copy-start.4 = (s32[2,64]{1,0:T(2,128)S(1)}, s32[2,64]{1,0:T(2,128)}, u32[]{:S(2)}) copy-start(s32[2,64]{1,0:T(2,128)} %param.13) | copy-start | bytes 1540
  20.1 16.2 %all-to-all-start = ((f32[8,128,128]{2,1,0:T(8,128)}), f32[8,128,128]{2,1,0:T(8,128)S(1)}, u32[]{:S(2)}, u32[]{:S(2)}) async-start(f32[8,128,128]{2,1,0:T(8,128)} %gather_fusion), calls=%async_computation | async-start | bytes 1048576 | tf_op jit(solution)/shard_map/all_to_all | solution.py:61
  39.7 64.8 %all-to-all-start.1 = ((f32[16,128,512]{2,1,0:T(8,128)}), f32[16,128,512]{2,1,0:T(8,128)}, u32[]{:S(2)}, u32[]{:S(2)}) async-start(f32[16,128,512]{2,1,0:T(8,128)} %broadcast_in_dim.163), calls=%async_computation.1 | async-start | bytes 8388608 | tf_op jit(solution)/shard_map/all_to_all | solution.py:108
  104.6 142.5 %all-to-all-start.2 = ((f32[128,1,128,128]{3,2,1,0:T(8,128)}), f32[128,1,128,128]{3,2,1,0:T(8,128)}, u32[]{:S(2)}, u32[]{:S(2)}) async-start(f32[128,1,128,128]{3,2,1,0:T(8,128)} %bitcast.76), calls=%async_computation.2 | async-start | bytes 16777216 | tf_op jit(solution)/shard_map/all_to_all | solution.py:62
  133.4 3.3 %copy-start.3 = (f32[1280]{0:T(1024)S(1)}, f32[1280]{0:T(1024)}, u32[]{:S(2)}) copy-start(f32[1280]{0:T(1024)} %param.14) | copy-start | bytes 15364
  142.1 1.5 copy-start.1
  143.6 79.9 %collective-permute-start = (f32[80,512]{1,0:T(8,128)S(1)}, f32[80,512]{1,0:T(8,128)S(1)}, u32[]{:S(2)}, u32[]{:S(2)}) collective-permute-start(f32[80,512]{1,0:T(8,128)S(1)} %constant_dynamic-slice_fusion.3), channel_id=1, source_target_pairs={{0,0},{1,16},{2,32},{3,48},{4,64},{5,80},{6,96},{7,112},{8,1},{9,1... | collective-permute-start | bytes 491528 | tf_op jit(solution)/shard_map/ppermute | solution.py:139
  223.5 7.2 %collective-permute-start.1 = (f32[80,512]{1,0:T(8,128)S(1)}, f32[80,512]{1,0:T(8,128)S(1)}, u32[]{:S(2)}, u32[]{:S(2)}) collective-permute-start(f32[80,512]{1,0:T(8,128)S(1)} %collective-permute-done), channel_id=1, source_target_pairs={{0,16},{16,32},{32,48},{48,64},{64,80},{80,96},{96,112},{112,0},{1... | collective-permute-start | bytes 491528 | tf_op jit(solution)/shard_map/ppermute | solution.py:143
  227.3 8.5 %collective-permute-start.2 = (f32[80,512]{1,0:T(8,128)S(1)}, f32[80,512]{1,0:T(8,128)S(1)}, u32[]{:S(2)}, u32[]{:S(2)}) collective-permute-start(f32[80,512]{1,0:T(8,128)S(1)} %collective-permute-done), channel_id=1, source_target_pairs={{0,32},{16,48},{32,64},{48,80},{64,96},{80,112},{96,0},{112,16},{1... | collective-permute-start | bytes 491528 | tf_op jit(solution)/shard_map/ppermute | solution.py:143
  227.3 14.2 %collective-permute-start.3 = (f32[80,512]{1,0:T(8,128)S(1)}, f32[80,512]{1,0:T(8,128)S(1)}, u32[]{:S(2)}, u32[]{:S(2)}) collective-permute-start(f32[80,512]{1,0:T(8,128)S(1)} %collective-permute-done), channel_id=1, source_target_pairs={{0,48},{16,64},{32,80},{48,96},{64,112},{80,0},{96,16},{112,32},{1... | collective-permute-start | bytes 491528 | tf_op jit(solution)/shard_map/ppermute | solution.py:143
  227.3 14.2 %collective-permute-start.4 = (f32[80,512]{1,0:T(8,128)S(1)}, f32[80,512]{1,0:T(8,128)S(1)}, u32[]{:S(2)}, u32[]{:S(2)}) collective-permute-start(f32[80,512]{1,0:T(8,128)S(1)} %collective-permute-done), channel_id=1, source_target_pairs={{0,64},{16,80},{32,96},{48,112},{64,0},{80,16},{96,32},{112,48},{1... | collective-permute-start | bytes 491528 | tf_op jit(solution)/shard_map/ppermute | solution.py:143
  230.6 11.0 %collective-permute-start.5 = (f32[80,512]{1,0:T(8,128)S(1)}, f32[80,512]{1,0:T(8,128)S(1)}, u32[]{:S(2)}, u32[]{:S(2)}) collective-permute-start(f32[80,512]{1,0:T(8,128)S(1)} %collective-permute-done), channel_id=1, source_target_pairs={{0,80},{16,96},{32,112},{48,0},{64,16},{80,32},{96,48},{112,64},{1... | collective-permute-start | bytes 491528 | tf_op jit(solution)/shard_map/ppermute | solution.py:143
  230.8 11.7 %collective-permute-start.6 = (f32[80,512]{1,0:T(8,128)S(1)}, f32[80,512]{1,0:T(8,128)S(1)}, u32[]{:S(2)}, u32[]{:S(2)}) collective-permute-start(f32[80,512]{1,0:T(8,128)S(1)} %collective-permute-done), channel_id=1, source_target_pairs={{0,96},{16,112},{32,0},{48,16},{64,32},{80,48},{96,64},{112,80},{1... | collective-permute-start | bytes 491528 | tf_op jit(solution)/shard_map/ppermute | solution.py:143
  235.8 8.1 %collective-permute-start.7 = (f32[80,512]{1,0:T(8,128)S(1)}, f32[80,512]{1,0:T(8,128)S(1)}, u32[]{:S(2)}, u32[]{:S(2)}) collective-permute-start(f32[80,512]{1,0:T(8,128)S(1)} %collective-permute-done), channel_id=1, source_target_pairs={{0,112},{16,0},{32,16},{48,32},{64,48},{80,64},{96,80},{112,96},{1... | collective-permute-start | bytes 491528 | tf_op jit(solution)/shard_map/ppermute | solution.py:143
  262.1 2.0 copy-start.2

commit v14 on v10

--- a/solution.py
+++ b/solution.py
@@ -135,16 +135,19 @@
     for q in range(1, row_count):
         shift = [(r, (r + q) % row_count) for r in range(row_count)]
         stack.append(lax.ppermute(moved, "row", shift))
-    order = (row_index - jnp.arange(row_count, dtype=jnp.int32)) % row_count
-    across = jnp.take(jnp.stack(stack), order, axis=0).reshape(col_width, PANEL)
-    update_term = lax.dot_general(
-        factor_panel,
-        across,
-        (((1,), (1,)), ((), ())),
-        precision=lax.Precision.HIGHEST,
-        preferred_element_type=jnp.float32,
-    )
-    trailing = front_local - update_term
+    chunk = col_width // row_count
+    trailing = front_local
+    for q in range(row_count):
+        offset = ((row_index - q) % row_count) * chunk
+        update_term = lax.dot_general(
+            factor_panel,
+            stack[q],
+            (((1,), (1,)), ((), ())),
+            precision=lax.Precision.HIGHEST,
+            preferred_element_type=jnp.float32,
+        )
+        current = lax.dynamic_slice_in_dim(front_local, offset, chunk, 1)
+        trailing = lax.dynamic_update_slice_in_dim(trailing, current - update_term, offset, 1)
     return (factor_panel, trailing)
 
 

time: 255 us -> 271 us (1.063)
  matrix products: 14.9 us -> 32.8 us
  waiting for transfers between devices: 127 us -> 121 us
  other arithmetic: 8.89 us -> 14.6 us
    dot_general x1 -> x8, matrix products: 10.4 us -> 28.4 us  [on_device(): lax.dot_general(factor_panel, stack[q], (((1,), (1,)), ((), ())), precisi...]
    ppermute x7, waiting for transfers between devices: 7.47 us -> 0.02 us  [on_device(): stack.append(lax.ppermute(moved, 'row', shift))]
    reshape x0 -> x1, local copies, waits for them, and re-layouts: none -> 5.87 us  [assemble(): return total.reshape(front_rows, width, BLK, BLK).transpose(0, 2, 1, 3).r...]
    add x1, other arithmetic: 0.46 us -> 5.1 us  [assemble(): total = part if total is None else total + part]
    transpose x1 -> x0, local copies, waits for them, and re-layouts: 4.23 us -> none  [assemble(): return total.reshape(front_rows, width, BLK, BLK).transpose(0, 2, 1, 3).r...]
    unnamed x22 -> x15, local copies, waits for them, and re-layouts: 9.54 us -> 9.47 us
  transfers between devices with their start and end apart: 11 -> 11, of which waited for: 6 -> 3; matrix products, arithmetic and copies ran while one was open for 14% -> 24% of each run, Pallas kernels for 0% -> 0%
where the time goes in v14:
time: 271 us; the launch traced here: 270 us
  waiting for transfers between devices  121 us (45%)
  local copies, waits for them, and re-layouts  61 us (23%)
  matrix products  32.8 us (12%)
  starting transfers between devices  26.3 us (10%)
  between operations  14.7 us (5%)
  other arithmetic  14.6 us (5%)
    all_to_all x1, waiting for transfers between devices, on_device(): lax.all_to_all(outgoing, ('row', 'col'), split_axis=0, concat_axis=0, til...  112 us
    dot_general x8, matrix products, on_device(): lax.dot_general(factor_panel, stack[q], (((1,), (1,)), ((), ())), precisi...  28.4 us
    gather x2, local copies, waits for them, and re-layouts, assemble(): jnp.take(incoming, source[:, :width].reshape(-1), axis=0, mode='fill', fi...  11.7 us
    unnamed x15, local copies, waits for them, and re-layouts  9.47 us
    ppermute x7, starting transfers between devices, on_device(): stack.append(lax.ppermute(moved, 'row', shift))  8.94 us
    gather x2, local copies, waits for them, and re-layouts, on_device(): part = jnp.take(panel_parts, holder, axis=0, mode='fill', fill_value=0.0)  8.78 us
    all_to_all x1, starting transfers between devices, on_device(): lax.all_to_all(outgoing, ('row', 'col'), split_axis=0, concat_axis=0, til...  8.55 us
    all_to_all x1, starting transfers between devices, on_device(): lax.all_to_all(panel_out, 'row', split_axis=0, concat_axis=0, tiled=True)  6.8 us
  transfers between devices with their start and end apart: 11, of which 3 were waited for; matrix products, arithmetic and copies ran while one was open for 24% of the time, Pallas kernels for 0%

profile of v14, /device:TPU:1, one launch (start us, length us, event | category | flops | bytes accessed | tf_op | source)
XLA Modules:
  0.0 270.1 jit_solution(1637962980068956768)
XLA Ops:
  17.6 4.7 %concatenate.3 = f32[65,128,128]{2,1,0:T(8,128)} pad(f32[64,128,128]{2,1,0:T(8,128)} %bitcast.74, f32[]{:T(128)} %constant.247.clone.1), padding=0_1x0_0x0_0 | pad | bytes 8454148 | tf_op jit(solution)/shard_map/concatenate | solution.py:50
  22.3 3.6 %gather_fusion = f32[8,128,128]{2,1,0:T(8,128)} fusion(f32[65,128,128]{2,1,0:T(8,128)} %concatenate.3, s32[1024]{0:T(1024)S(1)} %pad_clamp_fusion.7), kind=kCustom, calls=%fused_computation.8 | custom fusion | bytes 1048608 | tf_op jit(solution)/shard_map/jit(_take)/gather | solution.py:60
  25.9 6.8 %all-to-all-start = ((f32[8,128,128]{2,1,0:T(8,128)}), f32[8,128,128]{2,1,0:T(8,128)S(1)}, u32[]{:S(2)}, u32[]{:S(2)}) async-start(f32[8,128,128]{2,1,0:T(8,128)} %gather_fusion), calls=%async_computation | async-start | bytes 1048576 | tf_op jit(solution)/shard_map/all_to_all | solution.py:61
  33.5 6.5 %gather_fusion.2 = f32[128,128,128]{2,1,0:T(8,128)} fusion(f32[65,128,128]{2,1,0:T(8,128)} %concatenate.3, s32[1024]{0:T(1024)S(1)} %pad_clamp_fusion.2), kind=kCustom, calls=%fused_computation.10 | custom fusion | bytes 16777728 | tf_op jit(solution)/shard_map/jit(_take)/gather | solution.py:51
  42.1 8.6 %all-to-all-start.1 = ((f32[128,1,128,128]{3,2,1,0:T(8,128)}), f32[128,1,128,128]{3,2,1,0:T(8,128)}, u32[]{:S(2)}, u32[]{:S(2)}) async-start(f32[128,1,128,128]{3,2,1,0:T(8,128)} %bitcast.70), calls=%async_computation.1 | async-start | bytes 16777216 | tf_op jit(solution)/shard_map/all_to_all | solution.py:62
  57.6 112.4 %all-to-all-done.1 = f32[128,1,128,128]{3,2,1,0:T(8,128)} async-done(((f32[128,1,128,128]{3,2,1,0:T(8,128)}), f32[128,1,128,128]{3,2,1,0:T(8,128)}, u32[]{:S(2)}, u32[]{:S(2)}) %all-to-all-start.1) | async-done | bytes 8388640 | tf_op jit(solution)/shard_map/all_to_all | solution.py:62
  170.0 5.8 %gather_fusion.10 = f32[50,128,128]{2,1,0:T(8,128)} fusion(f32[128,128,128]{2,1,0:T(8,128)} %bitcast.16, s32[1024]{0:T(1024)S(1)} %pad_clamp_fusion), kind=kCustom, calls=%fused_computation.7.clone | custom fusion | bytes 6553800 | tf_op jit(solution)/shard_map/jit(_take)/gather | solution.py:87
  175.9 5.9 %gather_fusion.8 = f32[50,128,128]{2,1,0:T(8,128)} fusion(f32[128,128,128]{2,1,0:T(8,128)} %bitcast.16, s32[1024]{0:T(1024)S(1)} %pad_clamp_fusion.1), kind=kCustom, calls=%fused_computation.3.clone | custom fusion | bytes 6553800 | tf_op jit(solution)/shard_map/jit(_take)/gather | solution.py:87
  181.8 5.1 %select_add_fusion = f32[50,128,128]{2,1,0:T(8,128)} fusion(f32[50,128,128]{2,1,0:T(8,128)} %gather_fusion.10, f32[50,128,128]{2,1,0:T(8,128)} %gather_fusion.8, pred[50]{0:T(512)(128)(4,1)S(1)} %get-tuple-element.43, pred[50]{0:T(512)(128)(4,1)S(1)} %get-tuple-element.44), kind=kLoop, calls=%fused_computation.17 | loop fusion | flops 2457600 | bytes 9830500 | tf_op jit(solution)/shard_map/add | solution.py:90
  186.9 5.9 %copy.24 = f32[10,128,5,128]{1,0,3,2:T(8,128)} copy(f32[10,128,5,128]{3,1,2,0:T(8,128)} %bitcast.76) | data formatting | bytes 6553600 | tf_op jit(solution)/shard_map/reshape | solution.py:94
  192.7 4.4 %gather_fusion.6 = f32[10,128,512]{2,1,0:T(8,128)} fusion(f32[16,128,512]{2,1,0:T(8,128)} %all-gather.2.cloned.1.call-done, s32[1024]{0:T(1024)S(1)} %pad_clamp_fusion.4), kind=kCustom, calls=%fused_computation.5.clone | custom fusion | bytes 5242920 | tf_op jit(solution)/shard_map/jit(_take)/gather | solution.py:113
  197.1 4.4 %gather_fusion.4 = f32[10,128,512]{2,1,0:T(8,128)} fusion(f32[16,128,512]{2,1,0:T(8,128)} %all-gather.2.cloned.1.call-done, s32[1024]{0:T(1024)S(1)} %pad_clamp_fusion.5), kind=kCustom, calls=%fused_computation.1.clone | custom fusion | bytes 5242920 | tf_op jit(solution)/shard_map/jit(_take)/gather | solution.py:113
  201.5 3.4 %select_add_fusion.1 = f32[10,128,512]{2,1,0:T(8,128)S(1)} fusion(f32[10,128,512]{2,1,0:T(8,128)} %gather_fusion.6, f32[10,128,512]{2,1,0:T(8,128)} %gather_fusion.4, pred[10]{0:T(512)(128)(4,1)S(1)} %get-tuple-element.29, pred[10]{0:T(512)(128)(4,1)S(1)} %get-tuple-element.27), kind=kLoop, calls=%fused_computation.19 | loop fusion | flops 1966080 | bytes 7864340 | tf_op jit(solution)/shard_map/add | solution.py:114
  205.9 4.3 %fusion.21 = f32[1280,512]{1,0:T(8,128)S(1)} fusion(f32[1280,512]{1,0:T(8,128)S(1)} %bitcast_add_fusion.1, f32[512,512]{1,0:T(8,128)S(1)} %copy-done), kind=kOutput, calls=%fused_computation.121 | convolution fusion | flops 4026531840 | bytes 6291456 | tf_op jit(solution)/shard_map/dot_general | solution.py:118
  215.0 6.3 %collective-permute-done = f32[80,512]{1,0:T(8,128)S(1)} collective-permute-done((f32[80,512]{1,0:T(8,128)S(1)}, f32[80,512]{1,0:T(8,128)S(1)}, u32[]{:S(2)}, u32[]{:S(2)}) %collective-permute-start) | collective-permute-done | bytes 163872 | tf_op jit(solution)/shard_map/ppermute | solution.py:133
  227.4 4.4 %fusion.7 = f32[1280,640]{0,1:T(8,128)} fusion(f32[1280,640]{0,1:T(8,128)} %copy.29, s32[]{:T(128)S(6)} %select_n.296, f32[1280,512]{1,0:T(8,128)S(1)} %fusion.21, f32[80,512]{1,0:T(8,128)S(1)} %collective-permute-done), kind=kOutput, calls=%fused_computation.36 | convolution fusion | flops 629248000 | bytes 3604484 | tf_op jit(solution)/shard_map/dot_general | solution.py:142
  232.8 3.4 %fusion.6 = f32[1280,640]{0,1:T(8,128)} fusion(f32[1280,640]{0,1:T(8,128)} %fusion.7, s32[]{:T(128)S(6)} %select_n.299, f32[1280,512]{1,0:T(8,128)S(1)} %fusion.21, f32[80,512]{1,0:T(8,128)S(1)} %collective-permute-done.1, f32[1280,640]{0,1:T(8,128)S(1)} %bitcast_add_fusion), kind=kOutput, calls=%fused_computation.34 | convolution fusion | flops 629248000 | bytes 3604484 | tf_op jit(solution)/shard_map/dot_general | solution.py:142
  238.1 3.4 %fusion.5 = f32[1280,640]{0,1:T(8,128)} fusion(f32[1280,640]{0,1:T(8,128)} %fusion.6, s32[]{:T(128)S(6)} %select_n.301, f32[1280,512]{1,0:T(8,128)S(1)} %fusion.21, f32[80,512]{1,0:T(8,128)S(1)} %collective-permute-done.2, f32[1280,640]{0,1:T(8,128)S(1)} %bitcast_add_fusion), kind=kOutput, calls=%fused_computation.32 | convolution fusion | flops 629248000 | bytes 3604484 | tf_op jit(solution)/shard_map/dot_general | solution.py:142
  241.5 3.4 %fusion.4 = f32[1280,640]{0,1:T(8,128)} fusion(f32[1280,640]{0,1:T(8,128)} %fusion.5, s32[]{:T(128)S(6)} %select_n.303, f32[1280,512]{1,0:T(8,128)S(1)} %fusion.21, f32[80,512]{1,0:T(8,128)S(1)} %collective-permute-done.3, f32[1280,640]{0,1:T(8,128)S(1)} %bitcast_add_fusion), kind=kOutput, calls=%fused_computation.30 | convolution fusion | flops 629248000 | bytes 3604484 | tf_op jit(solution)/shard_map/dot_general | solution.py:142
  244.9 3.4 %fusion.3 = f32[1280,640]{0,1:T(8,128)} fusion(f32[1280,640]{0,1:T(8,128)} %fusion.4, s32[]{:T(128)S(6)} %select_n.305, f32[1280,512]{1,0:T(8,128)S(1)} %fusion.21, f32[80,512]{1,0:T(8,128)S(1)} %collective-permute-done.4, f32[1280,640]{0,1:T(8,128)S(1)} %bitcast_add_fusion), kind=kOutput, calls=%fused_computation.28 | convolution fusion | flops 629248000 | bytes 3604484 | tf_op jit(solution)/shard_map/dot_general | solution.py:142
  248.3 3.4 %fusion.2 = f32[1280,640]{0,1:T(8,128)} fusion(f32[1280,640]{0,1:T(8,128)} %fusion.3, s32[]{:T(128)S(6)} %select_n.307, f32[1280,512]{1,0:T(8,128)S(1)} %fusion.21, f32[80,512]{1,0:T(8,128)S(1)} %collective-permute-done.5, f32[1280,640]{0,1:T(8,128)S(1)} %bitcast_add_fusion), kind=kOutput, calls=%fused_computation.26 | convolution fusion | flops 629248000 | bytes 3604484 | tf_op jit(solution)/shard_map/dot_general | solution.py:142
  251.7 3.7 %fusion.1 = f32[1280,640]{0,1:T(8,128)} fusion(f32[1280,640]{0,1:T(8,128)} %fusion.2, s32[]{:T(128)S(6)} %select_n.309, f32[1280,512]{1,0:T(8,128)S(1)} %fusion.21, f32[80,512]{1,0:T(8,128)S(1)} %collective-permute-done.6, f32[1280,640]{0,1:T(8,128)S(1)} %bitcast_add_fusion), kind=kOutput, calls=%fused_computation.24 | convolution fusion | flops 629248000 | bytes 3604484 | tf_op jit(solution)/shard_map/dot_general | solution.py:142
  255.3 3.4 %fusion = f32[1280,640]{0,1:T(8,128)} fusion(f32[1280,640]{0,1:T(8,128)} %fusion.1, s32[]{:T(128)S(6)} %select_n.311, f32[1280,512]{1,0:T(8,128)S(1)} %fusion.21, f32[80,512]{1,0:T(8,128)S(1)} %collective-permute-done.7, f32[1280,640]{0,1:T(8,128)S(1)} %bitcast_add_fusion), kind=kOutput, calls=%fused_computation.22 | convolution fusion | flops 629248000 | bytes 3604484 | tf_op jit(solution)/shard_map/dot_general | solution.py:142
  258.7 4.6 %copy.23 = f32[1280,640]{1,0:T(8,128)} copy(f32[1280,640]{0,1:T(8,128)} %fusion) | data formatting | bytes 6553600
  (93 shorter events, 34.3 us)
Async XLA Ops:
  7.2 198.7 %copy-start = (f32[512,512]{1,0:T(8,128)S(1)}, f32[512,512]{1,0:T(8,128)}, u32[]{:S(2)}) copy-start(f32[512,512]{1,0:T(8,128)} %param.15) | copy-start | bytes 3145732
  25.9 16.2 %all-to-all-start = ((f32[8,128,128]{2,1,0:T(8,128)}), f32[8,128,128]{2,1,0:T(8,128)S(1)}, u32[]{:S(2)}, u32[]{:S(2)}) async-start(f32[8,128,128]{2,1,0:T(8,128)} %gather_fusion), calls=%async_computation | async-start | bytes 1048576 | tf_op jit(solution)/shard_map/all_to_all | solution.py:61
  42.1 8.6 %copy-start.3 = (s32[2,64]{1,0:T(2,128)S(1)}, s32[2,64]{1,0:T(2,128)}, u32[]{:S(2)}) copy-start(s32[2,64]{1,0:T(2,128)} %param.13) | copy-start | bytes 1540
  42.1 128.0 %all-to-all-start.1 = ((f32[128,1,128,128]{3,2,1,0:T(8,128)}), f32[128,1,128,128]{3,2,1,0:T(8,128)}, u32[]{:S(2)}, u32[]{:S(2)}) async-start(f32[128,1,128,128]{3,2,1,0:T(8,128)} %bitcast.70), calls=%async_computation.1 | async-start | bytes 16777216 | tf_op jit(solution)/shard_map/all_to_all | solution.py:62
  50.6 142.1 %all-gather.2.cloned.1.call-start = ((), (), s32[]{:S(2)}) async-start(), calls=%async_computation.2 | async-start | bytes 4456448 | tf_op jit(solution)/shard_map/all_gather | solution.py:108
  201.5 3.4 %copy-start.2 = (f32[1280]{0:T(1024)S(1)}, f32[1280]{0:T(1024)}, u32[]{:S(2)}) copy-start(f32[1280]{0:T(1024)} %param.14) | copy-start | bytes 15364
  201.5 10.6 %slice-start = ((s8[5242880]{0:T(1024)(128)(4,1)}), s8[4194304]{0:T(1024)(128)(4,1)S(1)}, s32[]{:S(2)}) async-start(s8[5242880]{0:T(1024)(128)(4,1)} %bitcast.71), calls=%async_computation.3 | async-start | bytes 8388608
  204.9 7.2 %slice-start.1 = ((s8[5242880]{0:T(1024)(128)(4,1)}), s8[1048576]{0:T(1024)(128)(4,1)S(1)}, s32[]{:S(2)}) async-start(s8[5242880]{0:T(1024)(128)(4,1)} %bitcast.71), calls=%async_computation.4 | async-start | bytes 2097152
  210.2 45.1 %copy-start.1 = (f32[1280,512]{1,0:T(8,128)}, f32[1280,512]{1,0:T(8,128)S(1)}, u32[]{:S(2)}) copy-start(f32[1280,512]{1,0:T(8,128)S(1)} %fusion.21) | copy-start | bytes 7864324
  210.2 11.1 %collective-permute-start = (f32[80,512]{1,0:T(8,128)S(1)}, f32[80,512]{1,0:T(8,128)S(1)}, u32[]{:S(2)}, u32[]{:S(2)}) collective-permute-start(f32[80,512]{1,0:T(8,128)S(1)} %constant_dynamic-slice_fusion.3), channel_id=1, source_target_pairs={{0,0},{1,16},{2,32},{3,48},{4,64},{5,80},{6,96},{7,112},{8,1},{9,1... | collective-permute-start | bytes 491528 | tf_op jit(solution)/shard_map/ppermute | solution.py:133
  221.3 10.5 %collective-permute-start.1 = (f32[80,512]{1,0:T(8,128)S(1)}, f32[80,512]{1,0:T(8,128)S(1)}, u32[]{:S(2)}, u32[]{:S(2)}) collective-permute-start(f32[80,512]{1,0:T(8,128)S(1)} %collective-permute-done), channel_id=1, source_target_pairs={{0,16},{16,32},{32,48},{48,64},{64,80},{80,96},{96,112},{112,0},{1... | collective-permute-start | bytes 491528 | tf_op jit(solution)/shard_map/ppermute | solution.py:137
  223.9 12.2 %collective-permute-start.2 = (f32[80,512]{1,0:T(8,128)S(1)}, f32[80,512]{1,0:T(8,128)S(1)}, u32[]{:S(2)}, u32[]{:S(2)}) collective-permute-start(f32[80,512]{1,0:T(8,128)S(1)} %collective-permute-done), channel_id=1, source_target_pairs={{0,32},{16,48},{32,64},{48,80},{64,96},{80,112},{96,0},{112,16},{1... | collective-permute-start | bytes 491528 | tf_op jit(solution)/shard_map/ppermute | solution.py:137
  223.9 17.6 %collective-permute-start.3 = (f32[80,512]{1,0:T(8,128)S(1)}, f32[80,512]{1,0:T(8,128)S(1)}, u32[]{:S(2)}, u32[]{:S(2)}) collective-permute-start(f32[80,512]{1,0:T(8,128)S(1)} %collective-permute-done), channel_id=1, source_target_pairs={{0,48},{16,64},{32,80},{48,96},{64,112},{80,0},{96,16},{112,32},{1... | collective-permute-start | bytes 491528 | tf_op jit(solution)/shard_map/ppermute | solution.py:137
  225.1 19.8 %collective-permute-start.4 = (f32[80,512]{1,0:T(8,128)S(1)}, f32[80,512]{1,0:T(8,128)S(1)}, u32[]{:S(2)}, u32[]{:S(2)}) collective-permute-start(f32[80,512]{1,0:T(8,128)S(1)} %collective-permute-done), channel_id=1, source_target_pairs={{0,64},{16,80},{32,96},{48,112},{64,0},{80,16},{96,32},{112,48},{1... | collective-permute-start | bytes 491528 | tf_op jit(solution)/shard_map/ppermute | solution.py:137
  227.2 21.1 %collective-permute-start.5 = (f32[80,512]{1,0:T(8,128)S(1)}, f32[80,512]{1,0:T(8,128)S(1)}, u32[]{:S(2)}, u32[]{:S(2)}) collective-permute-start(f32[80,512]{1,0:T(8,128)S(1)} %collective-permute-done), channel_id=1, source_target_pairs={{0,80},{16,96},{32,112},{48,0},{64,16},{80,32},{96,48},{112,64},{1... | collective-permute-start | bytes 491528 | tf_op jit(solution)/shard_map/ppermute | solution.py:137
  231.8 19.8 %collective-permute-start.6 = (f32[80,512]{1,0:T(8,128)S(1)}, f32[80,512]{1,0:T(8,128)S(1)}, u32[]{:S(2)}, u32[]{:S(2)}) collective-permute-start(f32[80,512]{1,0:T(8,128)S(1)} %collective-permute-done), channel_id=1, source_target_pairs={{0,96},{16,112},{32,0},{48,16},{64,32},{80,48},{96,64},{112,80},{1... | collective-permute-start | bytes 491528 | tf_op jit(solution)/shard_map/ppermute | solution.py:137
  236.2 19.2 %collective-permute-start.7 = (f32[80,512]{1,0:T(8,128)S(1)}, f32[80,512]{1,0:T(8,128)S(1)}, u32[]{:S(2)}, u32[]{:S(2)}) collective-permute-start(f32[80,512]{1,0:T(8,128)S(1)} %collective-permute-done), channel_id=1, source_target_pairs={{0,112},{16,0},{32,16},{48,32},{64,48},{80,64},{96,80},{112,96},{1... | collective-permute-start | bytes 491528 | tf_op jit(solution)/shard_map/ppermute | solution.py:137
Sparse Core Ops, SparseCore 0:
  54.3 112.4 all-gather.1

commit v15 on v10

--- a/solution.py
+++ b/solution.py
@@ -121,6 +121,7 @@
         precision=lax.Precision.HIGHEST,
         preferred_element_type=jnp.float32,
     )
+    incoming, factor_panel = lax.optimization_barrier((incoming, factor_panel))
     front_local = assemble(front_cols) + diag
     piece_rows = height // col_count
     factor_piece = lax.dynamic_slice_in_dim(factor_panel, col_index * piece_rows, piece_rows, 0)

time: 255 us -> 262 us (1.027)
  starting transfers between devices: 26 us -> 31.8 us
  local copies, waits for them, and re-layouts: 62.2 us -> 58.6 us
  other arithmetic: 8.89 us -> 11.8 us
    all_to_all x1, waiting for transfers between devices: 114 us -> 0.01 us  [on_device(): lax.all_to_all(outgoing, ('row', 'col'), split_axis=0, concat_axis=0, til...]
    all_gather x1, waiting for transfers between devices: 0.01 us -> 112 us  [on_device(): panel_parts = lax.all_gather(panel_part, 'col', axis=0, tiled=False)]
    all_to_all x1, waiting for transfers between devices: 1.2 us -> 7.7 us  [on_device(): lax.all_to_all(panel_out, 'row', split_axis=0, concat_axis=0, tiled=True)]
    ppermute x7, starting transfers between devices: 8.28 us -> 14.5 us  [on_device(): stack.append(lax.ppermute(moved, 'row', shift))]
    ppermute x1, waiting for transfers between devices: 4.4 us -> 0.01 us  [on_device(): moved = lax.ppermute(factor_piece, ('row', 'col'), pairs)]
    add x1, other arithmetic: 0.46 us -> 3.39 us  [assemble(): total = part if total is None else total + part]
    unnamed x22 -> x16, local copies, waits for them, and re-layouts: 9.54 us -> 9.53 us
  transfers between devices with their start and end apart: 11 -> 11, of which waited for: 6 -> 3; matrix products, arithmetic and copies ran while one was open for 14% -> 16% of each run, Pallas kernels for 0% -> 0%
where the time goes in v15:
time: 262 us; the launch traced here: 260 us
  waiting for transfers between devices  127 us (48%)
  local copies, waits for them, and re-layouts  58.6 us (22%)
  starting transfers between devices  31.8 us (12%)
  matrix products  16.2 us (6%)
  between operations  14.5 us (6%)
  other arithmetic  11.8 us (5%)
    all_gather x1, waiting for transfers between devices, on_device(): panel_parts = lax.all_gather(panel_part, 'col', axis=0, tiled=False)  112 us
    ppermute x7, starting transfers between devices, on_device(): stack.append(lax.ppermute(moved, 'row', shift))  14.5 us
    gather x2, local copies, waits for them, and re-layouts, assemble(): jnp.take(incoming, source[:, :width].reshape(-1), axis=0, mode='fill', fi...  11.7 us
    dot_general x1, matrix products, on_device(): lax.dot_general(factor_panel, across, (((1,), (1,)), ((), ())), precision...  10.4 us
    unnamed x16, local copies, waits for them, and re-layouts  9.53 us
    gather x2, local copies, waits for them, and re-layouts, on_device(): part = jnp.take(panel_parts, holder, axis=0, mode='fill', fill_value=0.0)  8.78 us
    all_to_all x1, starting transfers between devices, on_device(): lax.all_to_all(outgoing, ('row', 'col'), split_axis=0, concat_axis=0, til...  8.56 us
    all_to_all x1, waiting for transfers between devices, on_device(): lax.all_to_all(panel_out, 'row', split_axis=0, concat_axis=0, tiled=True)  7.7 us
  transfers between devices with their start and end apart: 11, of which 3 were waited for; matrix products, arithmetic and copies ran while one was open for 16% of the time, Pallas kernels for 0%

profile of v15, /device:TPU:1, one launch (start us, length us, event | category | flops | bytes accessed | tf_op | source)
XLA Modules:
  0.0 260.1 jit_solution(14828425165580940932)
XLA Ops:
  12.2 3.2 %copy.17 = f32[128,8,8,128]{3,2,1,0:T(8,128)S(1)} copy(f32[128,8,8,128]{3,1,2,0:T(8,128)} %bitcast.81) | data formatting | bytes 8388608
  16.5 2.3 concatenate.3
  18.8 3.6 %gather_fusion.1 = f32[8,128,128]{2,1,0:T(8,128)} fusion(f32[65,128,128]{2,1,0:T(8,128)} %concatenate.3, s32[1024]{0:T(1024)S(1)} %get-tuple-element.43), kind=kCustom, calls=%fused_computation.9 | custom fusion | bytes 1048608 | tf_op jit(solution)/shard_map/jit(_take)/gather | solution.py:60
  22.3 6.8 %all-to-all-start.1 = ((f32[8,128,128]{2,1,0:T(8,128)}), f32[8,128,128]{2,1,0:T(8,128)S(1)}, u32[]{:S(2)}, u32[]{:S(2)}) async-start(f32[8,128,128]{2,1,0:T(8,128)} %gather_fusion.1), calls=%async_computation.1 | async-start | bytes 1048576 | tf_op jit(solution)/shard_map/all_to_all | solution.py:61
  30.8 7.7 %all-to-all-done.1 = f32[8,128,128]{2,1,0:T(8,128)S(1)} async-done(((f32[8,128,128]{2,1,0:T(8,128)}), f32[8,128,128]{2,1,0:T(8,128)S(1)}, u32[]{:S(2)}, u32[]{:S(2)}) %all-to-all-start.1) | async-done | bytes 524320 | tf_op jit(solution)/shard_map/all_to_all | solution.py:61
  40.2 6.5 %gather_fusion = f32[128,128,128]{2,1,0:T(8,128)} fusion(f32[65,128,128]{2,1,0:T(8,128)} %concatenate.3, s32[1024]{0:T(1024)S(1)} %get-tuple-element.44), kind=kCustom, calls=%fused_computation.8 | custom fusion | bytes 16777728 | tf_op jit(solution)/shard_map/jit(_take)/gather | solution.py:51
  46.7 8.6 %all-to-all-start = ((f32[128,1,128,128]{3,2,1,0:T(8,128)}), f32[128,1,128,128]{3,2,1,0:T(8,128)}, u32[]{:S(2)}, u32[]{:S(2)}) async-start(f32[128,1,128,128]{3,2,1,0:T(8,128)} %bitcast.76), calls=%async_computation | async-start | bytes 16777216 | tf_op jit(solution)/shard_map/all_to_all | solution.py:62
  58.7 112.3 %all-gather.2.cloned.1.call-done = f32[16,128,512]{2,1,0:T(8,128)} async-done(((f32[1,128,512]{2,1,0:T(8,128)}), f32[16,128,512]{2,1,0:T(8,128)}) %all-gather.2.cloned.1.call-update) | async-done | bytes 4194320 | tf_op jit(solution)/shard_map/all_gather | solution.py:108
  171.0 4.4 %gather_fusion.5 = f32[10,128,512]{2,1,0:T(8,128)} fusion(f32[16,128,512]{2,1,0:T(8,128)} %all-gather.2.cloned.1.call-done, s32[1024]{0:T(1024)S(1)} %get-tuple-element.42), kind=kCustom, calls=%fused_computation.1.clone | custom fusion | bytes 5242920 | tf_op jit(solution)/shard_map/jit(_take)/gather | solution.py:113
  175.4 4.4 %gather_fusion.7 = f32[10,128,512]{2,1,0:T(8,128)} fusion(f32[16,128,512]{2,1,0:T(8,128)} %all-gather.2.cloned.1.call-done, s32[1024]{0:T(1024)S(1)} %get-tuple-element.41), kind=kCustom, calls=%fused_computation.5.clone | custom fusion | bytes 5242920 | tf_op jit(solution)/shard_map/jit(_take)/gather | solution.py:113
  179.8 3.2 %select_add_fusion.1 = f32[10,128,512]{2,1,0:T(8,128)S(1)} fusion(f32[10,128,512]{2,1,0:T(8,128)} %gather_fusion.7, f32[10,128,512]{2,1,0:T(8,128)} %gather_fusion.5, pred[10]{0:T(512)(128)(4,1)S(1)} %get-tuple-element.25, pred[10]{0:T(512)(128)(4,1)S(1)} %get-tuple-element.23), kind=kLoop, calls=%fused_computation.21 | loop fusion | flops 1966080 | bytes 7864340 | tf_op jit(solution)/shard_map/add | solution.py:114
  183.9 5.8 %fusion.16 = f32[1280,512]{1,0:T(8,128)} fusion(f32[1280,512]{1,0:T(8,128)S(1)} %bitcast_add_fusion.1, f32[512,512]{1,0:T(8,128)S(1)} %copy-done), kind=kOutput, calls=%fused_computation.129 | convolution fusion | flops 4026531840 | bytes 6291456 | tf_op jit(solution)/shard_map/dot_general | solution.py:118
  189.8 5.9 %gather_fusion.9 = f32[50,128,128]{2,1,0:T(8,128)} fusion(f32[128,128,128]{2,1,0:T(8,128)} %bitcast.8, s32[1024]{0:T(1024)S(1)} %pad_clamp_fusion.2), kind=kCustom, calls=%fused_computation.3.clone | custom fusion | bytes 6553800 | tf_op jit(solution)/shard_map/jit(_take)/gather | solution.py:87
  195.7 5.8 %gather_fusion.11 = f32[50,128,128]{2,1,0:T(8,128)} fusion(f32[128,128,128]{2,1,0:T(8,128)} %bitcast.8, s32[1024]{0:T(1024)S(1)} %pad_clamp_fusion.1), kind=kCustom, calls=%fused_computation.7.clone | custom fusion | bytes 6553800 | tf_op jit(solution)/shard_map/jit(_take)/gather | solution.py:87
  202.4 1.9 collective-permute-start
  204.4 3.4 %select_add_fusion = f32[50,128,128]{2,1,0:T(8,128)S(1)} fusion(f32[50,128,128]{2,1,0:T(8,128)} %gather_fusion.11, f32[50,128,128]{2,1,0:T(8,128)} %gather_fusion.9, pred[50]{0:T(512)(128)(4,1)S(1)} %get-tuple-element.39, pred[50]{0:T(512)(128)(4,1)S(1)} %get-tuple-element.40), kind=kLoop, calls=%fused_computation.19 | loop fusion | flops 2457600 | bytes 9830500 | tf_op jit(solution)/shard_map/add | solution.py:90
  207.8 4.2 %copy.16 = f32[10,128,5,128]{3,2,1,0:T(8,128)} copy(f32[10,128,5,128]{3,1,2,0:T(8,128)S(1)} %bitcast.80) | data formatting | bytes 6553600 | tf_op jit(solution)/shard_map/transpose | solution.py:93
  212.0 5.0 %collective-permute-start.1 = (f32[80,512]{1,0:T(8,128)S(1)}, f32[80,512]{1,0:T(8,128)S(1)}, u32[]{:S(2)}, u32[]{:S(2)}) collective-permute-start(f32[80,512]{1,0:T(8,128)S(1)} %collective-permute-done), channel_id=1, source_target_pairs={{0,16},{16,32},{32,48},{48,64},{64,80},{80,96},{96,112},{112,0},{1... | collective-permute-start | bytes 491528 | tf_op jit(solution)/shard_map/ppermute | solution.py:138
  217.0 3.1 %collective-permute-start.2 = (f32[80,512]{1,0:T(8,128)S(1)}, f32[80,512]{1,0:T(8,128)S(1)}, u32[]{:S(2)}, u32[]{:S(2)}) collective-permute-start(f32[80,512]{1,0:T(8,128)S(1)} %collective-permute-done), channel_id=1, source_target_pairs={{0,32},{16,48},{32,64},{48,80},{64,96},{80,112},{96,0},{112,16},{1... | collective-permute-start | bytes 491528 | tf_op jit(solution)/shard_map/ppermute | solution.py:138
  220.1 2.2 collective-permute-start.3
  229.2 7.2 %collective-permute-done.4 = f32[80,512]{1,0:T(8,128)S(1)} collective-permute-done((f32[80,512]{1,0:T(8,128)S(1)}, f32[80,512]{1,0:T(8,128)S(1)}, u32[]{:S(2)}, u32[]{:S(2)}) %collective-permute-start.4) | collective-permute-done | bytes 163872 | tf_op jit(solution)/shard_map/ppermute | solution.py:138
  239.1 1.9 gather_fusion.3
  241.3 1.6 copy-done.1
  242.8 10.4 %convolution_subtract_fusion = f32[1280,640]{1,0:T(8,128)} fusion(f32[1280,512]{1,0:T(8,128)S(1)} %copy-done.1, f32[640,512]{1,0:T(8,128)S(1)} %bitcast_select_fusion, f32[160,8,5,128]{3,2,1,0:T(8,128)} %bitcast.79, f32[1280]{0:T(1024)S(1)} %copy-done.2, s32[640]{0:T(1024)S(1)} %iota_add_fusion.1, s32[1280]{0:T(1024)S(1)} %iota_add_fusion), kind=kOutput, calls=%fused_computation.17 | convolution fusion | flops 5036441600 | bytes 10498560 | tf_op jit(solution)/shard_map/dot_general | solution.py:141
  (91 shorter events, 24.1 us)
Async XLA Ops:
  7.2 176.8 %copy-start = (f32[512,512]{1,0:T(8,128)S(1)}, f32[512,512]{1,0:T(8,128)}, u32[]{:S(2)}) copy-start(f32[512,512]{1,0:T(8,128)} %param.15) | copy-start | bytes 3145732
  16.4 12.7 %copy-start.3 = (s32[2,64]{1,0:T(2,128)S(1)}, s32[2,64]{1,0:T(2,128)}, u32[]{:S(2)}) copy-start(s32[2,64]{1,0:T(2,128)} %param.13) | copy-start | bytes 1540
  22.3 16.2 %all-to-all-start.1 = ((f32[8,128,128]{2,1,0:T(8,128)}), f32[8,128,128]{2,1,0:T(8,128)S(1)}, u32[]{:S(2)}, u32[]{:S(2)}) async-start(f32[8,128,128]{2,1,0:T(8,128)} %gather_fusion.1), calls=%async_computation.1 | async-start | bytes 1048576 | tf_op jit(solution)/shard_map/all_to_all | solution.py:61
  29.1 141.9 %all-gather.2.cloned.1.call-start = ((), (), s32[]{:S(2)}) async-start(), calls=%async_computation.2 | async-start | bytes 4456448 | tf_op jit(solution)/shard_map/all_gather | solution.py:108
  46.7 143.1 %all-to-all-start = ((f32[128,1,128,128]{3,2,1,0:T(8,128)}), f32[128,1,128,128]{3,2,1,0:T(8,128)}, u32[]{:S(2)}, u32[]{:S(2)}) async-start(f32[128,1,128,128]{3,2,1,0:T(8,128)} %bitcast.76), calls=%async_computation | async-start | bytes 16777216 | tf_op jit(solution)/shard_map/all_to_all | solution.py:62
  179.8 3.3 %copy-start.2 = (f32[1280]{0:T(1024)S(1)}, f32[1280]{0:T(1024)}, u32[]{:S(2)}) copy-start(f32[1280]{0:T(1024)} %param.14) | copy-start | bytes 15364
  202.4 9.6 %collective-permute-start = (f32[80,512]{1,0:T(8,128)S(1)}, f32[80,512]{1,0:T(8,128)S(1)}, u32[]{:S(2)}, u32[]{:S(2)}) collective-permute-start(f32[80,512]{1,0:T(8,128)S(1)} %constant_dynamic-slice_fusion.3), channel_id=1, source_target_pairs={{0,0},{1,16},{2,32},{3,48},{4,64},{5,80},{6,96},{7,112},{8,1},{9,1... | collective-permute-start | bytes 491528 | tf_op jit(solution)/shard_map/ppermute | solution.py:134
  212.0 13.3 %collective-permute-start.1 = (f32[80,512]{1,0:T(8,128)S(1)}, f32[80,512]{1,0:T(8,128)S(1)}, u32[]{:S(2)}, u32[]{:S(2)}) collective-permute-start(f32[80,512]{1,0:T(8,128)S(1)} %collective-permute-done), channel_id=1, source_target_pairs={{0,16},{16,32},{32,48},{48,64},{64,80},{80,96},{96,112},{112,0},{1... | collective-permute-start | bytes 491528 | tf_op jit(solution)/shard_map/ppermute | solution.py:138
  217.0 9.9 %collective-permute-start.2 = (f32[80,512]{1,0:T(8,128)S(1)}, f32[80,512]{1,0:T(8,128)S(1)}, u32[]{:S(2)}, u32[]{:S(2)}) collective-permute-start(f32[80,512]{1,0:T(8,128)S(1)} %collective-permute-done), channel_id=1, source_target_pairs={{0,32},{16,48},{32,64},{48,80},{64,96},{80,112},{96,0},{112,16},{1... | collective-permute-start | bytes 491528 | tf_op jit(solution)/shard_map/ppermute | solution.py:138
  220.1 8.5 %collective-permute-start.3 = (f32[80,512]{1,0:T(8,128)S(1)}, f32[80,512]{1,0:T(8,128)S(1)}, u32[]{:S(2)}, u32[]{:S(2)}) collective-permute-start(f32[80,512]{1,0:T(8,128)S(1)} %collective-permute-done), channel_id=1, source_target_pairs={{0,48},{16,64},{32,80},{48,96},{64,112},{80,0},{96,16},{112,32},{1... | collective-permute-start | bytes 491528 | tf_op jit(solution)/shard_map/ppermute | solution.py:138
  222.3 14.1 %collective-permute-start.4 = (f32[80,512]{1,0:T(8,128)S(1)}, f32[80,512]{1,0:T(8,128)S(1)}, u32[]{:S(2)}, u32[]{:S(2)}) collective-permute-start(f32[80,512]{1,0:T(8,128)S(1)} %collective-permute-done), channel_id=1, source_target_pairs={{0,64},{16,80},{32,96},{48,112},{64,0},{80,16},{96,32},{112,48},{1... | collective-permute-start | bytes 491528 | tf_op jit(solution)/shard_map/ppermute | solution.py:138
  223.7 13.4 %collective-permute-start.5 = (f32[80,512]{1,0:T(8,128)S(1)}, f32[80,512]{1,0:T(8,128)S(1)}, u32[]{:S(2)}, u32[]{:S(2)}) collective-permute-start(f32[80,512]{1,0:T(8,128)S(1)} %collective-permute-done), channel_id=1, source_target_pairs={{0,80},{16,96},{32,112},{48,0},{64,16},{80,32},{96,48},{112,64},{1... | collective-permute-start | bytes 491528 | tf_op jit(solution)/shard_map/ppermute | solution.py:138
  225.3 12.5 %collective-permute-start.6 = (f32[80,512]{1,0:T(8,128)S(1)}, f32[80,512]{1,0:T(8,128)S(1)}, u32[]{:S(2)}, u32[]{:S(2)}) collective-permute-start(f32[80,512]{1,0:T(8,128)S(1)} %collective-permute-done), channel_id=1, source_target_pairs={{0,96},{16,112},{32,0},{48,16},{64,32},{80,48},{96,64},{112,80},{1... | collective-permute-start | bytes 491528 | tf_op jit(solution)/shard_map/ppermute | solution.py:138
  226.8 11.6 %collective-permute-start.7 = (f32[80,512]{1,0:T(8,128)S(1)}, f32[80,512]{1,0:T(8,128)S(1)}, u32[]{:S(2)}, u32[]{:S(2)}) collective-permute-start(f32[80,512]{1,0:T(8,128)S(1)} %collective-permute-done), channel_id=1, source_target_pairs={{0,112},{16,0},{32,16},{48,32},{64,48},{80,64},{96,80},{112,96},{1... | collective-permute-start | bytes 491528 | tf_op jit(solution)/shard_map/ppermute | solution.py:138
  241.1 1.7 copy-start.1
Sparse Core Ops, SparseCore 0:
  40.3 130.6 all-gather.1
